TPU v7x, 128 devices: a whole 4x4x4 slice. The times are simulated.
128 devices in a mesh: head: 4 (over z), page: 32 (over x, y, core).
Axes of the slice: x: 4, y: 4, z: 4, core: 2. Of those that a mesh axis runs over, the one named last changes fastest.
Arguments:
- hidden_in: bfloat16 [32, 1024, 1024], P('page', 'head'), may hold values from -6 to 6
- norm_gain: float32 [1024], replicated, may hold values from 0.1 to 1.9
- w_qkv: bfloat16 [1024, 3, 1024], P(None, None, 'head'), may hold values from -0.1875 to 0.1875
- w_out: bfloat16 [1024, 1024], P('head'), may hold values from -0.75 to 0.75
- cache_kv: bfloat16 [2, 64, 128, 1024], P(None, 'page', None, 'head'), may hold values from -110 to 110, as said below
- page_node: int32 [64], replicated, may hold values from 0 to 18, as said below
- page_fill: int32 [64], replicated, may hold values from 1 to 128
- node_parent: int32 [19], replicated, may hold values from 0 to 2, as said below
- tok_seg: int32 [32, 1024], P('page'), may hold values from 0 to 7, never falling along the last dimension, each value on 1 to 256 neighbouring positions
- req_leaf: int32 [32, 8], P('page'), may hold values from 3 to 18, as said below
Outputs:
- attn_out: bfloat16 [32, 1024, 1024], P('page', 'head')
Inputs may be any that keep to these rules, and one draw needn't show every extreme that they name: `cache_kv`: entries of the cache; keys and values. `page_node`: every node owns at least one page. `node_parent`: node 0 is the root and its own parent; nodes 1 to 2 have parent 0; the others have a parent among nodes 1 to 2, and each of those has a child. `req_leaf`: each request names a lowest-level node; every lowest-level node is named by some request.
All inputs are finite; a program needn't handle non-finite values.
Results may differ from a plain program's by a relative error of at most 0.018.
Values may be sent and summed in bfloat16 or wider, within the bound.
No kernel may reach another device: no remote copies, remote signals or barrier semaphores. Data moves between devices by JAX's collectives and lax.ppermute only.
A program may use at most 64 MiB of HBM per device.

v0:
```python
import jax
import jax.numpy as jnp
from jax import lax
from jax.experimental import pallas as pl
from jax.experimental.pallas import tpu as pltpu
from jax.sharding import PartitionSpec as P

HD = 64
EPSILON = 1e-06
FLOOR_SCORE = -1e30
Q_BLOCK = 256
K_BLOCK = 128
INTERPRET = False


def lookup(indices, lookup_table):
    matches = indices[:, None] == jnp.arange(lookup_table.shape[0], dtype=jnp.int32)[None, :]
    return jnp.sum(jnp.where(matches, lookup_table[None, :], 0), axis=1)


def attn_kernel(
    plist_ref, pcount_ref, pnode_ref, pfill_ref, kfirst_ref,
    qt_ref, tok_ref, kn_ref, vnt_ref, segk_ref, cache_ref,
    o_ref,
    ma_sc, la_sc, acca_sc, mb_sc, lb_sc, accb_sc, cvt_ref,
):
    i = pl.program_id(0)
    width, tq = qt_ref.shape
    groups = width // HD
    pages = cache_ref.shape[1]
    kb = cache_ref.shape[2]

    @pl.when(i == 0)
    def _():
        def transpose_page(g, carry):
            cvt_ref[g] = cache_ref[1, g].astype(jnp.float32).T.astype(cvt_ref.dtype)
            return carry

        lax.fori_loop(0, pages, transpose_page, 0)

    qt = qt_ref[...] * jnp.asarray(0.125, jnp.bfloat16)
    seg_q = tok_ref[0:1, :]
    leaf = tok_ref[1:2, :]
    upper = tok_ref[2:3, :]
    root = tok_ref[3:4, :]
    for m_sc, l_sc, acc_sc in ((ma_sc, la_sc, acca_sc), (mb_sc, lb_sc, accb_sc)):
        m_sc[...] = jnp.full(m_sc.shape, FLOOR_SCORE, jnp.float32)
        l_sc[...] = jnp.zeros(l_sc.shape, jnp.float32)
        acc_sc[...] = jnp.zeros(acc_sc.shape, jnp.float32)
    col_head = lax.broadcasted_iota(jnp.int32, (kb, width), 1) // HD
    row_head = lax.broadcasted_iota(jnp.int32, (width, kb), 0) // HD
    slot = lax.broadcasted_iota(jnp.int32, (kb, 1), 0)

    def update(state, k, vt, mask):
        m_sc, l_sc, acc_sc = state
        zk = jnp.zeros_like(k)
        kbd = jnp.concatenate([jnp.where(col_head == h, k, zk) for h in range(groups)], axis=0)
        st = jnp.dot(kbd, qt, preferred_element_type=jnp.float32)
        probs = []
        scales = []
        for h in range(groups):
            s_h = jnp.where(mask, st[h * kb:(h + 1) * kb, :], FLOOR_SCORE)
            m_old = m_sc[h]
            m_new = jnp.maximum(m_old, jnp.max(s_h, axis=0, keepdims=True))
            alpha = jnp.exp(m_old - m_new)
            p_h = jnp.exp(s_h - m_new)
            l_sc[h] = alpha * l_sc[h] + jnp.sum(p_h, axis=0, keepdims=True)
            m_sc[h] = m_new
            probs.append(p_h.astype(jnp.bfloat16))
            scales.append(jnp.broadcast_to(alpha, (HD, tq)))
        zv = jnp.zeros_like(vt)
        vbdt = jnp.concatenate([jnp.where(row_head == h, vt, zv) for h in range(groups)], axis=1)
        pv = jnp.dot(vbdt, jnp.concatenate(probs, axis=0), preferred_element_type=jnp.float32)
        acc_sc[...] = acc_sc[...] * jnp.concatenate(scales, axis=0) + pv

    chain_a = (ma_sc, la_sc, acca_sc)
    chain_b = (mb_sc, lb_sc, accb_sc)
    qpos = i * tq + lax.broadcasted_iota(jnp.int32, (1, tq), 1)

    def suffix_step(b, carry):
        start = pl.multiple_of(b * kb, kb)
        kpos = start + slot
        mask = (segk_ref[pl.ds(start, kb), :] == seg_q) & (kpos <= qpos)
        update(chain_a, kn_ref[pl.ds(start, kb), :], vnt_ref[:, pl.ds(start, kb)], mask)
        return carry

    last = (i * tq + tq - 1) // kb
    lax.fori_loop(kfirst_ref[i], last + 1, suffix_step, 0)

    count = pcount_ref[i]

    def page_mask(g, valid):
        node = pnode_ref[g]
        fill = jnp.where(valid, pfill_ref[g], 0)
        tok_ok = (leaf == node) | (upper == node) | (root == node)
        return tok_ok & (slot < fill)

    def pair_step(j, carry):
        g0 = plist_ref[i * pages + 2 * j]
        g1 = plist_ref[i * pages + 2 * j + 1]
        update(chain_a, cache_ref[0, g0], cvt_ref[g0], page_mask(g0, True))
        update(chain_b, cache_ref[0, g1], cvt_ref[g1], page_mask(g1, 2 * j + 1 < count))
        return carry

    lax.fori_loop(0, (count + 1) // 2, pair_step, 0)

    parts = []
    for h in range(groups):
        m_all = jnp.maximum(ma_sc[h], mb_sc[h])
        wa = jnp.exp(ma_sc[h] - m_all)
        wb = jnp.exp(mb_sc[h] - m_all)
        l_all = la_sc[h] * wa + lb_sc[h] * wb
        rows = slice(h * HD, (h + 1) * HD)
        acc_h = acca_sc[rows, :] * wa + accb_sc[rows, :] * wb
        parts.append(acc_h / l_all)
    o_ref[...] = jnp.concatenate(parts, axis=0).astype(o_ref.dtype)


def attention(plist, pcount, page_node, page_fill, kfirst, qt, tok, proj, vnt, segk, cache):
    width, tokens = qt.shape
    groups = width // HD
    nqb = tokens // Q_BLOCK
    state = [
        pltpu.VMEM((groups, 1, Q_BLOCK), jnp.float32),
        pltpu.VMEM((groups, 1, Q_BLOCK), jnp.float32),
        pltpu.VMEM((width, Q_BLOCK), jnp.float32),
    ]
    grid_spec = pltpu.PrefetchScalarGridSpec(
        num_scalar_prefetch=5,
        grid=(nqb,),
        in_specs=[
            pl.BlockSpec((width, Q_BLOCK), lambda i, *_: (0, i)),
            pl.BlockSpec((tok.shape[0], Q_BLOCK), lambda i, *_: (0, i)),
            pl.BlockSpec((tokens, width), lambda i, *_: (0, 1)),
            pl.BlockSpec(memory_space=pltpu.VMEM),
            pl.BlockSpec(memory_space=pltpu.VMEM),
            pl.BlockSpec(memory_space=pltpu.VMEM),
        ],
        out_specs=pl.BlockSpec((width, Q_BLOCK), lambda i, *_: (0, i)),
        scratch_shapes=state + state + [
            pltpu.VMEM((cache.shape[1], width, cache.shape[2]), jnp.bfloat16),
        ],
    )
    return pl.pallas_call(
        attn_kernel,
        grid_spec=grid_spec,
        interpret=INTERPRET,
        out_shape=jax.ShapeDtypeStruct((width, tokens), jnp.bfloat16),
        compiler_params=pltpu.CompilerParams(
            dimension_semantics=("arbitrary",), vmem_limit_bytes=48 * 1024 * 1024
        ),
    )(plist, pcount, page_node, page_fill, kfirst, qt, tok, proj, vnt, segk, cache)


def shift_perm(n, d):
    return [(j, (j + d) % n) for j in range(n)]


def head_gather(x, n):
    me = lax.axis_index("head")
    parts = [x] + [lax.ppermute(x, "head", shift_perm(n, d)) for d in range(1, n)]
    stacked = jnp.stack(parts)
    order = (me - jnp.arange(n, dtype=jnp.int32)) % n
    gathered = jnp.take(stacked, order, axis=0)
    return gathered.reshape(n * x.shape[0], x.shape[1])


def head_reduce_scatter(partial, n):
    me = lax.axis_index("head")
    rows = partial.shape[0] // n
    chunks = partial.reshape(n, rows, partial.shape[1])
    total = lax.dynamic_index_in_dim(chunks, me, 0, keepdims=False)
    for d in range(1, n):
        send = lax.dynamic_index_in_dim(chunks, (me + d) % n, 0, keepdims=False)
        recv = lax.ppermute(send.astype(jnp.bfloat16), "head", shift_perm(n, d))
        total = total + recv.astype(jnp.float32)
    return total.astype(jnp.bfloat16)


def shards(
    hidden_in,
    norm_gain,
    w_qkv,
    w_out,
    cache_kv,
    page_node,
    page_fill,
    node_parent,
    tok_seg,
    req_leaf,
):
    widened = hidden_in[0].astype(jnp.float32)
    normed = (
        widened
        * lax.rsqrt(jnp.mean(widened * widened, axis=1, keepdims=True) + EPSILON)
        * norm_gain
    ).astype(jnp.bfloat16)
    model_width = widened.shape[1]
    group_width = w_qkv.shape[2]
    weight_flat = w_qkv.reshape(model_width, 3 * group_width)
    n_head = tok_seg.shape[1] // hidden_in.shape[1]
    projected = jnp.dot(
        head_gather(normed, n_head),
        weight_flat,
        preferred_element_type=jnp.float32,
    ).astype(jnp.bfloat16)
    tokens = projected.shape[0]
    segment = tok_seg[0]
    leaf_node = lookup(segment, req_leaf[0])
    upper_node = lookup(leaf_node, node_parent)
    root_node = lookup(upper_node, node_parent)
    zero_row = jnp.zeros_like(segment)
    tok = jnp.stack(
        [segment, leaf_node, upper_node, root_node] + [zero_row] * 4, axis=0
    )
    pages = page_node.shape[0]
    seen = (
        (page_node[None, :] == leaf_node[:, None])
        | (page_node[None, :] == upper_node[:, None])
        | (page_node[None, :] == root_node[:, None])
    )
    nqb = tokens // Q_BLOCK
    vis = jnp.any(seen.reshape(nqb, Q_BLOCK, pages), axis=1).astype(jnp.int32)
    rank = jnp.cumsum(vis, axis=1) - 1
    picked = (vis[:, :, None] > 0) & (rank[:, :, None] == jnp.arange(pages)[None, None, :])
    plist = jnp.sum(
        jnp.where(picked, jnp.arange(pages, dtype=jnp.int32)[None, :, None], 0), axis=1
    ).astype(jnp.int32).reshape(-1)
    pcount = jnp.sum(vis, axis=1).astype(jnp.int32)
    first_seg = segment[::Q_BLOCK]
    kfirst = (
        jnp.sum((segment[None, :] < first_seg[:, None]).astype(jnp.int32), axis=1) // K_BLOCK
    ).astype(jnp.int32)
    segk = segment[:, None]
    qt = projected[:, :group_width].T
    vnt = projected[:, 2 * group_width:].T
    cache = lax.all_gather(cache_kv, "page", axis=1, tiled=True)
    attn_t = attention(
        plist, pcount, page_node, page_fill, kfirst, qt, tok, projected, vnt, segk, cache
    )
    result = head_reduce_scatter(
        lax.dot_general(
            attn_t, w_out, (((0,), (0,)), ((), ())), preferred_element_type=jnp.float32
        ),
        n_head,
    )
    return result[None]


def solution(mesh):
    placed = (
        P("page", "head", None),
        P(),
        P(None, None, "head"),
        P("head", None),
        P(None, "page", None, "head"),
        P(),
        P(),
        P(),
        P("page", None),
        P("page", None),
    )
    return jax.shard_map(
        shards, mesh=mesh, in_specs=placed, out_specs=P("page", "head", None), check_vma=False
    )
```

profile of v0, /device:TPU:1, one launch (start us, length us, event | category | flops | bytes accessed | tf_op | source)
XLA Modules:
  0.0 156.4 jit_solution(1359323305166354905)
XLA Ops:
  7.3 1.2 fusion.2
  8.5 2.0 %fusion.4 = bf16[256,1024]{1,0:T(8,128)(2,1)} fusion(bf16[1,256,1024]{2,1,0:T(8,128)(2,1)} %param.10, f32[1024]{0:T(1024)} %param.11, f32[256]{0:T(256)S(1)} %add_rsqrt_fusion), kind=kLoop, calls=%fused_computation.10 | loop fusion | flops 1048576 | bytes 1053696 | tf_op jit(solution)/shard_map/convert_element_type | solution.py:197
  10.5 2.5 %collective-permute-start = (bf16[256,1024]{1,0:T(8,128)(2,1)}, bf16[256,1024]{1,0:T(8,128)(2,1)}, u32[]{:S(2)}, u32[]{:S(2)}) collective-permute-start(bf16[256,1024]{1,0:T(8,128)(2,1)} %fusion.4), channel_id=1, source_target_pairs={{0,32},{32,64},{64,96},{96,0},{1,33},{33,65},{65,97},{97,1},{2,34}... | collective-permute-start | bytes 1572872 | tf_op jit(solution)/shard_map/ppermute | solution.py:161
  13.0 3.3 %collective-permute-start.1 = (bf16[256,1024]{1,0:T(8,128)(2,1)}, bf16[256,1024]{1,0:T(8,128)(2,1)}, u32[]{:S(2)}, u32[]{:S(2)}) collective-permute-start(bf16[256,1024]{1,0:T(8,128)(2,1)} %fusion.4), channel_id=1, source_target_pairs={{0,64},{32,96},{64,0},{96,32},{1,65},{33,97},{65,1},{97,33},{2,66}... | collective-permute-start | bytes 1572872 | tf_op jit(solution)/shard_map/ppermute | solution.py:161
  20.1 0.9 or_reduce_fusion
  22.6 1.7 %copy.17 = bf16[1024,3,256]{0,2,1:T(8,128)(2,1)} copy(bf16[1024,3,256]{2,0,1:T(8,128)(2,1)S(1)} %copy-done.6) | data formatting | bytes 3145728 | tf_op args[2]
  24.9 2.2 %collective-permute-done = bf16[256,1024]{1,0:T(8,128)(2,1)} collective-permute-done((bf16[256,1024]{1,0:T(8,128)(2,1)}, bf16[256,1024]{1,0:T(8,128)(2,1)}, u32[]{:S(2)}, u32[]{:S(2)}) %collective-permute-start) | collective-permute-done | bytes 524320 | tf_op jit(solution)/shard_map/ppermute | solution.py:161
  27.1 12.1 %collective-permute-done.1 = bf16[256,1024]{1,0:T(8,128)(2,1)} collective-permute-done((bf16[256,1024]{1,0:T(8,128)(2,1)}, bf16[256,1024]{1,0:T(8,128)(2,1)}, u32[]{:S(2)}, u32[]{:S(2)}) %collective-permute-start.1) | collective-permute-done | bytes 524320 | tf_op jit(solution)/shard_map/ppermute | solution.py:161
  39.2 1.6 %pad_maximum_fusion = bf16[4,256,1024]{2,1,0:T(8,128)(2,1)S(1)} fusion(bf16[1,256,1024]{2,1,0:T(8,128)(2,1)} %bitcast.5, bf16[1,256,1024]{2,1,0:T(8,128)(2,1)} %bitcast.4, bf16[1,256,1024]{2,1,0:T(8,128)(2,1)} %bitcast.3, bf16[1,256,1024]{2,1,0:T(8,128)(2,1)S(1)} %fusion.6), kind=kLoop, calls=%fused_computation.1 | loop fusion | flops 3145728 | bytes 4194304 | tf_op jit(solution)/shard_map/stack | solution.py:162
  40.8 2.1 %gather_fusion = bf16[4,256,1024]{2,1,0:T(8,128)(2,1)} fusion(bf16[4,256,1024]{2,1,0:T(8,128)(2,1)S(1)} %pad_maximum_fusion, s32[1024]{0:T(1024)S(1)} %pad_clamp_fusion), kind=kCustom, calls=%fused_computation | custom fusion | bytes 4194320 | tf_op jit(solution)/shard_map/jit(_take)/gather | solution.py:164
  42.9 2.4 %broadcast_select_fusion = bf16[4,256,1024]{2,1,0:T(8,128)(2,1)S(1)} fusion(bf16[4,256,1024]{2,1,0:T(8,128)(2,1)} %gather_fusion, pred[4]{0:T(512)(128)(4,1)S(1)} %compare_and_fusion), kind=kLoop, calls=%fused_computation.2 | loop fusion | flops 1048576 | bytes 4194308 | tf_op jit(solution)/shard_map/jit(_take)/select_n | solution.py:164
  45.6 3.1 %convolution_convert_fusion = bf16[1024,768]{0,1:T(8,128)(2,1)} fusion(bf16[1024,1024]{1,0:T(8,128)(2,1)S(1)} %bitcast.54, bf16[1024,768]{0,1:T(8,128)(2,1)S(1)} %bitcast.55), kind=kOutput, calls=%fused_computation.3 | convolution fusion | flops 1611399168 | bytes 5242880 | tf_op jit(solution)/shard_map/dot_general | solution.py:202
  48.7 1.8 %copy.19.kn_ref = bf16[1024,768]{1,0:T(8,128)(2,1)S(1)} copy(bf16[1024,768]{0,1:T(8,128)(2,1)} %convolution_convert_fusion) | data formatting | bytes 3145728 | tf_op jit(solution)/shard_map/convert_element_type | solution.py:206
  50.5 2.1 %slice_bitcast_fusion = (bf16[256,1024]{1,0:T(8,128)(2,1)S(1)}, bf16[256,1024]{1,0:T(8,128)(2,1)}) fusion(bf16[1024,768]{0,1:T(8,128)(2,1)} %convolution_convert_fusion), kind=kLoop, calls=%fused_computation.24 | loop fusion | bytes 2097152 | tf_op jit(solution)/shard_map/transpose | solution.py:236
  52.6 13.3 %all-gather.2.cloned.1.call-done.cache_ref = bf16[2,64,128,256]{3,2,1,0:T(8,128)(2,1)} async-done(((bf16[2,2,128,256]{3,2,1,0:T(8,128)(2,1)}), bf16[2,64,128,256]{3,2,1,0:T(8,128)(2,1)}) %all-gather.2.cloned.1.call-update) | async-done | bytes 8388624 | tf_op jit(solution)/shard_map/all_gather | solution.py:237
  65.9 1.0 copy-done.1
  67.0 50.0 %shard_map.100 = bf16[256,1024]{1,0:T(8,128)(2,1)S(1)} custom-call(s32[256]{0:T(256)S(1)} %reshape.173.plist_ref, s32[4]{0:T(128)S(1)} %convert_reduce_fusion.1.pcount_ref, s32[64]{0:T(128)S(1)} %copy-done.2, s32[64]{0:T(128)S(1)} %copy-done.3, s32[4]{0:T(128)S(1)} %and_select_fusion.2.kfirst_ref, bf16[256,1024]{1,0:T(8,128)(2,1)S(1)} %copy-done.1, ...), custom_call_target="tpu_custom_call" | custom-call | tf_op jit(solution)/shard_map/pallas_call | solution.py:144
  117.7 1.9 %copy-done.4 = f32[1024,1024]{1,0:T(8,128)} copy-done((f32[1024,1024]{1,0:T(8,128)}, f32[1024,1024]{1,0:T(8,128)S(1)}, u32[]{:S(2)}) %copy-start.4) | copy-done | bytes 4194328
  119.9 1.3 collective-permute-start.3
  121.2 2.6 %collective-permute-start.4 = (bf16[256,1024]{1,0:T(8,128)(2,1)S(1)}, bf16[256,1024]{1,0:T(8,128)(2,1)S(1)}, u32[]{:S(2)}, u32[]{:S(2)}) collective-permute-start(bf16[256,1024]{1,0:T(8,128)(2,1)S(1)} %get-tuple-element.7), channel_id=1, source_target_pairs={{0,64},{32,96},{64,0},{96,32},{1,65},{33,97},{65,1},{97,33},{2,66}... | collective-permute-start | bytes 1572872 | tf_op jit(solution)/shard_map/ppermute | solution.py:175
  123.8 1.1 collective-permute-start.5
  124.9 9.7 %collective-permute-done.3 = bf16[256,1024]{1,0:T(8,128)(2,1)S(1)} collective-permute-done((bf16[256,1024]{1,0:T(8,128)(2,1)S(1)}, bf16[256,1024]{1,0:T(8,128)(2,1)S(1)}, u32[]{:S(2)}, u32[]{:S(2)}) %collective-permute-start.3) | collective-permute-done | bytes 524320 | tf_op jit(solution)/shard_map/ppermute | solution.py:175
  134.6 12.4 %collective-permute-done.4 = bf16[256,1024]{1,0:T(8,128)(2,1)S(1)} collective-permute-done((bf16[256,1024]{1,0:T(8,128)(2,1)S(1)}, bf16[256,1024]{1,0:T(8,128)(2,1)S(1)}, u32[]{:S(2)}, u32[]{:S(2)}) %collective-permute-start.4) | collective-permute-done | bytes 524320 | tf_op jit(solution)/shard_map/ppermute | solution.py:175
  147.0 2.5 %fusion.13 = bf16[1,256,1024]{2,1,0:T(8,128)(2,1)} fusion(bf16[256,1024]{1,0:T(8,128)(2,1)} %collective-permute-done.5, bf16[256,1024]{1,0:T(8,128)(2,1)S(1)} %collective-permute-done.4, bf16[256,1024]{1,0:T(8,128)(2,1)S(1)} %collective-permute-done.3, f32[4,256,1024]{2,1,0:T(8,128)} %bitcast.53, s32[]{:T(128)S(6)} %select_n.105), kind=kLoop, calls=%fused_computation.23 | loop fusion | flops 1835008 | bytes 3145732 | tf_op jit(solution)/shard_map/broadcast_in_dim | solution.py:247
  (48 shorter events, 7.8 us)
Async XLA Ops:
  6.5 110.4 %copy-start = (bf16[256,1024]{1,0:T(8,128)(2,1)S(1)}, bf16[256,1024]{1,0:T(8,128)(2,1)}, u32[]{:S(2)}) copy-start(bf16[256,1024]{1,0:T(8,128)(2,1)} %param.13) | copy-start | bytes 1572868
  6.5 16.1 %copy-start.6 = (bf16[1024,3,256]{2,0,1:T(8,128)(2,1)S(1)}, bf16[1024,3,256]{2,0,1:T(8,128)(2,1)}, u32[]{:S(2)}) copy-start(bf16[1024,3,256]{2,0,1:T(8,128)(2,1)} %param.12) | copy-start | bytes 4718596
  6.5 59.4 %all-gather.2.cloned.1.call-start = ((), (), s32[]{:S(2)}) async-start(), calls=%async_computation | async-start | bytes 8650752 | tf_op jit(solution)/shard_map/all_gather | solution.py:237
  8.5 15.8 %copy-start.8 = (s32[1,1024]{1,0:T(1,128)S(1)}, s32[1,1024]{1,0:T(1,128)}, u32[]{:S(2)}) copy-start(s32[1,1024]{1,0:T(1,128)} %param.18) | copy-start | bytes 12292
  10.5 14.1 %copy-start.5 = (bf16[1,256,1024]{2,1,0:T(8,128)(2,1)S(1)}, bf16[1,256,1024]{2,1,0:T(8,128)(2,1)}, u32[]{:S(2)}) copy-start(bf16[1,256,1024]{2,1,0:T(8,128)(2,1)} %param.10) | copy-start | bytes 1572868
  10.5 14.1 %copy-start.9 = (f32[1024]{0:T(1024)S(1)}, f32[1024]{0:T(1024)}, u32[]{:S(2)}) copy-start(f32[1024]{0:T(1024)} %param.11) | copy-start | bytes 12292
  10.5 16.5 %collective-permute-start = (bf16[256,1024]{1,0:T(8,128)(2,1)}, bf16[256,1024]{1,0:T(8,128)(2,1)}, u32[]{:S(2)}, u32[]{:S(2)}) collective-permute-start(bf16[256,1024]{1,0:T(8,128)(2,1)} %fusion.4), channel_id=1, source_target_pairs={{0,32},{32,64},{64,96},{96,0},{1,33},{33,65},{65,97},{97,1},{2,34}... | collective-permute-start | bytes 1572872 | tf_op jit(solution)/shard_map/ppermute | solution.py:161
  13.0 26.2 %collective-permute-start.1 = (bf16[256,1024]{1,0:T(8,128)(2,1)}, bf16[256,1024]{1,0:T(8,128)(2,1)}, u32[]{:S(2)}, u32[]{:S(2)}) collective-permute-start(bf16[256,1024]{1,0:T(8,128)(2,1)} %fusion.4), channel_id=1, source_target_pairs={{0,64},{32,96},{64,0},{96,32},{1,65},{33,97},{65,1},{97,33},{2,66}... | collective-permute-start | bytes 1572872 | tf_op jit(solution)/shard_map/ppermute | solution.py:161
  16.3 22.9 %collective-permute-start.2 = (bf16[256,1024]{1,0:T(8,128)(2,1)}, bf16[256,1024]{1,0:T(8,128)(2,1)}, u32[]{:S(2)}, u32[]{:S(2)}) collective-permute-start(bf16[256,1024]{1,0:T(8,128)(2,1)} %fusion.4), channel_id=1, source_target_pairs={{0,96},{32,0},{64,32},{96,64},{1,97},{33,1},{65,33},{97,65},{2,98}... | collective-permute-start | bytes 1572872 | tf_op jit(solution)/shard_map/ppermute | solution.py:161
  42.9 2.7 %copy-start.7 = (bf16[1024,3,256]{0,2,1:T(8,128)(2,1)S(1)}, bf16[1024,3,256]{0,2,1:T(8,128)(2,1)}, u32[]{:S(2)}) copy-start(bf16[1024,3,256]{0,2,1:T(8,128)(2,1)} %copy.17) | copy-start | bytes 4718596
  48.7 17.2 %copy-start.2 = (s32[64]{0:T(128)S(1)}, s32[64]{0:T(128)}, u32[]{:S(2)}) copy-start(s32[64]{0:T(128)} %pnode_ref.1) | copy-start | bytes 772
  48.7 17.2 %copy-start.3 = (s32[64]{0:T(128)S(1)}, s32[64]{0:T(128)}, u32[]{:S(2)}) copy-start(s32[64]{0:T(128)} %pfill_ref.1) | copy-start | bytes 772
  65.9 1.0 copy-start.1
  117.7 1.9 %copy-start.4 = (f32[1024,1024]{1,0:T(8,128)}, f32[1024,1024]{1,0:T(8,128)S(1)}, u32[]{:S(2)}) copy-start(f32[1024,1024]{1,0:T(8,128)S(1)} %fusion.18) | copy-start | bytes 12582916
  119.9 14.7 %collective-permute-start.3 = (bf16[256,1024]{1,0:T(8,128)(2,1)S(1)}, bf16[256,1024]{1,0:T(8,128)(2,1)S(1)}, u32[]{:S(2)}, u32[]{:S(2)}) collective-permute-start(bf16[256,1024]{1,0:T(8,128)(2,1)S(1)} %get-tuple-element.5), channel_id=1, source_target_pairs={{0,32},{32,64},{64,96},{96,0},{1,33},{33,65},{65,97},{97,1},{2,34}... | collective-permute-start | bytes 1572872 | tf_op jit(solution)/shard_map/ppermute | solution.py:175
  121.2 25.8 %collective-permute-start.4 = (bf16[256,1024]{1,0:T(8,128)(2,1)S(1)}, bf16[256,1024]{1,0:T(8,128)(2,1)S(1)}, u32[]{:S(2)}, u32[]{:S(2)}) collective-permute-start(bf16[256,1024]{1,0:T(8,128)(2,1)S(1)} %get-tuple-element.7), channel_id=1, source_target_pairs={{0,64},{32,96},{64,0},{96,32},{1,65},{33,97},{65,1},{97,33},{2,66}... | collective-permute-start | bytes 1572872 | tf_op jit(solution)/shard_map/ppermute | solution.py:175
  123.8 23.2 %collective-permute-start.5 = (bf16[256,1024]{1,0:T(8,128)(2,1)S(1)}, bf16[256,1024]{1,0:T(8,128)(2,1)}, u32[]{:S(2)}, u32[]{:S(2)}) collective-permute-start(bf16[256,1024]{1,0:T(8,128)(2,1)S(1)} %get-tuple-element.6), channel_id=1, source_target_pairs={{0,96},{32,0},{64,32},{96,64},{1,97},{33,1},{65,33},{97,65},{2,98}... | collective-permute-start | bytes 1572872 | tf_op jit(solution)/shard_map/ppermute | solution.py:175
Sparse Core Ops, SparseCore 0:
  9.7 56.1 all-gather.1
where the time goes:
time: 153 us; the launch traced here: 156 us
  waiting for transfers between devices  50.5 us (33%)
  Pallas kernels  50 us (33%)
  other arithmetic  14.7 us (10%)
  between operations  13.6 us (9%)
  local copies, waits for them, and re-layouts  12.3 us (8%)
  starting transfers between devices  11.5 us (8%)
  matrix products  3.83 us (3%)
    pallas_call x1, Pallas kernels, attention(): pl.pallas_call(attn_kernel, grid_spec=grid_spec, interpret=INTERPRET, out...  50 us
    ppermute x3, waiting for transfers between devices, head_reduce_scatter(): recv = lax.ppermute(send.astype(jnp.bfloat16), 'head', shift_perm(n, d))  22.1 us
    ppermute x3, waiting for transfers between devices, head_gather(): lax.ppermute(x, 'head', shift_perm(n, d))  14.3 us
    all_gather x1, waiting for transfers between devices, shards(): cache = lax.all_gather(cache_kv, 'page', axis=1, tiled=True)  13.3 us
    ppermute x3, starting transfers between devices, head_gather(): lax.ppermute(x, 'head', shift_perm(n, d))  6.49 us
    ppermute x3, starting transfers between devices, head_reduce_scatter(): recv = lax.ppermute(send.astype(jnp.bfloat16), 'head', shift_perm(n, d))  5.01 us
    unnamed x21, local copies, waits for them, and re-layouts  5.01 us
    dot_general x1, matrix products, shards(): jnp.dot(head_gather(normed, n_head), weight_flat, preferred_element_type=...  3.06 us
  transfers between devices with their start and end apart: 7, of which 5 were waited for; matrix products, arithmetic and copies ran while one was open for 15% of the time, Pallas kernels for 0%

commit v1 on v0

--- a/solution.py
+++ b/solution.py
@@ -20,20 +20,20 @@
 
 def attn_kernel(
     plist_ref, pcount_ref, pnode_ref, pfill_ref, kfirst_ref,
-    qt_ref, tok_ref, kn_ref, vnt_ref, segk_ref, cache_ref,
+    qt_ref, tok_ref, kn_ref, vnt_ref, segk_ref, ck_ref, cv_ref,
     o_ref,
     ma_sc, la_sc, acca_sc, mb_sc, lb_sc, accb_sc, cvt_ref,
 ):
     i = pl.program_id(0)
     width, tq = qt_ref.shape
     groups = width // HD
-    pages = cache_ref.shape[1]
-    kb = cache_ref.shape[2]
+    pages = ck_ref.shape[0]
+    kb = ck_ref.shape[1]
 
     @pl.when(i == 0)
     def _():
         def transpose_page(g, carry):
-            cvt_ref[g] = cache_ref[1, g].astype(jnp.float32).T.astype(cvt_ref.dtype)
+            cvt_ref[g] = cv_ref[g].astype(jnp.float32).T.astype(cvt_ref.dtype)
             return carry
 
         lax.fori_loop(0, pages, transpose_page, 0)
@@ -98,8 +98,8 @@
     def pair_step(j, carry):
         g0 = plist_ref[i * pages + 2 * j]
         g1 = plist_ref[i * pages + 2 * j + 1]
-        update(chain_a, cache_ref[0, g0], cvt_ref[g0], page_mask(g0, True))
-        update(chain_b, cache_ref[0, g1], cvt_ref[g1], page_mask(g1, 2 * j + 1 < count))
+        update(chain_a, ck_ref[g0], cvt_ref[g0], page_mask(g0, True))
+        update(chain_b, ck_ref[g1], cvt_ref[g1], page_mask(g1, 2 * j + 1 < count))
         return carry
 
     lax.fori_loop(0, (count + 1) // 2, pair_step, 0)
@@ -116,7 +116,7 @@
     o_ref[...] = jnp.concatenate(parts, axis=0).astype(o_ref.dtype)
 
 
-def attention(plist, pcount, page_node, page_fill, kfirst, qt, tok, proj, vnt, segk, cache):
+def attention(plist, pcount, page_node, page_fill, kfirst, qt, tok, proj, vnt, segk, ck, cv):
     width, tokens = qt.shape
     groups = width // HD
     nqb = tokens // Q_BLOCK
@@ -135,10 +135,11 @@
             pl.BlockSpec(memory_space=pltpu.VMEM),
             pl.BlockSpec(memory_space=pltpu.VMEM),
             pl.BlockSpec(memory_space=pltpu.VMEM),
+            pl.BlockSpec(memory_space=pltpu.VMEM),
         ],
         out_specs=pl.BlockSpec((width, Q_BLOCK), lambda i, *_: (0, i)),
         scratch_shapes=state + state + [
-            pltpu.VMEM((cache.shape[1], width, cache.shape[2]), jnp.bfloat16),
+            pltpu.VMEM((ck.shape[0], width, ck.shape[1]), jnp.bfloat16),
         ],
     )
     return pl.pallas_call(
@@ -149,7 +150,7 @@
         compiler_params=pltpu.CompilerParams(
             dimension_semantics=("arbitrary",), vmem_limit_bytes=48 * 1024 * 1024
         ),
-    )(plist, pcount, page_node, page_fill, kfirst, qt, tok, proj, vnt, segk, cache)
+    )(plist, pcount, page_node, page_fill, kfirst, qt, tok, proj, vnt, segk, ck, cv)
 
 
 def shift_perm(n, d):
@@ -234,9 +235,15 @@
     segk = segment[:, None]
     qt = projected[:, :group_width].T
     vnt = projected[:, 2 * group_width:].T
-    cache = lax.all_gather(cache_kv, "page", axis=1, tiled=True)
+    chip_cache = lax.all_gather(cache_kv, "pc", axis=1, tiled=True)
+    core = lax.axis_index("pc")
+    mine = lax.dynamic_index_in_dim(chip_cache, core, 0, keepdims=False)
+    mine = lax.all_gather(mine, "chip", axis=0, tiled=True)
+    other = lax.ppermute(mine, "pc", [(0, 1), (1, 0)])
+    ck = jnp.where(core == 0, mine, other)
+    cv = jnp.where(core == 0, other, mine)
     attn_t = attention(
-        plist, pcount, page_node, page_fill, kfirst, qt, tok, projected, vnt, segk, cache
+        plist, pcount, page_node, page_fill, kfirst, qt, tok, projected, vnt, segk, ck, cv
     )
     result = head_reduce_scatter(
         lax.dot_general(
@@ -248,18 +255,23 @@
 
 
 def solution(mesh):
+    devices = mesh.devices
+    sub = jax.sharding.Mesh(
+        devices.reshape(devices.shape[0], devices.shape[1] // 2, 2), ("head", "chip", "pc")
+    )
+    page = ("chip", "pc")
     placed = (
-        P("page", "head", None),
+        P(page, "head", None),
         P(),
         P(None, None, "head"),
         P("head", None),
-        P(None, "page", None, "head"),
-        P(),
-        P(),
-        P(),
-        P("page", None),
-        P("page", None),
+        P(None, page, None, "head"),
+        P(),
+        P(),
+        P(),
+        P(page, None),
+        P(page, None),
     )
     return jax.shard_map(
-        shards, mesh=mesh, in_specs=placed, out_specs=P("page", "head", None), check_vma=False
-    )
+        shards, mesh=sub, in_specs=placed, out_specs=P(page, "head", None), check_vma=False
+    )

time: 153 us -> 196 us (1.28)
  waiting for transfers between devices: 50.5 us -> 95.1 us
  Pallas kernels: 50 us -> 46.6 us
  blocking collectives: 0 us -> 3.19 us
    all_gather x1, waiting for transfers between devices: 13.3 us -> 53.5 us  [shards(): mine = lax.all_gather(mine, 'chip', axis=0, tiled=True)]
    select_n x0 -> x1, other arithmetic: none -> 5.72 us  [shards(): cv = jnp.where(core == 0, other, mine)]
    ppermute x3, waiting for transfers between devices: 14.3 us -> 18.7 us  [head_gather(): lax.ppermute(x, 'head', shift_perm(n, d))]
    pallas_call x1, Pallas kernels: 50 us -> 46.6 us  [attention(): pl.pallas_call(attn_kernel, grid_spec=grid_spec, interpret=INTERPRET, out...]
    all_gather x0 -> x1, blocking collectives: none -> 3.19 us  [shards(): chip_cache = lax.all_gather(cache_kv, 'pc', axis=1, tiled=True)]
    reduce_sum x3, other arithmetic: 2.27 us -> 0.25 us  [lookup(): return jnp.sum(jnp.where(matches, lookup_table[None, :], 0), axis=1)]
    unnamed x21 -> x24, local copies, waits for them, and re-layouts: 5.01 us -> 4.87 us
  transfers between devices with their start and end apart: 7 -> 8, of which waited for: 5 -> 6; matrix products, arithmetic and copies ran while one was open for 15% -> 8% of each run, Pallas kernels for 0% -> 0%
where the time goes in v1:
time: 196 us; the launch traced here: 198 us
  waiting for transfers between devices  95.1 us (49%)
  Pallas kernels  46.6 us (24%)
  other arithmetic  14.5 us (7%)
  between operations  13.7 us (7%)
  local copies, waits for them, and re-layouts  11.3 us (6%)
  starting transfers between devices  10 us (5%)
  matrix products  3.8 us (2%)
  blocking collectives  3.19 us (2%)
    all_gather x1, waiting for transfers between devices, shards(): mine = lax.all_gather(mine, 'chip', axis=0, tiled=True)  53.5 us
    pallas_call x1, Pallas kernels, attention(): pl.pallas_call(attn_kernel, grid_spec=grid_spec, interpret=INTERPRET, out...  46.6 us
    ppermute x3, waiting for transfers between devices, head_reduce_scatter(): recv = lax.ppermute(send.astype(jnp.bfloat16), 'head', shift_perm(n, d))  23 us
    ppermute x3, waiting for transfers between devices, head_gather(): lax.ppermute(x, 'head', shift_perm(n, d))  18.7 us
    select_n x1, other arithmetic, shards(): cv = jnp.where(core == 0, other, mine)  5.72 us
    ppermute x3, starting transfers between devices, head_gather(): lax.ppermute(x, 'head', shift_perm(n, d))  4.94 us
    unnamed x24, local copies, waits for them, and re-layouts  4.87 us
    ppermute x3, starting transfers between devices, head_reduce_scatter(): recv = lax.ppermute(send.astype(jnp.bfloat16), 'head', shift_perm(n, d))  4.18 us
  transfers between devices with their start and end apart: 8, of which 6 were waited for; matrix products, arithmetic and copies ran while one was open for 8% of the time, Pallas kernels for 0%

profile of v1, /device:TPU:1, one launch (start us, length us, event | category | flops | bytes accessed | tf_op | source)
XLA Modules:
  0.0 198.2 jit_solution(6197362943897727349)
XLA Ops:
  6.6 1.1 copy.29
  7.8 3.2 %all_gather.6 = bf16[2,4,128,256]{3,2,0,1:T(8,128)(2,1)S(1)} all-gather(bf16[2,2,128,256]{3,2,0,1:T(8,128)(2,1)S(1)} %copy.29), channel_id=1, replica_groups=mesh['head'=4,'chip'=16,'pc'=2] {'pc'}, dimensions={1}, use_global_device_ids=true | all-gather | bytes 786432 | tf_op jit(solution)/shard_map/all_gather | solution.py:238
  11.7 53.5 %all-gather.3.cloned.1.call-done = bf16[1,64,128,256]{3,2,0,1:T(8,128)(2,1)} async-done(((bf16[1,4,128,256]{3,2,0,1:T(8,128)(2,1)}), bf16[1,64,128,256]{3,2,0,1:T(8,128)(2,1)}) %all-gather.3.cloned.1.call-update) | async-done | bytes 4194320 | tf_op jit(solution)/shard_map/all_gather | solution.py:241
  66.2 1.0 fusion.4
  67.2 1.3 collective-permute-start
  68.4 2.6 %collective-permute-start.1 = (bf16[256,1024]{1,0:T(8,128)(2,1)}, bf16[256,1024]{1,0:T(8,128)(2,1)}, u32[]{:S(2)}, u32[]{:S(2)}) collective-permute-start(bf16[256,1024]{1,0:T(8,128)(2,1)} %fusion.4), channel_id=1, source_target_pairs={{0,64},{32,96},{64,0},{96,32},{1,65},{33,97},{65,1},{97,33},{2,66}... | collective-permute-start | bytes 1572872 | tf_op jit(solution)/shard_map/ppermute | solution.py:162
  71.0 1.1 collective-permute-start.2
  73.7 1.7 copy.27
  75.9 6.3 %collective-permute-done = bf16[256,1024]{1,0:T(8,128)(2,1)} collective-permute-done((bf16[256,1024]{1,0:T(8,128)(2,1)}, bf16[256,1024]{1,0:T(8,128)(2,1)}, u32[]{:S(2)}, u32[]{:S(2)}) %collective-permute-start) | collective-permute-done | bytes 524320 | tf_op jit(solution)/shard_map/ppermute | solution.py:162
  82.2 12.4 %collective-permute-done.1 = bf16[256,1024]{1,0:T(8,128)(2,1)} collective-permute-done((bf16[256,1024]{1,0:T(8,128)(2,1)}, bf16[256,1024]{1,0:T(8,128)(2,1)}, u32[]{:S(2)}, u32[]{:S(2)}) %collective-permute-start.1) | collective-permute-done | bytes 524320 | tf_op jit(solution)/shard_map/ppermute | solution.py:162
  94.6 1.6 pad_maximum_fusion
  96.2 2.1 %gather_fusion = bf16[4,256,1024]{2,1,0:T(8,128)(2,1)} fusion(bf16[4,256,1024]{2,1,0:T(8,128)(2,1)S(1)} %pad_maximum_fusion, s32[1024]{0:T(1024)S(1)} %pad_clamp_fusion), kind=kCustom, calls=%fused_computation | custom fusion | bytes 4194320 | tf_op jit(solution)/shard_map/jit(_take)/gather | solution.py:165
  98.3 2.0 broadcast_select_fusion.2
  100.3 3.1 %convolution_convert_fusion = bf16[1024,768]{0,1:T(8,128)(2,1)} fusion(bf16[1024,1024]{1,0:T(8,128)(2,1)S(1)} %bitcast.58, bf16[1024,768]{0,1:T(8,128)(2,1)S(1)} %bitcast.59), kind=kOutput, calls=%fused_computation.5 | convolution fusion | flops 1611399168 | bytes 5242880 | tf_op jit(solution)/shard_map/dot_general | solution.py:203
  103.4 1.7 copy.30.kn_ref
  105.1 1.3 slice_bitcast_fusion
  106.4 5.7 %broadcast_select_fusion = (bf16[64,128,256]{2,1,0:T(8,128)(2,1)}, bf16[64,128,256]{2,1,0:T(8,128)(2,1)}) fusion(bf16[64,128,256]{2,1,0:T(8,128)(2,1)} %collective-permute-done.3, pred[]{:T(512)S(6)} %eq.131, bf16[1,64,128,256]{3,2,0,1:T(8,128)(2,1)} %all-gather.3.cloned.1.call-done), kind=kLoop, calls=%fused_computation.1 | loop fusion | flops 4194304 | bytes 16777216 | tf_op jit(solution)/shard_map/jit(_where)/select_n | solution.py:244
  112.1 46.6 %shard_map.100 = bf16[256,1024]{1,0:T(8,128)(2,1)S(1)} custom-call(s32[256]{0:T(256)S(1)} %reshape.173.plist_ref, s32[4]{0:T(128)S(1)} %convert_reduce_fusion.1.pcount_ref, s32[64]{0:T(128)S(1)} %copy-done.1, s32[64]{0:T(128)S(1)} %copy-done.2, s32[4]{0:T(128)S(1)} %and_select_fusion.2.kfirst_ref, bf16[256,1024]{1,0:T(8,128)(2,1)S(1)} %get-tuple-element.11.qt_ref, ...), custom_call_target="tpu_custom_call" | custom-call | tf_op jit(solution)/shard_map/pallas_call | solution.py:145
  159.5 1.9 copy-done.3
  162.2 2.9 %collective-permute-start.5 = (bf16[256,1024]{1,0:T(8,128)(2,1)S(1)}, bf16[256,1024]{1,0:T(8,128)(2,1)S(1)}, u32[]{:S(2)}, u32[]{:S(2)}) collective-permute-start(bf16[256,1024]{1,0:T(8,128)(2,1)S(1)} %get-tuple-element.9), channel_id=1, source_target_pairs={{0,64},{32,96},{64,0},{96,32},{1,65},{33,97},{65,1},{97,33},{2,66}... | collective-permute-start | bytes 1572872 | tf_op jit(solution)/shard_map/ppermute | solution.py:176
  165.9 11.1 %collective-permute-done.4 = bf16[256,1024]{1,0:T(8,128)(2,1)S(1)} collective-permute-done((bf16[256,1024]{1,0:T(8,128)(2,1)S(1)}, bf16[256,1024]{1,0:T(8,128)(2,1)S(1)}, u32[]{:S(2)}, u32[]{:S(2)}) %collective-permute-start.4) | collective-permute-done | bytes 524320 | tf_op jit(solution)/shard_map/ppermute | solution.py:176
  177.0 10.9 %collective-permute-done.5 = bf16[256,1024]{1,0:T(8,128)(2,1)S(1)} collective-permute-done((bf16[256,1024]{1,0:T(8,128)(2,1)S(1)}, bf16[256,1024]{1,0:T(8,128)(2,1)S(1)}, u32[]{:S(2)}, u32[]{:S(2)}) %collective-permute-start.5) | collective-permute-done | bytes 524320 | tf_op jit(solution)/shard_map/ppermute | solution.py:176
  187.8 1.0 collective-permute-done.6
  188.8 2.5 %fusion.13 = bf16[1,256,1024]{2,1,0:T(8,128)(2,1)} fusion(bf16[256,1024]{1,0:T(8,128)(2,1)} %collective-permute-done.6, bf16[256,1024]{1,0:T(8,128)(2,1)S(1)} %collective-permute-done.5, bf16[256,1024]{1,0:T(8,128)(2,1)S(1)} %collective-permute-done.4, f32[4,256,1024]{2,1,0:T(8,128)} %bitcast.56, s32[]{:T(128)S(6)} %select_n.125), kind=kLoop, calls=%fused_computation.25 | loop fusion | flops 1835008 | bytes 3145732 | tf_op jit(solution)/shard_map/broadcast_in_dim | solution.py:254
  (56 shorter events, 6.1 us)
Async XLA Ops:
  6.5 152.2 %copy-start = (bf16[256,1024]{1,0:T(8,128)(2,1)S(1)}, bf16[256,1024]{1,0:T(8,128)(2,1)}, u32[]{:S(2)}) copy-start(bf16[256,1024]{1,0:T(8,128)(2,1)} %param.13) | copy-start | bytes 1572868
  6.5 59.4 %copy-start.4 = (bf16[1,256,1024]{2,1,0:T(8,128)(2,1)S(1)}, bf16[1,256,1024]{2,1,0:T(8,128)(2,1)}, u32[]{:S(2)}) copy-start(bf16[1,256,1024]{2,1,0:T(8,128)(2,1)} %param.10) | copy-start | bytes 1572868
  6.5 59.6 %copy-start.8 = (f32[1024]{0:T(1024)S(1)}, f32[1024]{0:T(1024)}, u32[]{:S(2)}) copy-start(f32[1024]{0:T(1024)} %param.11) | copy-start | bytes 12292
  6.5 65.6 %copy-start.7 = (s32[1,1024]{1,0:T(1,128)S(1)}, s32[1,1024]{1,0:T(1,128)}, u32[]{:S(2)}) copy-start(s32[1,1024]{1,0:T(1,128)} %param.18) | copy-start | bytes 12292
  6.5 65.7 %copy-start.10 = (s32[1,8]{1,0:T(1,128)S(1)}, s32[1,8]{1,0:T(1,128)}, u32[]{:S(2)}) copy-start(s32[1,8]{1,0:T(1,128)} %param.19) | copy-start | bytes 100
  6.5 65.8 %copy-start.9 = (s32[19]{0:T(128)S(1)}, s32[19]{0:T(128)}, u32[]{:S(2)}) copy-start(s32[19]{0:T(128)} %param.17) | copy-start | bytes 232
  6.6 66.0 %copy-start.1 = (s32[64]{0:T(128)S(1)}, s32[64]{0:T(128)}, u32[]{:S(2)}) copy-start(s32[64]{0:T(128)} %pnode_ref.1) | copy-start | bytes 772
  6.6 67.1 %copy-start.5 = (bf16[1024,3,256]{2,0,1:T(8,128)(2,1)S(1)}, bf16[1024,3,256]{2,0,1:T(8,128)(2,1)}, u32[]{:S(2)}) copy-start(bf16[1024,3,256]{2,0,1:T(8,128)(2,1)} %param.12) | copy-start | bytes 4718596
  6.6 58.6 %all-gather.3.cloned.1.call-start = ((), (), s32[]{:S(2)}) async-start(), calls=%async_computation | async-start | bytes 4456448 | tf_op jit(solution)/shard_map/all_gather | solution.py:241
  65.1 41.2 %collective-permute-start.3 = (bf16[64,128,256]{2,1,0:T(8,128)(2,1)}, bf16[64,128,256]{2,1,0:T(8,128)(2,1)}, u32[]{:S(2)}, u32[]{:S(2)}) collective-permute-start(bf16[64,128,256]{2,1,0:T(8,128)(2,1)} %bitcast.57), channel_id=1, source_target_pairs={{0,1},{1,0},{2,3},{3,2},{4,5},{5,4},{6,7},{7,6},{8,9},{9,8},{10,11... | collective-permute-start | bytes 12582920 | tf_op jit(solution)/shard_map/ppermute | solution.py:242
  67.2 15.0 %collective-permute-start = (bf16[256,1024]{1,0:T(8,128)(2,1)}, bf16[256,1024]{1,0:T(8,128)(2,1)}, u32[]{:S(2)}, u32[]{:S(2)}) collective-permute-start(bf16[256,1024]{1,0:T(8,128)(2,1)} %fusion.4), channel_id=1, source_target_pairs={{0,32},{32,64},{64,96},{96,0},{1,33},{33,65},{65,97},{97,1},{2,34}... | collective-permute-start | bytes 1572872 | tf_op jit(solution)/shard_map/ppermute | solution.py:162
  68.4 26.1 %collective-permute-start.1 = (bf16[256,1024]{1,0:T(8,128)(2,1)}, bf16[256,1024]{1,0:T(8,128)(2,1)}, u32[]{:S(2)}, u32[]{:S(2)}) collective-permute-start(bf16[256,1024]{1,0:T(8,128)(2,1)} %fusion.4), channel_id=1, source_target_pairs={{0,64},{32,96},{64,0},{96,32},{1,65},{33,97},{65,1},{97,33},{2,66}... | collective-permute-start | bytes 1572872 | tf_op jit(solution)/shard_map/ppermute | solution.py:162
  71.0 23.6 %collective-permute-start.2 = (bf16[256,1024]{1,0:T(8,128)(2,1)}, bf16[256,1024]{1,0:T(8,128)(2,1)}, u32[]{:S(2)}, u32[]{:S(2)}) collective-permute-start(bf16[256,1024]{1,0:T(8,128)(2,1)} %fusion.4), channel_id=1, source_target_pairs={{0,96},{32,0},{64,32},{96,64},{1,97},{33,1},{65,33},{97,65},{2,98}... | collective-permute-start | bytes 1572872 | tf_op jit(solution)/shard_map/ppermute | solution.py:162
  98.3 2.0 %copy-start.6 = (bf16[1024,3,256]{0,2,1:T(8,128)(2,1)S(1)}, bf16[1024,3,256]{0,2,1:T(8,128)(2,1)}, u32[]{:S(2)}) copy-start(bf16[1024,3,256]{0,2,1:T(8,128)(2,1)} %copy.27) | copy-start | bytes 4718596
  106.4 5.7 %copy-start.2 = (s32[64]{0:T(128)S(1)}, s32[64]{0:T(128)}, u32[]{:S(2)}) copy-start(s32[64]{0:T(128)} %pfill_ref.1) | copy-start | bytes 772
  159.5 1.9 copy-start.3
  161.7 15.3 %collective-permute-start.4 = (bf16[256,1024]{1,0:T(8,128)(2,1)S(1)}, bf16[256,1024]{1,0:T(8,128)(2,1)S(1)}, u32[]{:S(2)}, u32[]{:S(2)}) collective-permute-start(bf16[256,1024]{1,0:T(8,128)(2,1)S(1)} %get-tuple-element.7), channel_id=1, source_target_pairs={{0,32},{32,64},{64,96},{96,0},{1,33},{33,65},{65,97},{97,1},{2,34}... | collective-permute-start | bytes 1572872 | tf_op jit(solution)/shard_map/ppermute | solution.py:176
  162.2 25.7 %collective-permute-start.5 = (bf16[256,1024]{1,0:T(8,128)(2,1)S(1)}, bf16[256,1024]{1,0:T(8,128)(2,1)S(1)}, u32[]{:S(2)}, u32[]{:S(2)}) collective-permute-start(bf16[256,1024]{1,0:T(8,128)(2,1)S(1)} %get-tuple-element.9), channel_id=1, source_target_pairs={{0,64},{32,96},{64,0},{96,32},{1,65},{33,97},{65,1},{97,33},{2,66}... | collective-permute-start | bytes 1572872 | tf_op jit(solution)/shard_map/ppermute | solution.py:176
  165.1 23.7 %collective-permute-start.6 = (bf16[256,1024]{1,0:T(8,128)(2,1)S(1)}, bf16[256,1024]{1,0:T(8,128)(2,1)}, u32[]{:S(2)}, u32[]{:S(2)}) collective-permute-start(bf16[256,1024]{1,0:T(8,128)(2,1)S(1)} %get-tuple-element.8), channel_id=1, source_target_pairs={{0,96},{32,0},{64,32},{96,64},{1,97},{33,1},{65,33},{97,65},{2,98}... | collective-permute-start | bytes 1572872 | tf_op jit(solution)/shard_map/ppermute | solution.py:176
Sparse Core Ops, SparseCore 0:
  11.8 53.2 all-gather.2

commit v2 on v0

--- a/solution.py
+++ b/solution.py
@@ -19,24 +19,16 @@
 
 
 def attn_kernel(
-    plist_ref, pcount_ref, pnode_ref, pfill_ref, kfirst_ref,
-    qt_ref, tok_ref, kn_ref, vnt_ref, segk_ref, cache_ref,
+    plist_ref, pcount_ref, pnode_ref, pfill_ref, kfirst_ref, qsel_ref,
+    qt_ref, tok_ref, kn_ref, vnt_ref, segk_ref, ck_ref, cvt_ref,
     o_ref,
-    ma_sc, la_sc, acca_sc, mb_sc, lb_sc, accb_sc, cvt_ref,
+    ma_sc, la_sc, acca_sc, mb_sc, lb_sc, accb_sc,
 ):
-    i = pl.program_id(0)
+    i = qsel_ref[0]
     width, tq = qt_ref.shape
     groups = width // HD
-    pages = cache_ref.shape[1]
-    kb = cache_ref.shape[2]
-
-    @pl.when(i == 0)
-    def _():
-        def transpose_page(g, carry):
-            cvt_ref[g] = cache_ref[1, g].astype(jnp.float32).T.astype(cvt_ref.dtype)
-            return carry
-
-        lax.fori_loop(0, pages, transpose_page, 0)
+    pages = ck_ref.shape[0]
+    kb = ck_ref.shape[1]
 
     qt = qt_ref[...] * jnp.asarray(0.125, jnp.bfloat16)
     seg_q = tok_ref[0:1, :]
@@ -98,8 +90,8 @@
     def pair_step(j, carry):
         g0 = plist_ref[i * pages + 2 * j]
         g1 = plist_ref[i * pages + 2 * j + 1]
-        update(chain_a, cache_ref[0, g0], cvt_ref[g0], page_mask(g0, True))
-        update(chain_b, cache_ref[0, g1], cvt_ref[g1], page_mask(g1, 2 * j + 1 < count))
+        update(chain_a, ck_ref[g0], cvt_ref[g0], page_mask(g0, True))
+        update(chain_b, ck_ref[g1], cvt_ref[g1], page_mask(g1, 2 * j + 1 < count))
         return carry
 
     lax.fori_loop(0, (count + 1) // 2, pair_step, 0)
@@ -116,40 +108,38 @@
     o_ref[...] = jnp.concatenate(parts, axis=0).astype(o_ref.dtype)
 
 
-def attention(plist, pcount, page_node, page_fill, kfirst, qt, tok, proj, vnt, segk, cache):
+def attention(plist, pcount, page_node, page_fill, kfirst, qsel, qt, tok, proj, vnt, segk, ck, cvt):
     width, tokens = qt.shape
     groups = width // HD
-    nqb = tokens // Q_BLOCK
     state = [
         pltpu.VMEM((groups, 1, Q_BLOCK), jnp.float32),
         pltpu.VMEM((groups, 1, Q_BLOCK), jnp.float32),
         pltpu.VMEM((width, Q_BLOCK), jnp.float32),
     ]
     grid_spec = pltpu.PrefetchScalarGridSpec(
-        num_scalar_prefetch=5,
-        grid=(nqb,),
+        num_scalar_prefetch=6,
+        grid=(1,),
         in_specs=[
-            pl.BlockSpec((width, Q_BLOCK), lambda i, *_: (0, i)),
-            pl.BlockSpec((tok.shape[0], Q_BLOCK), lambda i, *_: (0, i)),
-            pl.BlockSpec((tokens, width), lambda i, *_: (0, 1)),
+            pl.BlockSpec((width, Q_BLOCK), lambda i, *r: (0, r[5][0])),
+            pl.BlockSpec((tok.shape[0], Q_BLOCK), lambda i, *r: (0, r[5][0])),
+            pl.BlockSpec((tokens, width), lambda i, *r: (0, 1)),
+            pl.BlockSpec(memory_space=pltpu.VMEM),
             pl.BlockSpec(memory_space=pltpu.VMEM),
             pl.BlockSpec(memory_space=pltpu.VMEM),
             pl.BlockSpec(memory_space=pltpu.VMEM),
         ],
-        out_specs=pl.BlockSpec((width, Q_BLOCK), lambda i, *_: (0, i)),
-        scratch_shapes=state + state + [
-            pltpu.VMEM((cache.shape[1], width, cache.shape[2]), jnp.bfloat16),
-        ],
+        out_specs=pl.BlockSpec((width, Q_BLOCK), lambda i, *r: (0, 0)),
+        scratch_shapes=state + state,
     )
     return pl.pallas_call(
         attn_kernel,
         grid_spec=grid_spec,
         interpret=INTERPRET,
-        out_shape=jax.ShapeDtypeStruct((width, tokens), jnp.bfloat16),
+        out_shape=jax.ShapeDtypeStruct((width, Q_BLOCK), jnp.bfloat16),
         compiler_params=pltpu.CompilerParams(
             dimension_semantics=("arbitrary",), vmem_limit_bytes=48 * 1024 * 1024
         ),
-    )(plist, pcount, page_node, page_fill, kfirst, qt, tok, proj, vnt, segk, cache)
+    )(plist, pcount, page_node, page_fill, kfirst, qsel, qt, tok, proj, vnt, segk, ck, cvt)
 
 
 def shift_perm(n, d):
@@ -235,16 +225,28 @@
     qt = projected[:, :group_width].T
     vnt = projected[:, 2 * group_width:].T
     cache = lax.all_gather(cache_kv, "page", axis=1, tiled=True)
-    attn_t = attention(
-        plist, pcount, page_node, page_fill, kfirst, qt, tok, projected, vnt, segk, cache
-    )
-    result = head_reduce_scatter(
-        lax.dot_general(
+    ck = cache[0]
+    cvt = jnp.swapaxes(cache[1], 1, 2)
+    me = lax.axis_index("head")
+    total = None
+    received = []
+    for d in list(range(1, n_head)) + [0]:
+        block = ((me + d) % n_head).astype(jnp.int32)[None]
+        attn_t = attention(
+            plist, pcount, page_node, page_fill, kfirst, block, qt, tok, projected, vnt, segk,
+            ck, cvt,
+        )
+        partial = lax.dot_general(
             attn_t, w_out, (((0,), (0,)), ((), ())), preferred_element_type=jnp.float32
-        ),
-        n_head,
-    )
-    return result[None]
+        )
+        if d == 0:
+            total = partial
+        else:
+            send, qt = lax.optimization_barrier((partial.astype(jnp.bfloat16), qt))
+            received.append(lax.ppermute(send, "head", shift_perm(n_head, d)))
+    for recv in received:
+        total = total + recv.astype(jnp.float32)
+    return total.astype(jnp.bfloat16)[None]
 
 
 def solution(mesh):

time: 153 us -> 157 us (1.026); the launches traced: 156 us -> 156 us
  local copies, waits for them, and re-layouts: 12.3 us -> 24.6 us
  other arithmetic: 14.7 us -> 8.3 us
  matrix products: 3.83 us -> 9.04 us
  waiting for transfers between devices: 50.5 us -> 45.3 us
  Pallas kernels: 50 us -> 46.8 us
  starting transfers between devices: 11.5 us -> 8.75 us
    ppermute x3, waiting for transfers between devices: 22.1 us -> 12.8 us  [shards(): received.append(lax.ppermute(send, 'head', shift_perm(n_head, d)))]
    ppermute x3, waiting for transfers between devices: 14.3 us -> 21.8 us  [head_gather(): lax.ppermute(x, 'head', shift_perm(n, d))]
    squeeze x0 -> x1, local copies, waits for them, and re-layouts: none -> 6.4 us  [shards(): ck = cache[0]]
    transpose x0 -> x1, local copies, waits for them, and re-layouts: none -> 5.93 us  [shards(): cvt = jnp.swapaxes(cache[1], 1, 2)]
    dot_general x1 -> x4, matrix products: 0.77 us -> 5.98 us  [shards(): lax.dot_general(attn_t, w_out, (((0,), (0,)), ((), ())), preferred_elemen...]
    pallas_call x1 -> x4, Pallas kernels: 50 us -> 46.8 us  [attention(): pl.pallas_call(attn_kernel, grid_spec=grid_spec, interpret=INTERPRET, out...]
    all_gather x1, waiting for transfers between devices: 13.3 us -> 10.6 us  [shards(): cache = lax.all_gather(cache_kv, 'page', axis=1, tiled=True)]
    broadcast_in_dim x1 -> x0, other arithmetic: 2.52 us -> none  [shards(): return result[None]]
  transfers between devices with their start and end apart: 7 -> 7, of which waited for: 5 -> 5; matrix products, arithmetic and copies ran while one was open for 15% -> 12% of each run, Pallas kernels for 0% -> 7%
where the time goes in v2:
time: 157 us; the launch traced here: 156 us
  Pallas kernels  46.8 us (30%)
  waiting for transfers between devices  45.3 us (29%)
  local copies, waits for them, and re-layouts  24.6 us (16%)
  between operations  13.6 us (9%)
  matrix products  9.04 us (6%)
  starting transfers between devices  8.75 us (6%)
  other arithmetic  8.3 us (5%)
    pallas_call x4, Pallas kernels, attention(): pl.pallas_call(attn_kernel, grid_spec=grid_spec, interpret=INTERPRET, out...  46.8 us
    ppermute x3, waiting for transfers between devices, head_gather(): lax.ppermute(x, 'head', shift_perm(n, d))  21.8 us
    ppermute x3, waiting for transfers between devices, shards(): received.append(lax.ppermute(send, 'head', shift_perm(n_head, d)))  12.8 us
    all_gather x1, waiting for transfers between devices, shards(): cache = lax.all_gather(cache_kv, 'page', axis=1, tiled=True)  10.6 us
    squeeze x1, local copies, waits for them, and re-layouts, shards(): ck = cache[0]  6.4 us
    dot_general x4, matrix products, shards(): lax.dot_general(attn_t, w_out, (((0,), (0,)), ((), ())), preferred_elemen...  5.98 us
    transpose x1, local copies, waits for them, and re-layouts, shards(): cvt = jnp.swapaxes(cache[1], 1, 2)  5.93 us
    unnamed x28, local copies, waits for them, and re-layouts  5.85 us
  transfers between devices with their start and end apart: 7, of which 5 were waited for; matrix products, arithmetic and copies ran while one was open for 12% of the time, Pallas kernels for 7%

profile of v2, /device:TPU:1, one launch (start us, length us, event | category | flops | bytes accessed | tf_op | source)
XLA Modules:
  0.0 156.3 jit_solution(1955185317206082081)
XLA Ops:
  6.6 1.9 %copy.38 = bf16[2,2,128,256]{2,3,1,0:T(8,128)(2,1)} copy(bf16[2,2,128,256]{3,2,1,0:T(8,128)(2,1)} %param.14) | data formatting | bytes 524288 | tf_op args[4]
  8.6 1.2 fusion.2
  9.8 2.0 %fusion.4 = bf16[256,1024]{1,0:T(8,128)(2,1)} fusion(bf16[1,256,1024]{2,1,0:T(8,128)(2,1)} %param.10, f32[1024]{0:T(1024)} %param.11, f32[256]{0:T(256)S(1)} %add_rsqrt_fusion), kind=kLoop, calls=%fused_computation.15 | loop fusion | flops 1048576 | bytes 1053696 | tf_op jit(solution)/shard_map/convert_element_type | solution.py:187
  11.8 4.6 %collective-permute-start.2 = (bf16[256,1024]{1,0:T(8,128)(2,1)}, bf16[256,1024]{1,0:T(8,128)(2,1)}, u32[]{:S(2)}, u32[]{:S(2)}) collective-permute-start(bf16[256,1024]{1,0:T(8,128)(2,1)} %fusion.4), channel_id=1, source_target_pairs={{0,96},{32,0},{64,32},{96,64},{1,97},{33,1},{65,33},{97,65},{2,98}... | collective-permute-start | bytes 1572872 | tf_op jit(solution)/shard_map/ppermute | solution.py:151
  18.9 1.7 %copy.36 = bf16[1024,3,256]{0,2,1:T(8,128)(2,1)} copy(bf16[1024,3,256]{2,0,1:T(8,128)(2,1)S(1)} %copy-done.7) | data formatting | bytes 3145728 | tf_op args[2]
  20.9 17.5 %collective-permute-done.2 = bf16[256,1024]{1,0:T(8,128)(2,1)} collective-permute-done((bf16[256,1024]{1,0:T(8,128)(2,1)}, bf16[256,1024]{1,0:T(8,128)(2,1)}, u32[]{:S(2)}, u32[]{:S(2)}) %collective-permute-start.2) | collective-permute-done | bytes 524320 | tf_op jit(solution)/shard_map/ppermute | solution.py:151
  38.4 4.3 %collective-permute-done = bf16[256,1024]{1,0:T(8,128)(2,1)} collective-permute-done((bf16[256,1024]{1,0:T(8,128)(2,1)}, bf16[256,1024]{1,0:T(8,128)(2,1)}, u32[]{:S(2)}, u32[]{:S(2)}) %collective-permute-start) | collective-permute-done | bytes 524320 | tf_op jit(solution)/shard_map/ppermute | solution.py:151
  42.7 1.6 %pad_maximum_fusion = bf16[4,256,1024]{2,1,0:T(8,128)(2,1)S(1)} fusion(bf16[1,256,1024]{2,1,0:T(8,128)(2,1)} %bitcast.9, bf16[1,256,1024]{2,1,0:T(8,128)(2,1)} %bitcast.8, bf16[1,256,1024]{2,1,0:T(8,128)(2,1)} %bitcast.7, bf16[1,256,1024]{2,1,0:T(8,128)(2,1)S(1)} %fusion.6), kind=kLoop, calls=%fused_computation.3 | loop fusion | flops 3145728 | bytes 4194304 | tf_op jit(solution)/shard_map/stack | solution.py:152
  44.3 2.1 %gather_fusion = bf16[4,256,1024]{2,1,0:T(8,128)(2,1)} fusion(bf16[4,256,1024]{2,1,0:T(8,128)(2,1)S(1)} %pad_maximum_fusion, s32[1024]{0:T(1024)S(1)} %pad_clamp_fusion), kind=kCustom, calls=%fused_computation | custom fusion | bytes 4194320 | tf_op jit(solution)/shard_map/jit(_take)/gather | solution.py:154
  46.4 2.0 %broadcast_select_fusion = bf16[4,256,1024]{2,1,0:T(8,128)(2,1)S(1)} fusion(bf16[4,256,1024]{2,1,0:T(8,128)(2,1)} %gather_fusion, pred[4]{0:T(512)(128)(4,1)S(1)} %compare_and_fusion), kind=kLoop, calls=%fused_computation.4 | loop fusion | flops 1048576 | bytes 4194308 | tf_op jit(solution)/shard_map/jit(_take)/select_n | solution.py:154
  48.5 3.1 %convolution_convert_fusion = bf16[1024,768]{0,1:T(8,128)(2,1)} fusion(bf16[1024,1024]{1,0:T(8,128)(2,1)S(1)} %bitcast.51, bf16[1024,768]{0,1:T(8,128)(2,1)S(1)} %bitcast.52), kind=kOutput, calls=%fused_computation.5 | convolution fusion | flops 1611399168 | bytes 5242880 | tf_op jit(solution)/shard_map/dot_general | solution.py:192
  51.5 1.7 %copy.39.kn_ref = bf16[1024,768]{1,0:T(8,128)(2,1)S(1)} copy(bf16[1024,768]{0,1:T(8,128)(2,1)} %convolution_convert_fusion) | data formatting | bytes 3145728 | tf_op jit(solution)/shard_map/convert_element_type | solution.py:196
  53.3 2.1 %slice_bitcast_fusion.2 = (bf16[256,1024]{1,0:T(8,128)(2,1)S(1)}, bf16[256,1024]{1,0:T(8,128)(2,1)}) fusion(bf16[1024,768]{0,1:T(8,128)(2,1)} %convolution_convert_fusion), kind=kLoop, calls=%fused_computation.20 | loop fusion | bytes 2097152 | tf_op jit(solution)/shard_map/transpose | solution.py:226
  55.3 10.6 %all-gather.2.cloned.1.call-done = bf16[2,64,128,256]{2,3,1,0:T(8,128)(2,1)} async-done(((bf16[2,2,128,256]{2,3,1,0:T(8,128)(2,1)}), bf16[2,64,128,256]{2,3,1,0:T(8,128)(2,1)}) %all-gather.2.cloned.1.call-update) | async-done | bytes 8388624 | tf_op jit(solution)/shard_map/all_gather | solution.py:227
  65.9 5.9 %slice_bitcast_fusion = (bf16[64,256,128]{2,1,0:T(8,128)(2,1)}, bf16[64,128,256]{1,2,0:T(8,128)(2,1)}) fusion(bf16[2,64,128,256]{2,3,1,0:T(8,128)(2,1)} %all-gather.2.cloned.1.call-done), kind=kLoop, calls=%fused_computation.1 | loop fusion | bytes 16777216 | tf_op jit(solution)/shard_map/transpose | solution.py:229
  71.9 6.4 %copy.41.ck_ref = bf16[64,128,256]{2,1,0:T(8,128)(2,1)} copy(bf16[64,128,256]{1,2,0:T(8,128)(2,1)} %get-tuple-element.18) | data formatting | bytes 8388608 | tf_op jit(solution)/shard_map/squeeze | solution.py:228
  79.3 11.5 %shard_map.100 = bf16[256,256]{1,0:T(8,128)(2,1)S(1)} custom-call(s32[256]{0:T(256)S(1)} %reshape.167.plist_ref, s32[4]{0:T(128)S(1)} %convert_reduce_fusion.1.pcount_ref, s32[64]{0:T(128)S(1)} %copy-done.4, s32[64]{0:T(128)S(1)} %copy-done.5, s32[4]{0:T(128)S(1)} %and_select_fusion.2.kfirst_ref, s32[1]{0:T(128)} %bitcast.5.qsel_ref, ...), custom_call_target="tpu_custom_call" | custom-call | tf_op jit(solution)/shard_map/pallas_call | solution.py:134
  92.0 12.0 %shard_map.101 = bf16[256,256]{1,0:T(8,128)(2,1)S(1)} custom-call(s32[256]{0:T(256)S(1)} %reshape.167.plist_ref, s32[4]{0:T(128)S(1)} %convert_reduce_fusion.1.pcount_ref, s32[64]{0:T(128)S(1)} %copy-done.4, s32[64]{0:T(128)S(1)} %copy-done.5, s32[4]{0:T(128)S(1)} %and_select_fusion.2.kfirst_ref, s32[1]{0:T(128)} %bitcast.4.qsel_ref, ...), custom_call_target="tpu_custom_call" | custom-call | tf_op jit(solution)/shard_map/pallas_call | solution.py:134
  105.2 11.5 %shard_map.102 = bf16[256,256]{1,0:T(8,128)(2,1)S(1)} custom-call(s32[256]{0:T(256)S(1)} %reshape.167.plist_ref, s32[4]{0:T(128)S(1)} %convert_reduce_fusion.1.pcount_ref, s32[64]{0:T(128)S(1)} %copy-done.4, s32[64]{0:T(128)S(1)} %copy-done.5, s32[4]{0:T(128)S(1)} %and_select_fusion.2.kfirst_ref, s32[1]{0:T(128)} %bitcast.3.qsel_ref, ...), custom_call_target="tpu_custom_call" | custom-call | tf_op jit(solution)/shard_map/pallas_call | solution.py:134
  117.8 2.9 %collective-permute-start.5 = (bf16[256,1024]{1,0:T(8,128)(2,1)}, bf16[256,1024]{1,0:T(8,128)(2,1)}, u32[]{:S(2)}, u32[]{:S(2)}) collective-permute-start(bf16[256,1024]{1,0:T(8,128)(2,1)} %convolution_convert_fusion.1), channel_id=1, source_target_pairs={{0,96},{32,0},{64,32},{96,64},{1,97},{33,1},{65,33},{97,65},{2,98}... | collective-permute-start | bytes 1572872 | tf_op jit(solution)/shard_map/ppermute | solution.py:246
  122.3 11.7 %shard_map.103 = bf16[256,256]{1,0:T(8,128)(2,1)S(1)} custom-call(s32[256]{0:T(256)S(1)} %reshape.167.plist_ref, s32[4]{0:T(128)S(1)} %convert_reduce_fusion.1.pcount_ref, s32[64]{0:T(128)S(1)} %copy-done.4, s32[64]{0:T(128)S(1)} %copy-done.5, s32[4]{0:T(128)S(1)} %and_select_fusion.2.kfirst_ref, s32[1]{0:T(128)} %bitcast.2.qsel_ref, ...), custom_call_target="tpu_custom_call" | custom-call | tf_op jit(solution)/shard_map/pallas_call | solution.py:134
  134.0 9.4 %collective-permute-done.5 = bf16[256,1024]{1,0:T(8,128)(2,1)} collective-permute-done((bf16[256,1024]{1,0:T(8,128)(2,1)}, bf16[256,1024]{1,0:T(8,128)(2,1)}, u32[]{:S(2)}, u32[]{:S(2)}) %collective-permute-start.5) | collective-permute-done | bytes 524320 | tf_op jit(solution)/shard_map/ppermute | solution.py:246
  143.4 3.4 %collective-permute-done.3 = bf16[256,1024]{1,0:T(8,128)(2,1)} collective-permute-done((bf16[256,1024]{1,0:T(8,128)(2,1)}, bf16[256,1024]{1,0:T(8,128)(2,1)}, u32[]{:S(2)}, u32[]{:S(2)}) %collective-permute-start.3) | collective-permute-done | bytes 524320 | tf_op jit(solution)/shard_map/ppermute | solution.py:246
  146.8 2.6 %fusion.7 = bf16[1,256,1024]{2,1,0:T(8,128)(2,1)} fusion(bf16[256,1024]{1,0:T(8,128)(2,1)} %collective-permute-done.5, bf16[256,1024]{1,0:T(8,128)(2,1)} %collective-permute-done.4, bf16[256,1024]{1,0:T(8,128)(2,1)} %collective-permute-done.3, bf16[256,256]{1,0:T(8,128)(2,1)S(1)} %shard_map.103, bf16[256,1024]{1,0:T(8,128)(2,1)S(1)} %copy-done), kind=kOutput, calls=%fused_computation.19 | convolution fusion | flops 136052736 | bytes 2752512 | tf_op jit(solution)/shard_map/dot_general | solution.py:239
  (61 shorter events, 8.9 us)
Async XLA Ops:
  6.5 84.3 %copy-start = (bf16[256,1024]{1,0:T(8,128)(2,1)S(1)}, bf16[256,1024]{1,0:T(8,128)(2,1)}, u32[]{:S(2)}) copy-start(bf16[256,1024]{1,0:T(8,128)(2,1)} %param.13) | copy-start | bytes 1572868
  6.5 10.6 %copy-start.9 = (s32[1,1024]{1,0:T(1,128)S(1)}, s32[1,1024]{1,0:T(1,128)}, u32[]{:S(2)}) copy-start(s32[1,1024]{1,0:T(1,128)} %param.18) | copy-start | bytes 12292
  6.5 10.7 %copy-start.12 = (s32[1,8]{1,0:T(1,128)S(1)}, s32[1,8]{1,0:T(1,128)}, u32[]{:S(2)}) copy-start(s32[1,8]{1,0:T(1,128)} %param.19) | copy-start | bytes 100
  6.5 10.8 %copy-start.11 = (s32[19]{0:T(128)S(1)}, s32[19]{0:T(128)}, u32[]{:S(2)}) copy-start(s32[19]{0:T(128)} %param.17) | copy-start | bytes 232
  6.5 11.0 %copy-start.4 = (s32[64]{0:T(128)S(1)}, s32[64]{0:T(128)}, u32[]{:S(2)}) copy-start(s32[64]{0:T(128)} %pnode_ref.7) | copy-start | bytes 772
  6.5 12.3 %copy-start.7 = (bf16[1024,3,256]{2,0,1:T(8,128)(2,1)S(1)}, bf16[1024,3,256]{2,0,1:T(8,128)(2,1)}, u32[]{:S(2)}) copy-start(bf16[1024,3,256]{2,0,1:T(8,128)(2,1)} %param.12) | copy-start | bytes 4718596
  6.6 59.4 %all-gather.2.cloned.1.call-start = ((), (), s32[]{:S(2)}) async-start(), calls=%async_computation | async-start | bytes 8650752 | tf_op jit(solution)/shard_map/all_gather | solution.py:227
  11.8 8.9 %copy-start.6 = (bf16[1,256,1024]{2,1,0:T(8,128)(2,1)S(1)}, bf16[1,256,1024]{2,1,0:T(8,128)(2,1)}, u32[]{:S(2)}) copy-start(bf16[1,256,1024]{2,1,0:T(8,128)(2,1)} %param.10) | copy-start | bytes 1572868
  11.8 8.9 %copy-start.10 = (f32[1024]{0:T(1024)S(1)}, f32[1024]{0:T(1024)}, u32[]{:S(2)}) copy-start(f32[1024]{0:T(1024)} %param.11) | copy-start | bytes 12292
  11.8 26.6 %collective-permute-start.2 = (bf16[256,1024]{1,0:T(8,128)(2,1)}, bf16[256,1024]{1,0:T(8,128)(2,1)}, u32[]{:S(2)}, u32[]{:S(2)}) collective-permute-start(bf16[256,1024]{1,0:T(8,128)(2,1)} %fusion.4), channel_id=1, source_target_pairs={{0,96},{32,0},{64,32},{96,64},{1,97},{33,1},{65,33},{97,65},{2,98}... | collective-permute-start | bytes 1572872 | tf_op jit(solution)/shard_map/ppermute | solution.py:151
  16.4 22.0 %collective-permute-start.1 = (bf16[256,1024]{1,0:T(8,128)(2,1)}, bf16[256,1024]{1,0:T(8,128)(2,1)}, u32[]{:S(2)}, u32[]{:S(2)}) collective-permute-start(bf16[256,1024]{1,0:T(8,128)(2,1)} %fusion.4), channel_id=1, source_target_pairs={{0,64},{32,96},{64,0},{96,32},{1,65},{33,97},{65,1},{97,33},{2,66}... | collective-permute-start | bytes 1572872 | tf_op jit(solution)/shard_map/ppermute | solution.py:151
  16.4 26.3 %collective-permute-start = (bf16[256,1024]{1,0:T(8,128)(2,1)}, bf16[256,1024]{1,0:T(8,128)(2,1)}, u32[]{:S(2)}, u32[]{:S(2)}) collective-permute-start(bf16[256,1024]{1,0:T(8,128)(2,1)} %fusion.4), channel_id=1, source_target_pairs={{0,32},{32,64},{64,96},{96,0},{1,33},{33,65},{65,97},{97,1},{2,34}... | collective-permute-start | bytes 1572872 | tf_op jit(solution)/shard_map/ppermute | solution.py:151
  46.4 2.0 %copy-start.8 = (bf16[1024,3,256]{0,2,1:T(8,128)(2,1)S(1)}, bf16[1024,3,256]{0,2,1:T(8,128)(2,1)}, u32[]{:S(2)}) copy-start(bf16[1024,3,256]{0,2,1:T(8,128)(2,1)} %copy.36) | copy-start | bytes 4718596
  71.9 6.4 %copy-start.5 = (s32[64]{0:T(128)S(1)}, s32[64]{0:T(128)}, u32[]{:S(2)}) copy-start(s32[64]{0:T(128)} %pfill_ref.7) | copy-start | bytes 772
  78.3 1.0 copy-start.1
  92.0 13.2 %copy-start.2 = (bf16[256,1024]{1,0:T(8,128)(2,1)S(1)}, bf16[256,1024]{1,0:T(8,128)(2,1)}, u32[]{:S(2)}) copy-start(bf16[256,1024]{1,0:T(8,128)(2,1)} %get-tuple-element.13.qt_ref) | copy-start | bytes 1572868
  117.8 25.6 %collective-permute-start.5 = (bf16[256,1024]{1,0:T(8,128)(2,1)}, bf16[256,1024]{1,0:T(8,128)(2,1)}, u32[]{:S(2)}, u32[]{:S(2)}) collective-permute-start(bf16[256,1024]{1,0:T(8,128)(2,1)} %convolution_convert_fusion.1), channel_id=1, source_target_pairs={{0,96},{32,0},{64,32},{96,64},{1,97},{33,1},{65,33},{97,65},{2,98}... | collective-permute-start | bytes 1572872 | tf_op jit(solution)/shard_map/ppermute | solution.py:246
  120.7 22.8 %collective-permute-start.4 = (bf16[256,1024]{1,0:T(8,128)(2,1)}, bf16[256,1024]{1,0:T(8,128)(2,1)}, u32[]{:S(2)}, u32[]{:S(2)}) collective-permute-start(bf16[256,1024]{1,0:T(8,128)(2,1)} %convolution_convert_fusion.2), channel_id=1, source_target_pairs={{0,64},{32,96},{64,0},{96,32},{1,65},{33,97},{65,1},{97,33},{2,66}... | collective-permute-start | bytes 1572872 | tf_op jit(solution)/shard_map/ppermute | solution.py:246
  121.1 25.8 %collective-permute-start.3 = (bf16[256,1024]{1,0:T(8,128)(2,1)}, bf16[256,1024]{1,0:T(8,128)(2,1)}, u32[]{:S(2)}, u32[]{:S(2)}) collective-permute-start(bf16[256,1024]{1,0:T(8,128)(2,1)} %convolution_convert_fusion.3), channel_id=1, source_target_pairs={{0,32},{32,64},{64,96},{96,0},{1,33},{33,65},{65,97},{97,1},{2,34}... | collective-permute-start | bytes 1572872 | tf_op jit(solution)/shard_map/ppermute | solution.py:246
  121.3 1.0 copy-start.3
Sparse Core Ops, SparseCore 0:
  9.7 56.1 all-gather.1

commit v3 on v0

--- a/solution.py
+++ b/solution.py
@@ -8,7 +8,7 @@
 HD = 64
 EPSILON = 1e-06
 FLOOR_SCORE = -1e30
-Q_BLOCK = 256
+Q_BLOCK = 512
 K_BLOCK = 128
 INTERPRET = False
 

time: 153 us -> 155 us (1.013)
  the two profiles are of different devices: /device:TPU:1 before, /device:TPU:5 now
where the time goes in v3:
time: 155 us; the launch traced here: 154 us
  waiting for transfers between devices  49.8 us (32%)
  Pallas kernels  49.3 us (32%)
  other arithmetic  14.5 us (9%)
  between operations  13.6 us (9%)
  local copies, waits for them, and re-layouts  12.4 us (8%)
  starting transfers between devices  10.7 us (7%)
  matrix products  3.83 us (2%)
    pallas_call x1, Pallas kernels, attention(): pl.pallas_call(attn_kernel, grid_spec=grid_spec, interpret=INTERPRET, out...  49.3 us
    ppermute x3, waiting for transfers between devices, head_reduce_scatter(): recv = lax.ppermute(send.astype(jnp.bfloat16), 'head', shift_perm(n, d))  21.4 us
    ppermute x3, waiting for transfers between devices, head_gather(): lax.ppermute(x, 'head', shift_perm(n, d))  14.4 us
    all_gather x1, waiting for transfers between devices, shards(): cache = lax.all_gather(cache_kv, 'page', axis=1, tiled=True)  13.3 us
    ppermute x3, starting transfers between devices, head_gather(): lax.ppermute(x, 'head', shift_perm(n, d))  5.67 us
    unnamed x21, local copies, waits for them, and re-layouts  5.14 us
    ppermute x3, starting transfers between devices, head_reduce_scatter(): recv = lax.ppermute(send.astype(jnp.bfloat16), 'head', shift_perm(n, d))  5.01 us
  transfers between devices with their start and end apart: 7, of which 5 were waited for; matrix products, arithmetic and copies ran while one was open for 15% of the time, Pallas kernels for 0%

profile of v3, /device:TPU:5, one launch (start us, length us, event | category | flops | bytes accessed | tf_op | source)
XLA Modules:
  0.0 154.1 jit_solution(2298860359488694561)
XLA Ops:
  7.3 1.2 fusion.2
  8.5 2.0 %fusion.4 = bf16[256,1024]{1,0:T(8,128)(2,1)} fusion(bf16[1,256,1024]{2,1,0:T(8,128)(2,1)} %param.10, f32[1024]{0:T(1024)} %param.11, f32[256]{0:T(256)S(1)} %add_rsqrt_fusion), kind=kLoop, calls=%fused_computation.10 | loop fusion | flops 1048576 | bytes 1053696 | tf_op jit(solution)/shard_map/convert_element_type | solution.py:197
  10.5 1.6 %collective-permute-start = (bf16[256,1024]{1,0:T(8,128)(2,1)}, bf16[256,1024]{1,0:T(8,128)(2,1)}, u32[]{:S(2)}, u32[]{:S(2)}) collective-permute-start(bf16[256,1024]{1,0:T(8,128)(2,1)} %fusion.4), channel_id=1, source_target_pairs={{0,32},{32,64},{64,96},{96,0},{1,33},{33,65},{65,97},{97,1},{2,34}... | collective-permute-start | bytes 1572872 | tf_op jit(solution)/shard_map/ppermute | solution.py:161
  12.2 3.3 %collective-permute-start.1 = (bf16[256,1024]{1,0:T(8,128)(2,1)}, bf16[256,1024]{1,0:T(8,128)(2,1)}, u32[]{:S(2)}, u32[]{:S(2)}) collective-permute-start(bf16[256,1024]{1,0:T(8,128)(2,1)} %fusion.4), channel_id=1, source_target_pairs={{0,64},{32,96},{64,0},{96,32},{1,65},{33,97},{65,1},{97,33},{2,66}... | collective-permute-start | bytes 1572872 | tf_op jit(solution)/shard_map/ppermute | solution.py:161
  19.3 0.9 or_reduce_fusion
  21.7 1.7 %copy.17 = bf16[1024,3,256]{0,2,1:T(8,128)(2,1)} copy(bf16[1024,3,256]{2,0,1:T(8,128)(2,1)S(1)} %copy-done.6) | data formatting | bytes 3145728 | tf_op args[2]
  24.0 2.2 %collective-permute-done = bf16[256,1024]{1,0:T(8,128)(2,1)} collective-permute-done((bf16[256,1024]{1,0:T(8,128)(2,1)}, bf16[256,1024]{1,0:T(8,128)(2,1)}, u32[]{:S(2)}, u32[]{:S(2)}) %collective-permute-start) | collective-permute-done | bytes 524320 | tf_op jit(solution)/shard_map/ppermute | solution.py:161
  26.2 12.1 %collective-permute-done.1 = bf16[256,1024]{1,0:T(8,128)(2,1)} collective-permute-done((bf16[256,1024]{1,0:T(8,128)(2,1)}, bf16[256,1024]{1,0:T(8,128)(2,1)}, u32[]{:S(2)}, u32[]{:S(2)}) %collective-permute-start.1) | collective-permute-done | bytes 524320 | tf_op jit(solution)/shard_map/ppermute | solution.py:161
  38.4 1.6 %pad_maximum_fusion = bf16[4,256,1024]{2,1,0:T(8,128)(2,1)S(1)} fusion(bf16[1,256,1024]{2,1,0:T(8,128)(2,1)} %bitcast.5, bf16[1,256,1024]{2,1,0:T(8,128)(2,1)} %bitcast.4, bf16[1,256,1024]{2,1,0:T(8,128)(2,1)} %bitcast.3, bf16[1,256,1024]{2,1,0:T(8,128)(2,1)S(1)} %fusion.6), kind=kLoop, calls=%fused_computation.1 | loop fusion | flops 3145728 | bytes 4194304 | tf_op jit(solution)/shard_map/stack | solution.py:162
  40.0 2.1 %gather_fusion = bf16[4,256,1024]{2,1,0:T(8,128)(2,1)} fusion(bf16[4,256,1024]{2,1,0:T(8,128)(2,1)S(1)} %pad_maximum_fusion, s32[1024]{0:T(1024)S(1)} %pad_clamp_fusion), kind=kCustom, calls=%fused_computation | custom fusion | bytes 4194320 | tf_op jit(solution)/shard_map/jit(_take)/gather | solution.py:164
  42.1 2.3 %broadcast_select_fusion = bf16[4,256,1024]{2,1,0:T(8,128)(2,1)S(1)} fusion(bf16[4,256,1024]{2,1,0:T(8,128)(2,1)} %gather_fusion, pred[4]{0:T(512)(128)(4,1)S(1)} %compare_and_fusion), kind=kLoop, calls=%fused_computation.2 | loop fusion | flops 1048576 | bytes 4194308 | tf_op jit(solution)/shard_map/jit(_take)/select_n | solution.py:164
  44.8 3.1 %convolution_convert_fusion = bf16[1024,768]{0,1:T(8,128)(2,1)} fusion(bf16[1024,1024]{1,0:T(8,128)(2,1)S(1)} %bitcast.54, bf16[1024,768]{0,1:T(8,128)(2,1)S(1)} %bitcast.55), kind=kOutput, calls=%fused_computation.3 | convolution fusion | flops 1611399168 | bytes 5242880 | tf_op jit(solution)/shard_map/dot_general | solution.py:202
  47.8 1.8 %copy.19.kn_ref = bf16[1024,768]{1,0:T(8,128)(2,1)S(1)} copy(bf16[1024,768]{0,1:T(8,128)(2,1)} %convolution_convert_fusion) | data formatting | bytes 3145728 | tf_op jit(solution)/shard_map/convert_element_type | solution.py:206
  49.6 2.1 %slice_bitcast_fusion = (bf16[256,1024]{1,0:T(8,128)(2,1)S(1)}, bf16[256,1024]{1,0:T(8,128)(2,1)}) fusion(bf16[1024,768]{0,1:T(8,128)(2,1)} %convolution_convert_fusion), kind=kLoop, calls=%fused_computation.24 | loop fusion | bytes 2097152 | tf_op jit(solution)/shard_map/transpose | solution.py:236
  51.7 13.3 %all-gather.2.cloned.1.call-done.cache_ref = bf16[2,64,128,256]{3,2,1,0:T(8,128)(2,1)} async-done(((bf16[2,2,128,256]{3,2,1,0:T(8,128)(2,1)}), bf16[2,64,128,256]{3,2,1,0:T(8,128)(2,1)}) %all-gather.2.cloned.1.call-update) | async-done | bytes 8388624 | tf_op jit(solution)/shard_map/all_gather | solution.py:237
  65.0 1.0 copy-done.1
  66.1 49.3 %shard_map.100 = bf16[256,1024]{1,0:T(8,128)(2,1)S(1)} custom-call(s32[128]{0:T(128)S(1)} %reshape.173.plist_ref, s32[2]{0:T(128)S(1)} %convert_reduce_fusion.pcount_ref, s32[64]{0:T(128)S(1)} %copy-done.2, s32[64]{0:T(128)S(1)} %copy-done.3, s32[2]{0:T(128)S(1)} %and_select_fusion.2.kfirst_ref, bf16[256,1024]{1,0:T(8,128)(2,1)S(1)} %copy-done.1, ...), custom_call_target="tpu_custom_call" | custom-call | tf_op jit(solution)/shard_map/pallas_call | solution.py:144
  116.2 1.9 %copy-done.4 = f32[1024,1024]{1,0:T(8,128)} copy-done((f32[1024,1024]{1,0:T(8,128)}, f32[1024,1024]{1,0:T(8,128)S(1)}, u32[]{:S(2)}) %copy-start.4) | copy-done | bytes 4194328
  118.4 1.3 collective-permute-start.3
  119.7 2.6 %collective-permute-start.4 = (bf16[256,1024]{1,0:T(8,128)(2,1)S(1)}, bf16[256,1024]{1,0:T(8,128)(2,1)S(1)}, u32[]{:S(2)}, u32[]{:S(2)}) collective-permute-start(bf16[256,1024]{1,0:T(8,128)(2,1)S(1)} %get-tuple-element.7), channel_id=1, source_target_pairs={{0,64},{32,96},{64,0},{96,32},{1,65},{33,97},{65,1},{97,33},{2,66}... | collective-permute-start | bytes 1572872 | tf_op jit(solution)/shard_map/ppermute | solution.py:175
  122.3 1.1 collective-permute-start.5
  123.4 9.0 %collective-permute-done.3 = bf16[256,1024]{1,0:T(8,128)(2,1)S(1)} collective-permute-done((bf16[256,1024]{1,0:T(8,128)(2,1)S(1)}, bf16[256,1024]{1,0:T(8,128)(2,1)S(1)}, u32[]{:S(2)}, u32[]{:S(2)}) %collective-permute-start.3) | collective-permute-done | bytes 524320 | tf_op jit(solution)/shard_map/ppermute | solution.py:175
  132.3 12.4 %collective-permute-done.4 = bf16[256,1024]{1,0:T(8,128)(2,1)S(1)} collective-permute-done((bf16[256,1024]{1,0:T(8,128)(2,1)S(1)}, bf16[256,1024]{1,0:T(8,128)(2,1)S(1)}, u32[]{:S(2)}, u32[]{:S(2)}) %collective-permute-start.4) | collective-permute-done | bytes 524320 | tf_op jit(solution)/shard_map/ppermute | solution.py:175
  144.8 2.5 %fusion.13 = bf16[1,256,1024]{2,1,0:T(8,128)(2,1)} fusion(bf16[256,1024]{1,0:T(8,128)(2,1)} %collective-permute-done.5, bf16[256,1024]{1,0:T(8,128)(2,1)S(1)} %collective-permute-done.4, bf16[256,1024]{1,0:T(8,128)(2,1)S(1)} %collective-permute-done.3, f32[4,256,1024]{2,1,0:T(8,128)} %bitcast.53, s32[]{:T(128)S(6)} %select_n.106), kind=kLoop, calls=%fused_computation.23 | loop fusion | flops 1835008 | bytes 3145732 | tf_op jit(solution)/shard_map/broadcast_in_dim | solution.py:247
  (48 shorter events, 7.9 us)
Async XLA Ops:
  6.5 108.9 %copy-start = (bf16[256,1024]{1,0:T(8,128)(2,1)S(1)}, bf16[256,1024]{1,0:T(8,128)(2,1)}, u32[]{:S(2)}) copy-start(bf16[256,1024]{1,0:T(8,128)(2,1)} %param.13) | copy-start | bytes 1572868
  6.5 15.2 %copy-start.6 = (bf16[1024,3,256]{2,0,1:T(8,128)(2,1)S(1)}, bf16[1024,3,256]{2,0,1:T(8,128)(2,1)}, u32[]{:S(2)}) copy-start(bf16[1024,3,256]{2,0,1:T(8,128)(2,1)} %param.12) | copy-start | bytes 4718596
  6.5 58.5 %all-gather.2.cloned.1.call-start = ((), (), s32[]{:S(2)}) async-start(), calls=%async_computation | async-start | bytes 8650752 | tf_op jit(solution)/shard_map/all_gather | solution.py:237
  8.5 15.0 %copy-start.8 = (s32[1,1024]{1,0:T(1,128)S(1)}, s32[1,1024]{1,0:T(1,128)}, u32[]{:S(2)}) copy-start(s32[1,1024]{1,0:T(1,128)} %param.18) | copy-start | bytes 12292
  10.5 13.3 %copy-start.5 = (bf16[1,256,1024]{2,1,0:T(8,128)(2,1)S(1)}, bf16[1,256,1024]{2,1,0:T(8,128)(2,1)}, u32[]{:S(2)}) copy-start(bf16[1,256,1024]{2,1,0:T(8,128)(2,1)} %param.10) | copy-start | bytes 1572868
  10.5 13.3 %copy-start.9 = (f32[1024]{0:T(1024)S(1)}, f32[1024]{0:T(1024)}, u32[]{:S(2)}) copy-start(f32[1024]{0:T(1024)} %param.11) | copy-start | bytes 12292
  10.5 15.7 %collective-permute-start = (bf16[256,1024]{1,0:T(8,128)(2,1)}, bf16[256,1024]{1,0:T(8,128)(2,1)}, u32[]{:S(2)}, u32[]{:S(2)}) collective-permute-start(bf16[256,1024]{1,0:T(8,128)(2,1)} %fusion.4), channel_id=1, source_target_pairs={{0,32},{32,64},{64,96},{96,0},{1,33},{33,65},{65,97},{97,1},{2,34}... | collective-permute-start | bytes 1572872 | tf_op jit(solution)/shard_map/ppermute | solution.py:161
  12.2 26.2 %collective-permute-start.1 = (bf16[256,1024]{1,0:T(8,128)(2,1)}, bf16[256,1024]{1,0:T(8,128)(2,1)}, u32[]{:S(2)}, u32[]{:S(2)}) collective-permute-start(bf16[256,1024]{1,0:T(8,128)(2,1)} %fusion.4), channel_id=1, source_target_pairs={{0,64},{32,96},{64,0},{96,32},{1,65},{33,97},{65,1},{97,33},{2,66}... | collective-permute-start | bytes 1572872 | tf_op jit(solution)/shard_map/ppermute | solution.py:161
  15.5 22.9 %collective-permute-start.2 = (bf16[256,1024]{1,0:T(8,128)(2,1)}, bf16[256,1024]{1,0:T(8,128)(2,1)}, u32[]{:S(2)}, u32[]{:S(2)}) collective-permute-start(bf16[256,1024]{1,0:T(8,128)(2,1)} %fusion.4), channel_id=1, source_target_pairs={{0,96},{32,0},{64,32},{96,64},{1,97},{33,1},{65,33},{97,65},{2,98}... | collective-permute-start | bytes 1572872 | tf_op jit(solution)/shard_map/ppermute | solution.py:161
  42.1 2.7 %copy-start.7 = (bf16[1024,3,256]{0,2,1:T(8,128)(2,1)S(1)}, bf16[1024,3,256]{0,2,1:T(8,128)(2,1)}, u32[]{:S(2)}) copy-start(bf16[1024,3,256]{0,2,1:T(8,128)(2,1)} %copy.17) | copy-start | bytes 4718596
  47.8 17.2 %copy-start.2 = (s32[64]{0:T(128)S(1)}, s32[64]{0:T(128)}, u32[]{:S(2)}) copy-start(s32[64]{0:T(128)} %pnode_ref.1) | copy-start | bytes 772
  47.8 17.2 %copy-start.3 = (s32[64]{0:T(128)S(1)}, s32[64]{0:T(128)}, u32[]{:S(2)}) copy-start(s32[64]{0:T(128)} %pfill_ref.1) | copy-start | bytes 772
  65.0 1.0 copy-start.1
  116.2 1.9 %copy-start.4 = (f32[1024,1024]{1,0:T(8,128)}, f32[1024,1024]{1,0:T(8,128)S(1)}, u32[]{:S(2)}) copy-start(f32[1024,1024]{1,0:T(8,128)S(1)} %fusion.19) | copy-start | bytes 12582916
  118.4 14.0 %collective-permute-start.3 = (bf16[256,1024]{1,0:T(8,128)(2,1)S(1)}, bf16[256,1024]{1,0:T(8,128)(2,1)S(1)}, u32[]{:S(2)}, u32[]{:S(2)}) collective-permute-start(bf16[256,1024]{1,0:T(8,128)(2,1)S(1)} %get-tuple-element.5), channel_id=1, source_target_pairs={{0,32},{32,64},{64,96},{96,0},{1,33},{33,65},{65,97},{97,1},{2,34}... | collective-permute-start | bytes 1572872 | tf_op jit(solution)/shard_map/ppermute | solution.py:175
  119.7 25.1 %collective-permute-start.4 = (bf16[256,1024]{1,0:T(8,128)(2,1)S(1)}, bf16[256,1024]{1,0:T(8,128)(2,1)S(1)}, u32[]{:S(2)}, u32[]{:S(2)}) collective-permute-start(bf16[256,1024]{1,0:T(8,128)(2,1)S(1)} %get-tuple-element.7), channel_id=1, source_target_pairs={{0,64},{32,96},{64,0},{96,32},{1,65},{33,97},{65,1},{97,33},{2,66}... | collective-permute-start | bytes 1572872 | tf_op jit(solution)/shard_map/ppermute | solution.py:175
  122.3 22.5 %collective-permute-start.5 = (bf16[256,1024]{1,0:T(8,128)(2,1)S(1)}, bf16[256,1024]{1,0:T(8,128)(2,1)}, u32[]{:S(2)}, u32[]{:S(2)}) collective-permute-start(bf16[256,1024]{1,0:T(8,128)(2,1)S(1)} %get-tuple-element.6), channel_id=1, source_target_pairs={{0,96},{32,0},{64,32},{96,64},{1,97},{33,1},{65,33},{97,65},{2,98}... | collective-permute-start | bytes 1572872 | tf_op jit(solution)/shard_map/ppermute | solution.py:175
Sparse Core Ops, SparseCore 0:
  9.7 55.2 all-gather.1

commit v4 on v2

--- a/solution.py
+++ b/solution.py
@@ -5,6 +5,7 @@
 from jax.experimental.pallas import tpu as pltpu
 from jax.sharding import PartitionSpec as P
 
+
 HD = 64
 EPSILON = 1e-06
 FLOOR_SCORE = -1e30
@@ -20,15 +21,15 @@
 
 def attn_kernel(
     plist_ref, pcount_ref, pnode_ref, pfill_ref, kfirst_ref, qsel_ref,
-    qt_ref, tok_ref, kn_ref, vnt_ref, segk_ref, ck_ref, cvt_ref,
+    qt_ref, tok_ref, kn_ref, vnt_ref, segk_ref, cache_ref, cvt_ref,
     o_ref,
     ma_sc, la_sc, acca_sc, mb_sc, lb_sc, accb_sc,
 ):
     i = qsel_ref[0]
     width, tq = qt_ref.shape
     groups = width // HD
-    pages = ck_ref.shape[0]
-    kb = ck_ref.shape[1]
+    pages = cache_ref.shape[1]
+    kb = cache_ref.shape[2]
 
     qt = qt_ref[...] * jnp.asarray(0.125, jnp.bfloat16)
     seg_q = tok_ref[0:1, :]
@@ -90,8 +91,8 @@
     def pair_step(j, carry):
         g0 = plist_ref[i * pages + 2 * j]
         g1 = plist_ref[i * pages + 2 * j + 1]
-        update(chain_a, ck_ref[g0], cvt_ref[g0], page_mask(g0, True))
-        update(chain_b, ck_ref[g1], cvt_ref[g1], page_mask(g1, 2 * j + 1 < count))
+        update(chain_a, cache_ref[0, g0], cvt_ref[g0], page_mask(g0, True))
+        update(chain_b, cache_ref[0, g1], cvt_ref[g1], page_mask(g1, 2 * j + 1 < count))
         return carry
 
     lax.fori_loop(0, (count + 1) // 2, pair_step, 0)
@@ -108,7 +109,7 @@
     o_ref[...] = jnp.concatenate(parts, axis=0).astype(o_ref.dtype)
 
 
-def attention(plist, pcount, page_node, page_fill, kfirst, qsel, qt, tok, proj, vnt, segk, ck, cvt):
+def attention(plist, pcount, page_node, page_fill, kfirst, qsel, qt, tok, proj, vnt, segk, cache, cvt):
     width, tokens = qt.shape
     groups = width // HD
     state = [
@@ -139,7 +140,23 @@
         compiler_params=pltpu.CompilerParams(
             dimension_semantics=("arbitrary",), vmem_limit_bytes=48 * 1024 * 1024
         ),
-    )(plist, pcount, page_node, page_fill, kfirst, qsel, qt, tok, proj, vnt, segk, ck, cvt)
+    )(plist, pcount, page_node, page_fill, kfirst, qsel, qt, tok, proj, vnt, segk, cache, cvt)
+
+
+def transpose_kernel(v_ref, o_ref):
+    o_ref[0] = v_ref[0, 0].astype(jnp.float32).T.astype(o_ref.dtype)
+
+
+def transpose_values(cache):
+    pages, kb, width = cache.shape[1:]
+    return pl.pallas_call(
+        transpose_kernel,
+        grid=(pages,),
+        in_specs=[pl.BlockSpec((1, 1, kb, width), lambda g: (1, g, 0, 0))],
+        out_specs=pl.BlockSpec((1, width, kb), lambda g: (g, 0, 0)),
+        out_shape=jax.ShapeDtypeStruct((pages, width, kb), cache.dtype),
+        interpret=INTERPRET,
+    )(cache)
 
 
 def shift_perm(n, d):
@@ -155,19 +172,7 @@
     return gathered.reshape(n * x.shape[0], x.shape[1])
 
 
-def head_reduce_scatter(partial, n):
-    me = lax.axis_index("head")
-    rows = partial.shape[0] // n
-    chunks = partial.reshape(n, rows, partial.shape[1])
-    total = lax.dynamic_index_in_dim(chunks, me, 0, keepdims=False)
-    for d in range(1, n):
-        send = lax.dynamic_index_in_dim(chunks, (me + d) % n, 0, keepdims=False)
-        recv = lax.ppermute(send.astype(jnp.bfloat16), "head", shift_perm(n, d))
-        total = total + recv.astype(jnp.float32)
-    return total.astype(jnp.bfloat16)
-
-
-def shards(
+def shards_body(
     hidden_in,
     norm_gain,
     w_qkv,
@@ -225,16 +230,15 @@
     qt = projected[:, :group_width].T
     vnt = projected[:, 2 * group_width:].T
     cache = lax.all_gather(cache_kv, "page", axis=1, tiled=True)
-    ck = cache[0]
-    cvt = jnp.swapaxes(cache[1], 1, 2)
+    cvt = transpose_values(cache)
     me = lax.axis_index("head")
     total = None
     received = []
     for d in list(range(1, n_head)) + [0]:
         block = ((me + d) % n_head).astype(jnp.int32)[None]
         attn_t = attention(
-            plist, pcount, page_node, page_fill, kfirst, block, qt, tok, projected, vnt, segk,
-            ck, cvt,
+            plist, pcount, page_node, page_fill, kfirst, block, qt, tok, projected, vnt,
+            segk, cache, cvt,
         )
         partial = lax.dot_general(
             attn_t, w_out, (((0,), (0,)), ((), ())), preferred_element_type=jnp.float32
@@ -263,5 +267,5 @@
         P("page", None),
     )
     return jax.shard_map(
-        shards, mesh=mesh, in_specs=placed, out_specs=P("page", "head", None), check_vma=False
-    )
+        shards_body, mesh=mesh, in_specs=placed, out_specs=P("page", "head", None), check_vma=False
+    )

time: 157 us -> 186 us (1.18); the launches traced: 156 us -> 183 us
  Pallas kernels: 46.8 us -> 83.2 us
  local copies, waits for them, and re-layouts: 24.6 us -> 11.6 us
  other arithmetic: 8.3 us -> 11.7 us
  waiting for transfers between devices: 45.3 us -> 42.3 us
  starting transfers between devices: 8.75 us -> 11.4 us
    pallas_call x0 -> x1, Pallas kernels: none -> 34.4 us  [transpose_values(): pl.pallas_call(transpose_kernel, grid=(pages,), in_specs=[pl.BlockSpec((1...]
    squeeze x1 -> x0, local copies, waits for them, and re-layouts: 6.4 us -> none  [shards(): ck = cache[0]]
    transpose x2 -> x1, local copies, waits for them, and re-layouts: 8.02 us -> 2.07 us  [shards_body(): vnt = projected[:, 2 * group_width:].T]
    ppermute x3, waiting for transfers between devices: 21.8 us -> 17.1 us  [head_gather(): lax.ppermute(x, 'head', shift_perm(n, d))]
    ppermute x3, starting transfers between devices: 3.43 us -> 6.11 us  [shards_body(): received.append(lax.ppermute(send, 'head', shift_perm(n_head, d)))]
    reduce_sum x3, other arithmetic: 0.25 us -> 2.27 us  [lookup(): return jnp.sum(jnp.where(matches, lookup_table[None, :], 0), axis=1)]
    pallas_call x4, Pallas kernels: 46.8 us -> 48.7 us  [attention(): pl.pallas_call(attn_kernel, grid_spec=grid_spec, interpret=INTERPRET, out...]
    unnamed x28 -> x23, local copies, waits for them, and re-layouts: 5.85 us -> 3.91 us
  transfers between devices with their start and end apart: 7 -> 7, of which waited for: 5 -> 5; matrix products, arithmetic and copies ran while one was open for 12% -> 13% of each run, Pallas kernels for 7% -> 7%
where the time goes in v4:
time: 186 us; the launch traced here: 183 us
  Pallas kernels  83.2 us (45%)
  waiting for transfers between devices  42.3 us (23%)
  between operations  13.6 us (7%)
  other arithmetic  11.7 us (6%)
  local copies, waits for them, and re-layouts  11.6 us (6%)
  starting transfers between devices  11.4 us (6%)
  matrix products  9.09 us (5%)
    pallas_call x4, Pallas kernels, attention(): pl.pallas_call(attn_kernel, grid_spec=grid_spec, interpret=INTERPRET, out...  48.7 us
    pallas_call x1, Pallas kernels, transpose_values(): pl.pallas_call(transpose_kernel, grid=(pages,), in_specs=[pl.BlockSpec((1...  34.4 us
    ppermute x3, waiting for transfers between devices, head_gather(): lax.ppermute(x, 'head', shift_perm(n, d))  17.1 us
    ppermute x3, waiting for transfers between devices, shards_body(): received.append(lax.ppermute(send, 'head', shift_perm(n_head, d)))  12.6 us
    all_gather x1, waiting for transfers between devices, shards_body(): cache = lax.all_gather(cache_kv, 'page', axis=1, tiled=True)  11.9 us
    ppermute x3, starting transfers between devices, shards_body(): received.append(lax.ppermute(send, 'head', shift_perm(n_head, d)))  6.11 us
    dot_general x4, matrix products, shards_body(): lax.dot_general(attn_t, w_out, (((0,), (0,)), ((), ())), preferred_elemen...  6.03 us
    ppermute x3, starting transfers between devices, head_gather(): lax.ppermute(x, 'head', shift_perm(n, d))  5.27 us
  transfers between devices with their start and end apart: 7, of which 5 were waited for; matrix products, arithmetic and copies ran while one was open for 13% of the time, Pallas kernels for 7%

profile of v4, /device:TPU:1, one launch (start us, length us, event | category | flops | bytes accessed | tf_op | source)
XLA Modules:
  0.0 182.8 jit_solution(16616058920678460080)
XLA Ops:
  7.3 1.2 fusion.2
  8.5 2.0 %fusion.4 = bf16[256,1024]{1,0:T(8,128)(2,1)} fusion(bf16[1,256,1024]{2,1,0:T(8,128)(2,1)} %param.10, f32[1024]{0:T(1024)} %param.11, f32[256]{0:T(256)S(1)} %add_rsqrt_fusion), kind=kLoop, calls=%fused_computation.13 | loop fusion | flops 1048576 | bytes 1053696 | tf_op jit(solution)/shard_map/convert_element_type | solution.py:192
  10.5 4.6 %collective-permute-start.2 = (bf16[256,1024]{1,0:T(8,128)(2,1)}, bf16[256,1024]{1,0:T(8,128)(2,1)}, u32[]{:S(2)}, u32[]{:S(2)}) collective-permute-start(bf16[256,1024]{1,0:T(8,128)(2,1)} %fusion.4), channel_id=1, source_target_pairs={{0,96},{32,0},{64,32},{96,64},{1,97},{33,1},{65,33},{97,65},{2,98}... | collective-permute-start | bytes 1572872 | tf_op jit(solution)/shard_map/ppermute | solution.py:168
  22.3 1.7 copy.26
  24.3 12.8 %collective-permute-done.2 = bf16[256,1024]{1,0:T(8,128)(2,1)} collective-permute-done((bf16[256,1024]{1,0:T(8,128)(2,1)}, bf16[256,1024]{1,0:T(8,128)(2,1)}, u32[]{:S(2)}, u32[]{:S(2)}) %collective-permute-start.2) | collective-permute-done | bytes 524320 | tf_op jit(solution)/shard_map/ppermute | solution.py:168
  37.1 4.3 %collective-permute-done = bf16[256,1024]{1,0:T(8,128)(2,1)} collective-permute-done((bf16[256,1024]{1,0:T(8,128)(2,1)}, bf16[256,1024]{1,0:T(8,128)(2,1)}, u32[]{:S(2)}, u32[]{:S(2)}) %collective-permute-start) | collective-permute-done | bytes 524320 | tf_op jit(solution)/shard_map/ppermute | solution.py:168
  41.4 1.6 pad_maximum_fusion
  43.1 2.1 %gather_fusion = bf16[4,256,1024]{2,1,0:T(8,128)(2,1)} fusion(bf16[4,256,1024]{2,1,0:T(8,128)(2,1)S(1)} %pad_maximum_fusion, s32[1024]{0:T(1024)S(1)} %pad_clamp_fusion), kind=kCustom, calls=%fused_computation | custom fusion | bytes 4194320 | tf_op jit(solution)/shard_map/jit(_take)/gather | solution.py:171
  45.1 2.0 %broadcast_select_fusion = bf16[4,256,1024]{2,1,0:T(8,128)(2,1)S(1)} fusion(bf16[4,256,1024]{2,1,0:T(8,128)(2,1)} %gather_fusion, pred[4]{0:T(512)(128)(4,1)S(1)} %compare_and_fusion), kind=kLoop, calls=%fused_computation.2 | loop fusion | flops 1048576 | bytes 4194308 | tf_op jit(solution)/shard_map/jit(_take)/select_n | solution.py:171
  47.2 3.1 %convolution_convert_fusion = bf16[1024,768]{0,1:T(8,128)(2,1)} fusion(bf16[1024,1024]{1,0:T(8,128)(2,1)S(1)} %bitcast.45, bf16[1024,768]{0,1:T(8,128)(2,1)S(1)} %bitcast.46), kind=kOutput, calls=%fused_computation.3 | convolution fusion | flops 1611399168 | bytes 5242880 | tf_op jit(solution)/shard_map/dot_general | solution.py:197
  50.2 1.7 copy.28.kn_ref
  52.0 2.1 %slice_bitcast_fusion = (bf16[256,1024]{1,0:T(8,128)(2,1)S(1)}, bf16[256,1024]{1,0:T(8,128)(2,1)}) fusion(bf16[1024,768]{0,1:T(8,128)(2,1)} %convolution_convert_fusion), kind=kLoop, calls=%fused_computation.18 | loop fusion | bytes 2097152 | tf_op jit(solution)/shard_map/transpose | solution.py:231
  54.0 11.9 %all-gather.2.cloned.1.call-done.v_ref.cache_ref = bf16[2,64,128,256]{3,2,1,0:T(8,128)(2,1)} async-done(((bf16[2,2,128,256]{3,2,1,0:T(8,128)(2,1)}), bf16[2,64,128,256]{3,2,1,0:T(8,128)(2,1)}) %all-gather.2.cloned.1.call-update) | async-done | bytes 8388624 | tf_op jit(solution)/shard_map/all_gather | solution.py:232
  65.9 34.4 %shard_map.100.cvt_ref = bf16[64,256,128]{2,1,0:T(8,128)(2,1)} custom-call(bf16[2,64,128,256]{3,2,1,0:T(8,128)(2,1)} %all-gather.2.cloned.1.call-done.v_ref.cache_ref), custom_call_target="tpu_custom_call" | custom-call | tf_op jit(solution)/shard_map/pallas_call | solution.py:152
  101.4 15.5 %shard_map.101 = bf16[256,256]{1,0:T(8,128)(2,1)S(1)} custom-call(s32[256]{0:T(256)S(1)} %reshape.167.plist_ref, s32[4]{0:T(128)S(1)} %convert_reduce_fusion.1.pcount_ref, s32[64]{0:T(128)S(1)} %copy-done.4, s32[64]{0:T(128)S(1)} %copy-done.5, s32[4]{0:T(128)S(1)} %and_select_fusion.2.kfirst_ref, s32[1]{0:T(128)} %bitcast.5.qsel_ref, ...), custom_call_target="tpu_custom_call" | custom-call | tf_op jit(solution)/shard_map/pallas_call | solution.py:135
  116.9 1.1 convolution_convert_fusion.3
  118.0 11.9 %shard_map.102 = bf16[256,256]{1,0:T(8,128)(2,1)S(1)} custom-call(s32[256]{0:T(256)S(1)} %reshape.167.plist_ref, s32[4]{0:T(128)S(1)} %convert_reduce_fusion.1.pcount_ref, s32[64]{0:T(128)S(1)} %copy-done.4, s32[64]{0:T(128)S(1)} %copy-done.5, s32[4]{0:T(128)S(1)} %and_select_fusion.2.kfirst_ref, s32[1]{0:T(128)} %bitcast.4.qsel_ref, ...), custom_call_target="tpu_custom_call" | custom-call | tf_op jit(solution)/shard_map/pallas_call | solution.py:135
  130.0 1.2 convolution_convert_fusion.2
  131.1 9.2 %shard_map.103 = bf16[256,256]{1,0:T(8,128)(2,1)S(1)} custom-call(s32[256]{0:T(256)S(1)} %reshape.167.plist_ref, s32[4]{0:T(128)S(1)} %convert_reduce_fusion.1.pcount_ref, s32[64]{0:T(128)S(1)} %copy-done.4, s32[64]{0:T(128)S(1)} %copy-done.5, s32[4]{0:T(128)S(1)} %and_select_fusion.2.kfirst_ref, s32[1]{0:T(128)} %bitcast.3.qsel_ref, ...), custom_call_target="tpu_custom_call" | custom-call | tf_op jit(solution)/shard_map/pallas_call | solution.py:135
  141.5 5.5 %collective-permute-start.5 = (bf16[256,1024]{1,0:T(8,128)(2,1)}, bf16[256,1024]{1,0:T(8,128)(2,1)}, u32[]{:S(2)}, u32[]{:S(2)}) collective-permute-start(bf16[256,1024]{1,0:T(8,128)(2,1)} %convolution_convert_fusion.1), channel_id=1, source_target_pairs={{0,96},{32,0},{64,32},{96,64},{1,97},{33,1},{65,33},{97,65},{2,98}... | collective-permute-start | bytes 1572872 | tf_op jit(solution)/shard_map/ppermute | solution.py:250
  148.7 12.1 %shard_map.104 = bf16[256,256]{1,0:T(8,128)(2,1)S(1)} custom-call(s32[256]{0:T(256)S(1)} %reshape.167.plist_ref, s32[4]{0:T(128)S(1)} %convert_reduce_fusion.1.pcount_ref, s32[64]{0:T(128)S(1)} %copy-done.4, s32[64]{0:T(128)S(1)} %copy-done.5, s32[4]{0:T(128)S(1)} %and_select_fusion.2.kfirst_ref, s32[1]{0:T(128)} %bitcast.2.qsel_ref, ...), custom_call_target="tpu_custom_call" | custom-call | tf_op jit(solution)/shard_map/pallas_call | solution.py:135
  160.8 7.3 %collective-permute-done.5 = bf16[256,1024]{1,0:T(8,128)(2,1)} collective-permute-done((bf16[256,1024]{1,0:T(8,128)(2,1)}, bf16[256,1024]{1,0:T(8,128)(2,1)}, u32[]{:S(2)}, u32[]{:S(2)}) %collective-permute-start.5) | collective-permute-done | bytes 524320 | tf_op jit(solution)/shard_map/ppermute | solution.py:250
  168.1 5.3 %collective-permute-done.3 = bf16[256,1024]{1,0:T(8,128)(2,1)} collective-permute-done((bf16[256,1024]{1,0:T(8,128)(2,1)}, bf16[256,1024]{1,0:T(8,128)(2,1)}, u32[]{:S(2)}, u32[]{:S(2)}) %collective-permute-start.3) | collective-permute-done | bytes 524320 | tf_op jit(solution)/shard_map/ppermute | solution.py:250
  173.4 2.6 %fusion.7 = bf16[1,256,1024]{2,1,0:T(8,128)(2,1)} fusion(bf16[256,1024]{1,0:T(8,128)(2,1)} %collective-permute-done.5, bf16[256,1024]{1,0:T(8,128)(2,1)} %collective-permute-done.4, bf16[256,1024]{1,0:T(8,128)(2,1)} %collective-permute-done.3, bf16[256,256]{1,0:T(8,128)(2,1)S(1)} %shard_map.104, bf16[256,1024]{1,0:T(8,128)(2,1)S(1)} %copy-done), kind=kOutput, calls=%fused_computation.17 | convolution fusion | flops 136052736 | bytes 2752512 | tf_op jit(solution)/shard_map/dot_general | solution.py:243
  (55 shorter events, 11.9 us)
Async XLA Ops:
  6.5 110.4 %copy-start = (bf16[256,1024]{1,0:T(8,128)(2,1)S(1)}, bf16[256,1024]{1,0:T(8,128)(2,1)}, u32[]{:S(2)}) copy-start(bf16[256,1024]{1,0:T(8,128)(2,1)} %param.13) | copy-start | bytes 1572868
  6.5 15.7 %copy-start.7 = (bf16[1024,3,256]{2,0,1:T(8,128)(2,1)S(1)}, bf16[1024,3,256]{2,0,1:T(8,128)(2,1)}, u32[]{:S(2)}) copy-start(bf16[1024,3,256]{2,0,1:T(8,128)(2,1)} %param.12) | copy-start | bytes 4718596
  6.5 59.4 %all-gather.2.cloned.1.call-start = ((), (), s32[]{:S(2)}) async-start(), calls=%async_computation | async-start | bytes 8650752 | tf_op jit(solution)/shard_map/all_gather | solution.py:232
  10.5 13.5 %copy-start.9 = (s32[1,1024]{1,0:T(1,128)S(1)}, s32[1,1024]{1,0:T(1,128)}, u32[]{:S(2)}) copy-start(s32[1,1024]{1,0:T(1,128)} %param.18) | copy-start | bytes 12292
  10.5 13.6 %copy-start.6 = (bf16[1,256,1024]{2,1,0:T(8,128)(2,1)S(1)}, bf16[1,256,1024]{2,1,0:T(8,128)(2,1)}, u32[]{:S(2)}) copy-start(bf16[1,256,1024]{2,1,0:T(8,128)(2,1)} %param.10) | copy-start | bytes 1572868
  10.5 13.6 %copy-start.10 = (f32[1024]{0:T(1024)S(1)}, f32[1024]{0:T(1024)}, u32[]{:S(2)}) copy-start(f32[1024]{0:T(1024)} %param.11) | copy-start | bytes 12292
  10.5 26.6 %collective-permute-start.2 = (bf16[256,1024]{1,0:T(8,128)(2,1)}, bf16[256,1024]{1,0:T(8,128)(2,1)}, u32[]{:S(2)}, u32[]{:S(2)}) collective-permute-start(bf16[256,1024]{1,0:T(8,128)(2,1)} %fusion.4), channel_id=1, source_target_pairs={{0,96},{32,0},{64,32},{96,64},{1,97},{33,1},{65,33},{97,65},{2,98}... | collective-permute-start | bytes 1572872 | tf_op jit(solution)/shard_map/ppermute | solution.py:168
  15.1 22.0 %collective-permute-start.1 = (bf16[256,1024]{1,0:T(8,128)(2,1)}, bf16[256,1024]{1,0:T(8,128)(2,1)}, u32[]{:S(2)}, u32[]{:S(2)}) collective-permute-start(bf16[256,1024]{1,0:T(8,128)(2,1)} %fusion.4), channel_id=1, source_target_pairs={{0,64},{32,96},{64,0},{96,32},{1,65},{33,97},{65,1},{97,33},{2,66}... | collective-permute-start | bytes 1572872 | tf_op jit(solution)/shard_map/ppermute | solution.py:168
  15.1 26.3 %collective-permute-start = (bf16[256,1024]{1,0:T(8,128)(2,1)}, bf16[256,1024]{1,0:T(8,128)(2,1)}, u32[]{:S(2)}, u32[]{:S(2)}) collective-permute-start(bf16[256,1024]{1,0:T(8,128)(2,1)} %fusion.4), channel_id=1, source_target_pairs={{0,32},{32,64},{64,96},{96,0},{1,33},{33,65},{65,97},{97,1},{2,34}... | collective-permute-start | bytes 1572872 | tf_op jit(solution)/shard_map/ppermute | solution.py:168
  45.1 2.0 %copy-start.8 = (bf16[1024,3,256]{0,2,1:T(8,128)(2,1)S(1)}, bf16[1024,3,256]{0,2,1:T(8,128)(2,1)}, u32[]{:S(2)}) copy-start(bf16[1024,3,256]{0,2,1:T(8,128)(2,1)} %copy.26) | copy-start | bytes 4718596
  54.0 46.3 %copy-start.4 = (s32[64]{0:T(128)S(1)}, s32[64]{0:T(128)}, u32[]{:S(2)}) copy-start(s32[64]{0:T(128)} %pnode_ref.7) | copy-start | bytes 772
  54.0 46.3 %copy-start.5 = (s32[64]{0:T(128)S(1)}, s32[64]{0:T(128)}, u32[]{:S(2)}) copy-start(s32[64]{0:T(128)} %pfill_ref.7) | copy-start | bytes 772
  100.3 1.0 copy-start.1
  118.0 13.1 %copy-start.2 = (bf16[256,1024]{1,0:T(8,128)(2,1)S(1)}, bf16[256,1024]{1,0:T(8,128)(2,1)}, u32[]{:S(2)}) copy-start(bf16[256,1024]{1,0:T(8,128)(2,1)} %get-tuple-element.13.qt_ref) | copy-start | bytes 1572868
  141.5 26.6 %collective-permute-start.5 = (bf16[256,1024]{1,0:T(8,128)(2,1)}, bf16[256,1024]{1,0:T(8,128)(2,1)}, u32[]{:S(2)}, u32[]{:S(2)}) collective-permute-start(bf16[256,1024]{1,0:T(8,128)(2,1)} %convolution_convert_fusion.1), channel_id=1, source_target_pairs={{0,96},{32,0},{64,32},{96,64},{1,97},{33,1},{65,33},{97,65},{2,98}... | collective-permute-start | bytes 1572872 | tf_op jit(solution)/shard_map/ppermute | solution.py:250
  147.0 21.0 %collective-permute-start.4 = (bf16[256,1024]{1,0:T(8,128)(2,1)}, bf16[256,1024]{1,0:T(8,128)(2,1)}, u32[]{:S(2)}, u32[]{:S(2)}) collective-permute-start(bf16[256,1024]{1,0:T(8,128)(2,1)} %convolution_convert_fusion.2), channel_id=1, source_target_pairs={{0,64},{32,96},{64,0},{96,32},{1,65},{33,97},{65,1},{97,33},{2,66}... | collective-permute-start | bytes 1572872 | tf_op jit(solution)/shard_map/ppermute | solution.py:250
  147.0 26.3 %collective-permute-start.3 = (bf16[256,1024]{1,0:T(8,128)(2,1)}, bf16[256,1024]{1,0:T(8,128)(2,1)}, u32[]{:S(2)}, u32[]{:S(2)}) collective-permute-start(bf16[256,1024]{1,0:T(8,128)(2,1)} %convolution_convert_fusion.3), channel_id=1, source_target_pairs={{0,32},{32,64},{64,96},{96,0},{1,33},{33,65},{65,97},{97,1},{2,34}... | collective-permute-start | bytes 1572872 | tf_op jit(solution)/shard_map/ppermute | solution.py:250
  147.6 1.0 copy-start.3
Sparse Core Ops, SparseCore 0:
  9.7 56.1 all-gather.1

commit v5 on v4

--- a/solution.py
+++ b/solution.py
@@ -126,7 +126,7 @@
             pl.BlockSpec((tokens, width), lambda i, *r: (0, 1)),
             pl.BlockSpec(memory_space=pltpu.VMEM),
             pl.BlockSpec(memory_space=pltpu.VMEM),
-            pl.BlockSpec(memory_space=pltpu.VMEM),
+            pl.BlockSpec((1,) + cache.shape[1:], lambda i, *r: (0, 0, 0, 0)),
             pl.BlockSpec(memory_space=pltpu.VMEM),
         ],
         out_specs=pl.BlockSpec((width, Q_BLOCK), lambda i, *r: (0, 0)),
@@ -144,17 +144,22 @@
 
 
 def transpose_kernel(v_ref, o_ref):
-    o_ref[0] = v_ref[0, 0].astype(jnp.float32).T.astype(o_ref.dtype)
+    def page(g, carry):
+        o_ref[g] = v_ref[0, g].astype(jnp.float32).T.astype(o_ref.dtype)
+        return carry
+
+    lax.fori_loop(0, o_ref.shape[0], page, 0)
 
 
 def transpose_values(cache):
     pages, kb, width = cache.shape[1:]
     return pl.pallas_call(
         transpose_kernel,
-        grid=(pages,),
-        in_specs=[pl.BlockSpec((1, 1, kb, width), lambda g: (1, g, 0, 0))],
-        out_specs=pl.BlockSpec((1, width, kb), lambda g: (g, 0, 0)),
+        grid=(1,),
+        in_specs=[pl.BlockSpec((1, pages, kb, width), lambda g: (1, 0, 0, 0))],
+        out_specs=pl.BlockSpec((pages, width, kb), lambda g: (0, 0, 0)),
         out_shape=jax.ShapeDtypeStruct((pages, width, kb), cache.dtype),
+        compiler_params=pltpu.CompilerParams(vmem_limit_bytes=48 * 1024 * 1024),
         interpret=INTERPRET,
     )(cache)
 

time: 186 us -> 156 us (0.84); the launches traced: 183 us -> 155 us
  Pallas kernels: 83.2 us -> 53.2 us
    pallas_call x1, Pallas kernels: 34.4 us -> 8.91 us  [transpose_values(): pl.pallas_call(transpose_kernel, grid=(1,), in_specs=[pl.BlockSpec((1, pa...]
    pallas_call x4, Pallas kernels: 48.7 us -> 44.3 us  [attention(): pl.pallas_call(attn_kernel, grid_spec=grid_spec, interpret=INTERPRET, out...]
  transfers between devices with their start and end apart: 7 -> 7, of which waited for: 5 -> 5; matrix products, arithmetic and copies ran while one was open for 13% -> 16% of each run, Pallas kernels for 7% -> 7%
where the time goes in v5:
time: 156 us; the launch traced here: 155 us
  Pallas kernels  53.2 us (34%)
  waiting for transfers between devices  43.4 us (28%)
  between operations  13.6 us (9%)
  local copies, waits for them, and re-layouts  12.6 us (8%)
  other arithmetic  11.7 us (8%)
  starting transfers between devices  11.4 us (7%)
  matrix products  9.09 us (6%)
    pallas_call x4, Pallas kernels, attention(): pl.pallas_call(attn_kernel, grid_spec=grid_spec, interpret=INTERPRET, out...  44.3 us
    ppermute x3, waiting for transfers between devices, head_gather(): lax.ppermute(x, 'head', shift_perm(n, d))  17.1 us
    ppermute x3, waiting for transfers between devices, shards_body(): received.append(lax.ppermute(send, 'head', shift_perm(n_head, d)))  13.7 us
    all_gather x1, waiting for transfers between devices, shards_body(): cache = lax.all_gather(cache_kv, 'page', axis=1, tiled=True)  11.9 us
    pallas_call x1, Pallas kernels, transpose_values(): pl.pallas_call(transpose_kernel, grid=(1,), in_specs=[pl.BlockSpec((1, pa...  8.91 us
    ppermute x3, starting transfers between devices, shards_body(): received.append(lax.ppermute(send, 'head', shift_perm(n_head, d)))  6.12 us
    dot_general x4, matrix products, shards_body(): lax.dot_general(attn_t, w_out, (((0,), (0,)), ((), ())), preferred_elemen...  6.03 us
    ppermute x3, starting transfers between devices, head_gather(): lax.ppermute(x, 'head', shift_perm(n, d))  5.27 us
  transfers between devices with their start and end apart: 7, of which 5 were waited for; matrix products, arithmetic and copies ran while one was open for 16% of the time, Pallas kernels for 7%

profile of v5, /device:TPU:1, one launch (start us, length us, event | category | flops | bytes accessed | tf_op | source)
XLA Modules:
  0.0 154.9 jit_solution(8852807670369323511)
XLA Ops:
  7.3 1.2 fusion.2
  8.5 2.0 %fusion.4 = bf16[256,1024]{1,0:T(8,128)(2,1)} fusion(bf16[1,256,1024]{2,1,0:T(8,128)(2,1)} %param.10, f32[1024]{0:T(1024)} %param.11, f32[256]{0:T(256)S(1)} %add_rsqrt_fusion), kind=kLoop, calls=%fused_computation.13 | loop fusion | flops 1048576 | bytes 1053696 | tf_op jit(solution)/shard_map/convert_element_type | solution.py:197
  10.5 4.6 %collective-permute-start.2 = (bf16[256,1024]{1,0:T(8,128)(2,1)}, bf16[256,1024]{1,0:T(8,128)(2,1)}, u32[]{:S(2)}, u32[]{:S(2)}) collective-permute-start(bf16[256,1024]{1,0:T(8,128)(2,1)} %fusion.4), channel_id=1, source_target_pairs={{0,96},{32,0},{64,32},{96,64},{1,97},{33,1},{65,33},{97,65},{2,98}... | collective-permute-start | bytes 1572872 | tf_op jit(solution)/shard_map/ppermute | solution.py:173
  22.3 1.7 %copy.26 = bf16[1024,3,256]{0,2,1:T(8,128)(2,1)} copy(bf16[1024,3,256]{2,0,1:T(8,128)(2,1)S(1)} %copy-done.7) | data formatting | bytes 3145728 | tf_op args[2]
  24.3 12.8 %collective-permute-done.2 = bf16[256,1024]{1,0:T(8,128)(2,1)} collective-permute-done((bf16[256,1024]{1,0:T(8,128)(2,1)}, bf16[256,1024]{1,0:T(8,128)(2,1)}, u32[]{:S(2)}, u32[]{:S(2)}) %collective-permute-start.2) | collective-permute-done | bytes 524320 | tf_op jit(solution)/shard_map/ppermute | solution.py:173
  37.1 4.3 %collective-permute-done = bf16[256,1024]{1,0:T(8,128)(2,1)} collective-permute-done((bf16[256,1024]{1,0:T(8,128)(2,1)}, bf16[256,1024]{1,0:T(8,128)(2,1)}, u32[]{:S(2)}, u32[]{:S(2)}) %collective-permute-start) | collective-permute-done | bytes 524320 | tf_op jit(solution)/shard_map/ppermute | solution.py:173
  41.4 1.6 %pad_maximum_fusion = bf16[4,256,1024]{2,1,0:T(8,128)(2,1)S(1)} fusion(bf16[1,256,1024]{2,1,0:T(8,128)(2,1)} %bitcast.9, bf16[1,256,1024]{2,1,0:T(8,128)(2,1)} %bitcast.8, bf16[1,256,1024]{2,1,0:T(8,128)(2,1)} %bitcast.7, bf16[1,256,1024]{2,1,0:T(8,128)(2,1)S(1)} %fusion.6), kind=kLoop, calls=%fused_computation.1 | loop fusion | flops 3145728 | bytes 4194304 | tf_op jit(solution)/shard_map/stack | solution.py:174
  43.1 2.1 %gather_fusion = bf16[4,256,1024]{2,1,0:T(8,128)(2,1)} fusion(bf16[4,256,1024]{2,1,0:T(8,128)(2,1)S(1)} %pad_maximum_fusion, s32[1024]{0:T(1024)S(1)} %pad_clamp_fusion), kind=kCustom, calls=%fused_computation | custom fusion | bytes 4194320 | tf_op jit(solution)/shard_map/jit(_take)/gather | solution.py:176
  45.1 2.0 %broadcast_select_fusion = bf16[4,256,1024]{2,1,0:T(8,128)(2,1)S(1)} fusion(bf16[4,256,1024]{2,1,0:T(8,128)(2,1)} %gather_fusion, pred[4]{0:T(512)(128)(4,1)S(1)} %compare_and_fusion), kind=kLoop, calls=%fused_computation.2 | loop fusion | flops 1048576 | bytes 4194308 | tf_op jit(solution)/shard_map/jit(_take)/select_n | solution.py:176
  47.2 3.1 %convolution_convert_fusion = bf16[1024,768]{0,1:T(8,128)(2,1)} fusion(bf16[1024,1024]{1,0:T(8,128)(2,1)S(1)} %bitcast.45, bf16[1024,768]{0,1:T(8,128)(2,1)S(1)} %bitcast.46), kind=kOutput, calls=%fused_computation.3 | convolution fusion | flops 1611399168 | bytes 5242880 | tf_op jit(solution)/shard_map/dot_general | solution.py:202
  50.2 1.7 %copy.28.kn_ref = bf16[1024,768]{1,0:T(8,128)(2,1)S(1)} copy(bf16[1024,768]{0,1:T(8,128)(2,1)} %convolution_convert_fusion) | data formatting | bytes 3145728 | tf_op jit(solution)/shard_map/convert_element_type | solution.py:206
  52.0 2.1 %slice_bitcast_fusion = (bf16[256,1024]{1,0:T(8,128)(2,1)S(1)}, bf16[256,1024]{1,0:T(8,128)(2,1)}) fusion(bf16[1024,768]{0,1:T(8,128)(2,1)} %convolution_convert_fusion), kind=kLoop, calls=%fused_computation.18 | loop fusion | bytes 2097152 | tf_op jit(solution)/shard_map/transpose | solution.py:236
  54.0 11.9 %all-gather.2.cloned.1.call-done.v_ref.cache_ref = bf16[2,64,128,256]{3,2,1,0:T(8,128)(2,1)} async-done(((bf16[2,2,128,256]{3,2,1,0:T(8,128)(2,1)}), bf16[2,64,128,256]{3,2,1,0:T(8,128)(2,1)}) %all-gather.2.cloned.1.call-update) | async-done | bytes 8388624 | tf_op jit(solution)/shard_map/all_gather | solution.py:237
  65.9 8.9 %shard_map.100.cvt_ref = bf16[64,256,128]{2,1,0:T(8,128)(2,1)S(1)} custom-call(bf16[2,64,128,256]{3,2,1,0:T(8,128)(2,1)} %all-gather.2.cloned.1.call-done.v_ref.cache_ref), custom_call_target="tpu_custom_call" | custom-call | tf_op jit(solution)/shard_map/pallas_call | solution.py:156
  74.8 2.0 %copy-done.1 = bf16[64,256,128]{2,1,0:T(8,128)(2,1)} copy-done((bf16[64,256,128]{2,1,0:T(8,128)(2,1)}, bf16[64,256,128]{2,1,0:T(8,128)(2,1)S(1)}, u32[]{:S(2)}) %copy-start.1) | copy-done | bytes 4194328
  76.8 14.4 %shard_map.101 = bf16[256,256]{1,0:T(8,128)(2,1)S(1)} custom-call(s32[256]{0:T(256)S(1)} %reshape.167.plist_ref, s32[4]{0:T(128)S(1)} %convert_reduce_fusion.1.pcount_ref, s32[64]{0:T(128)S(1)} %copy-done.4, s32[64]{0:T(128)S(1)} %copy-done.5, s32[4]{0:T(128)S(1)} %and_select_fusion.2.kfirst_ref, s32[1]{0:T(128)} %bitcast.5.qsel_ref, ...), custom_call_target="tpu_custom_call" | custom-call | tf_op jit(solution)/shard_map/pallas_call | solution.py:135
  92.4 10.8 %shard_map.102 = bf16[256,256]{1,0:T(8,128)(2,1)S(1)} custom-call(s32[256]{0:T(256)S(1)} %reshape.167.plist_ref, s32[4]{0:T(128)S(1)} %convert_reduce_fusion.1.pcount_ref, s32[64]{0:T(128)S(1)} %copy-done.4, s32[64]{0:T(128)S(1)} %copy-done.5, s32[4]{0:T(128)S(1)} %and_select_fusion.2.kfirst_ref, s32[1]{0:T(128)} %bitcast.4.qsel_ref, ...), custom_call_target="tpu_custom_call" | custom-call | tf_op jit(solution)/shard_map/pallas_call | solution.py:135
  103.2 1.2 convolution_convert_fusion.2
  104.3 8.1 %shard_map.103 = bf16[256,256]{1,0:T(8,128)(2,1)S(1)} custom-call(s32[256]{0:T(256)S(1)} %reshape.167.plist_ref, s32[4]{0:T(128)S(1)} %convert_reduce_fusion.1.pcount_ref, s32[64]{0:T(128)S(1)} %copy-done.4, s32[64]{0:T(128)S(1)} %copy-done.5, s32[4]{0:T(128)S(1)} %and_select_fusion.2.kfirst_ref, s32[1]{0:T(128)} %bitcast.3.qsel_ref, ...), custom_call_target="tpu_custom_call" | custom-call | tf_op jit(solution)/shard_map/pallas_call | solution.py:135
  113.6 5.5 %collective-permute-start.5 = (bf16[256,1024]{1,0:T(8,128)(2,1)}, bf16[256,1024]{1,0:T(8,128)(2,1)}, u32[]{:S(2)}, u32[]{:S(2)}) collective-permute-start(bf16[256,1024]{1,0:T(8,128)(2,1)} %convolution_convert_fusion.1), channel_id=1, source_target_pairs={{0,96},{32,0},{64,32},{96,64},{1,97},{33,1},{65,33},{97,65},{2,98}... | collective-permute-start | bytes 1572872 | tf_op jit(solution)/shard_map/ppermute | solution.py:255
  120.8 11.0 %shard_map.104 = bf16[256,256]{1,0:T(8,128)(2,1)S(1)} custom-call(s32[256]{0:T(256)S(1)} %reshape.167.plist_ref, s32[4]{0:T(128)S(1)} %convert_reduce_fusion.1.pcount_ref, s32[64]{0:T(128)S(1)} %copy-done.4, s32[64]{0:T(128)S(1)} %copy-done.5, s32[4]{0:T(128)S(1)} %and_select_fusion.2.kfirst_ref, s32[1]{0:T(128)} %bitcast.2.qsel_ref, ...), custom_call_target="tpu_custom_call" | custom-call | tf_op jit(solution)/shard_map/pallas_call | solution.py:135
  131.8 8.4 %collective-permute-done.5 = bf16[256,1024]{1,0:T(8,128)(2,1)} collective-permute-done((bf16[256,1024]{1,0:T(8,128)(2,1)}, bf16[256,1024]{1,0:T(8,128)(2,1)}, u32[]{:S(2)}, u32[]{:S(2)}) %collective-permute-start.5) | collective-permute-done | bytes 524320 | tf_op jit(solution)/shard_map/ppermute | solution.py:255
  140.2 5.3 %collective-permute-done.3 = bf16[256,1024]{1,0:T(8,128)(2,1)} collective-permute-done((bf16[256,1024]{1,0:T(8,128)(2,1)}, bf16[256,1024]{1,0:T(8,128)(2,1)}, u32[]{:S(2)}, u32[]{:S(2)}) %collective-permute-start.3) | collective-permute-done | bytes 524320 | tf_op jit(solution)/shard_map/ppermute | solution.py:255
  145.5 2.6 %fusion.7 = bf16[1,256,1024]{2,1,0:T(8,128)(2,1)} fusion(bf16[256,1024]{1,0:T(8,128)(2,1)} %collective-permute-done.5, bf16[256,1024]{1,0:T(8,128)(2,1)} %collective-permute-done.4, bf16[256,1024]{1,0:T(8,128)(2,1)} %collective-permute-done.3, bf16[256,256]{1,0:T(8,128)(2,1)S(1)} %shard_map.104, bf16[256,1024]{1,0:T(8,128)(2,1)S(1)} %copy-done), kind=kOutput, calls=%fused_computation.17 | convolution fusion | flops 136052736 | bytes 2752512 | tf_op jit(solution)/shard_map/dot_general | solution.py:248
  (55 shorter events, 12.1 us)
Async XLA Ops:
  6.5 84.7 %copy-start = (bf16[256,1024]{1,0:T(8,128)(2,1)S(1)}, bf16[256,1024]{1,0:T(8,128)(2,1)}, u32[]{:S(2)}) copy-start(bf16[256,1024]{1,0:T(8,128)(2,1)} %param.13) | copy-start | bytes 1572868
  6.5 15.7 %copy-start.7 = (bf16[1024,3,256]{2,0,1:T(8,128)(2,1)S(1)}, bf16[1024,3,256]{2,0,1:T(8,128)(2,1)}, u32[]{:S(2)}) copy-start(bf16[1024,3,256]{2,0,1:T(8,128)(2,1)} %param.12) | copy-start | bytes 4718596
  6.5 59.4 %all-gather.2.cloned.1.call-start = ((), (), s32[]{:S(2)}) async-start(), calls=%async_computation | async-start | bytes 8650752 | tf_op jit(solution)/shard_map/all_gather | solution.py:237
  10.5 13.5 %copy-start.9 = (s32[1,1024]{1,0:T(1,128)S(1)}, s32[1,1024]{1,0:T(1,128)}, u32[]{:S(2)}) copy-start(s32[1,1024]{1,0:T(1,128)} %param.18) | copy-start | bytes 12292
  10.5 13.6 %copy-start.6 = (bf16[1,256,1024]{2,1,0:T(8,128)(2,1)S(1)}, bf16[1,256,1024]{2,1,0:T(8,128)(2,1)}, u32[]{:S(2)}) copy-start(bf16[1,256,1024]{2,1,0:T(8,128)(2,1)} %param.10) | copy-start | bytes 1572868
  10.5 13.6 %copy-start.10 = (f32[1024]{0:T(1024)S(1)}, f32[1024]{0:T(1024)}, u32[]{:S(2)}) copy-start(f32[1024]{0:T(1024)} %param.11) | copy-start | bytes 12292
  10.5 26.6 %collective-permute-start.2 = (bf16[256,1024]{1,0:T(8,128)(2,1)}, bf16[256,1024]{1,0:T(8,128)(2,1)}, u32[]{:S(2)}, u32[]{:S(2)}) collective-permute-start(bf16[256,1024]{1,0:T(8,128)(2,1)} %fusion.4), channel_id=1, source_target_pairs={{0,96},{32,0},{64,32},{96,64},{1,97},{33,1},{65,33},{97,65},{2,98}... | collective-permute-start | bytes 1572872 | tf_op jit(solution)/shard_map/ppermute | solution.py:173
  15.1 22.0 %collective-permute-start.1 = (bf16[256,1024]{1,0:T(8,128)(2,1)}, bf16[256,1024]{1,0:T(8,128)(2,1)}, u32[]{:S(2)}, u32[]{:S(2)}) collective-permute-start(bf16[256,1024]{1,0:T(8,128)(2,1)} %fusion.4), channel_id=1, source_target_pairs={{0,64},{32,96},{64,0},{96,32},{1,65},{33,97},{65,1},{97,33},{2,66}... | collective-permute-start | bytes 1572872 | tf_op jit(solution)/shard_map/ppermute | solution.py:173
  15.1 26.3 %collective-permute-start = (bf16[256,1024]{1,0:T(8,128)(2,1)}, bf16[256,1024]{1,0:T(8,128)(2,1)}, u32[]{:S(2)}, u32[]{:S(2)}) collective-permute-start(bf16[256,1024]{1,0:T(8,128)(2,1)} %fusion.4), channel_id=1, source_target_pairs={{0,32},{32,64},{64,96},{96,0},{1,33},{33,65},{65,97},{97,1},{2,34}... | collective-permute-start | bytes 1572872 | tf_op jit(solution)/shard_map/ppermute | solution.py:173
  45.1 2.0 %copy-start.8 = (bf16[1024,3,256]{0,2,1:T(8,128)(2,1)S(1)}, bf16[1024,3,256]{0,2,1:T(8,128)(2,1)}, u32[]{:S(2)}) copy-start(bf16[1024,3,256]{0,2,1:T(8,128)(2,1)} %copy.26) | copy-start | bytes 4718596
  54.0 22.8 %copy-start.4 = (s32[64]{0:T(128)S(1)}, s32[64]{0:T(128)}, u32[]{:S(2)}) copy-start(s32[64]{0:T(128)} %pnode_ref.7) | copy-start | bytes 772
  54.0 22.8 %copy-start.5 = (s32[64]{0:T(128)S(1)}, s32[64]{0:T(128)}, u32[]{:S(2)}) copy-start(s32[64]{0:T(128)} %pfill_ref.7) | copy-start | bytes 772
  65.9 10.9 %copy-start.2 = (bf16[256,1024]{1,0:T(8,128)(2,1)S(1)}, bf16[256,1024]{1,0:T(8,128)(2,1)}, u32[]{:S(2)}) copy-start(bf16[256,1024]{1,0:T(8,128)(2,1)} %get-tuple-element.13.qt_ref) | copy-start | bytes 1572868
  74.8 2.0 %copy-start.1 = (bf16[64,256,128]{2,1,0:T(8,128)(2,1)}, bf16[64,256,128]{2,1,0:T(8,128)(2,1)S(1)}, u32[]{:S(2)}) copy-start(bf16[64,256,128]{2,1,0:T(8,128)(2,1)S(1)} %shard_map.100.cvt_ref) | copy-start | bytes 12582916
  113.6 26.6 %collective-permute-start.5 = (bf16[256,1024]{1,0:T(8,128)(2,1)}, bf16[256,1024]{1,0:T(8,128)(2,1)}, u32[]{:S(2)}, u32[]{:S(2)}) collective-permute-start(bf16[256,1024]{1,0:T(8,128)(2,1)} %convolution_convert_fusion.1), channel_id=1, source_target_pairs={{0,96},{32,0},{64,32},{96,64},{1,97},{33,1},{65,33},{97,65},{2,98}... | collective-permute-start | bytes 1572872 | tf_op jit(solution)/shard_map/ppermute | solution.py:255
  119.1 21.1 %collective-permute-start.4 = (bf16[256,1024]{1,0:T(8,128)(2,1)}, bf16[256,1024]{1,0:T(8,128)(2,1)}, u32[]{:S(2)}, u32[]{:S(2)}) collective-permute-start(bf16[256,1024]{1,0:T(8,128)(2,1)} %convolution_convert_fusion.2), channel_id=1, source_target_pairs={{0,64},{32,96},{64,0},{96,32},{1,65},{33,97},{65,1},{97,33},{2,66}... | collective-permute-start | bytes 1572872 | tf_op jit(solution)/shard_map/ppermute | solution.py:255
  119.1 26.3 %collective-permute-start.3 = (bf16[256,1024]{1,0:T(8,128)(2,1)}, bf16[256,1024]{1,0:T(8,128)(2,1)}, u32[]{:S(2)}, u32[]{:S(2)}) collective-permute-start(bf16[256,1024]{1,0:T(8,128)(2,1)} %convolution_convert_fusion.3), channel_id=1, source_target_pairs={{0,32},{32,64},{64,96},{96,0},{1,33},{33,65},{65,97},{97,1},{2,34}... | collective-permute-start | bytes 1572872 | tf_op jit(solution)/shard_map/ppermute | solution.py:255
  119.7 1.0 copy-start.3
Sparse Core Ops, SparseCore 0:
  9.7 56.1 all-gather.1

commit v6 on v0

--- a/solution.py
+++ b/solution.py
@@ -199,6 +199,7 @@
     group_width = w_qkv.shape[2]
     weight_flat = w_qkv.reshape(model_width, 3 * group_width)
     n_head = tok_seg.shape[1] // hidden_in.shape[1]
+    w_full = head_gather(w_out, n_head)
     projected = jnp.dot(
         head_gather(normed, n_head),
         weight_flat,
@@ -238,12 +239,18 @@
     attn_t = attention(
         plist, pcount, page_node, page_fill, kfirst, qt, tok, projected, vnt, segk, cache
     )
-    result = head_reduce_scatter(
-        lax.dot_general(
-            attn_t, w_out, (((0,), (0,)), ((), ())), preferred_element_type=jnp.float32
-        ),
-        n_head,
-    )
+    me = lax.axis_index("head")
+    rows = tokens // n_head
+    parts = [lax.dynamic_slice_in_dim(attn_t, me * rows, rows, axis=1)]
+    for d in range(1, n_head):
+        send = lax.dynamic_slice_in_dim(attn_t, ((me + d) % n_head) * rows, rows, axis=1)
+        parts.append(lax.ppermute(send, "head", shift_perm(n_head, d)))
+    order = (me - jnp.arange(n_head, dtype=jnp.int32)) % n_head
+    mine = jnp.take(jnp.stack(parts), order, axis=0)
+    mine = mine.reshape(n_head * mine.shape[1], rows)
+    result = lax.dot_general(
+        mine, w_full, (((0,), (0,)), ((), ())), preferred_element_type=jnp.float32
+    ).astype(jnp.bfloat16)
     return result[None]
 
 

time: 153 us -> 132 us (0.86); the launches traced: 156 us -> 131 us
  waiting for transfers between devices: 50.5 us -> 28.8 us
  Pallas kernels: 50 us -> 46.6 us
  starting transfers between devices: 11.5 us -> 14 us
  other arithmetic: 14.7 us -> 12.6 us
    ppermute x3, waiting for transfers between devices: 22.1 us -> 0.7 us  [shards(): parts.append(lax.ppermute(send, 'head', shift_perm(n_head, d)))]
    pallas_call x1, Pallas kernels: 50 us -> 46.6 us  [attention(): pl.pallas_call(attn_kernel, grid_spec=grid_spec, interpret=INTERPRET, out...]
    unnamed x21 -> x19, local copies, waits for them, and re-layouts: 5.01 us -> 2.05 us
    ppermute x3 -> x6, waiting for transfers between devices: 14.3 us -> 11.7 us  [head_gather(): lax.ppermute(x, 'head', shift_perm(n, d))]
    broadcast_in_dim x1 -> x0, other arithmetic: 2.52 us -> none  [shards(): return result[None]]
    ppermute x3 -> x6, starting transfers between devices: 6.49 us -> 8.99 us  [head_gather(): lax.ppermute(x, 'head', shift_perm(n, d))]
    all_gather x1, waiting for transfers between devices: 13.3 us -> 15.7 us  [shards(): cache = lax.all_gather(cache_kv, 'page', axis=1, tiled=True)]
    gather x1 -> x2, local copies, waits for them, and re-layouts: 2.07 us -> 4.11 us  [head_gather(): gathered = jnp.take(stacked, order, axis=0)]
  transfers between devices with their start and end apart: 7 -> 10, of which waited for: 5 -> 4; matrix products, arithmetic and copies ran while one was open for 15% -> 20% of each run, Pallas kernels for 0% -> 35%
where the time goes in v6:
time: 132 us; the launch traced here: 131 us
  Pallas kernels  46.6 us (35%)
  waiting for transfers between devices  28.8 us (22%)
  starting transfers between devices  14 us (11%)
  between operations  13.6 us (10%)
  other arithmetic  12.6 us (10%)
  local copies, waits for them, and re-layouts  11 us (8%)
  matrix products  4.68 us (4%)
    pallas_call x1, Pallas kernels, attention(): pl.pallas_call(attn_kernel, grid_spec=grid_spec, interpret=INTERPRET, out...  46.6 us
    all_gather x1, waiting for transfers between devices, shards(): cache = lax.all_gather(cache_kv, 'page', axis=1, tiled=True)  15.7 us
    ppermute x6, waiting for transfers between devices, head_gather(): lax.ppermute(x, 'head', shift_perm(n, d))  11.7 us
    ppermute x6, starting transfers between devices, head_gather(): lax.ppermute(x, 'head', shift_perm(n, d))  8.99 us
    ppermute x3, starting transfers between devices, shards(): parts.append(lax.ppermute(send, 'head', shift_perm(n_head, d)))  5.01 us
    gather x2, local copies, waits for them, and re-layouts, head_gather(): gathered = jnp.take(stacked, order, axis=0)  4.11 us
    another operation x2, other arithmetic, head_gather(): stacked = jnp.stack(parts)  3.24 us
    dot_general x1, matrix products, shards(): jnp.dot(head_gather(normed, n_head), weight_flat, preferred_element_type=...  3.06 us
  transfers between devices with their start and end apart: 10, of which 4 were waited for; matrix products, arithmetic and copies ran while one was open for 20% of the time, Pallas kernels for 35%

profile of v6, /device:TPU:1, one launch (start us, length us, event | category | flops | bytes accessed | tf_op | source)
XLA Modules:
  0.0 131.3 jit_solution(15771854726094804756)
XLA Ops:
  7.3 1.2 fusion.14
  8.5 1.2 fusion.16
  9.8 2.5 %collective-permute-start = (bf16[256,1024]{1,0:T(8,128)(2,1)S(1)}, bf16[256,1024]{1,0:T(8,128)(2,1)}, u32[]{:S(2)}, u32[]{:S(2)}) collective-permute-start(bf16[256,1024]{1,0:T(8,128)(2,1)S(1)} %fusion.16), channel_id=1, source_target_pairs={{0,32},{32,64},{64,96},{96,0},{1,33},{33,65},{65,97},{97,1},{2,34}... | collective-permute-start | bytes 1572872 | tf_op jit(solution)/shard_map/ppermute | solution.py:161
  12.3 3.3 %collective-permute-start.1 = (bf16[256,1024]{1,0:T(8,128)(2,1)S(1)}, bf16[256,1024]{1,0:T(8,128)(2,1)}, u32[]{:S(2)}, u32[]{:S(2)}) collective-permute-start(bf16[256,1024]{1,0:T(8,128)(2,1)S(1)} %fusion.16), channel_id=1, source_target_pairs={{0,64},{32,96},{64,0},{96,32},{1,65},{33,97},{65,1},{97,33},{2,66}... | collective-permute-start | bytes 1572872 | tf_op jit(solution)/shard_map/ppermute | solution.py:161
  18.3 0.8 select_reduce_fusion.3
  20.6 0.9 or_reduce_fusion
  21.9 0.9 convert_reduce_fusion
  23.1 1.7 %copy.19 = bf16[1024,3,256]{0,2,1:T(8,128)(2,1)} copy(bf16[1024,3,256]{2,0,1:T(8,128)(2,1)S(1)} %copy-done.4) | data formatting | bytes 3145728 | tf_op args[2]
  26.2 1.2 collective-permute-start.8
  27.4 10.9 %collective-permute-done.1 = bf16[256,1024]{1,0:T(8,128)(2,1)} collective-permute-done((bf16[256,1024]{1,0:T(8,128)(2,1)S(1)}, bf16[256,1024]{1,0:T(8,128)(2,1)}, u32[]{:S(2)}, u32[]{:S(2)}) %collective-permute-start.1) | collective-permute-done | bytes 524320 | tf_op jit(solution)/shard_map/ppermute | solution.py:161
  38.3 1.6 %pad_maximum_fusion = bf16[4,256,1024]{2,1,0:T(8,128)(2,1)S(1)} fusion(bf16[1,256,1024]{2,1,0:T(8,128)(2,1)} %bitcast.5, bf16[1,256,1024]{2,1,0:T(8,128)(2,1)} %bitcast.4, bf16[1,256,1024]{2,1,0:T(8,128)(2,1)} %bitcast.3, bf16[1,256,1024]{2,1,0:T(8,128)(2,1)S(1)} %fusion.18), kind=kLoop, calls=%fused_computation.3 | loop fusion | flops 3145728 | bytes 4194304 | tf_op jit(solution)/shard_map/stack | solution.py:162
  40.0 2.1 %gather_fusion.1 = bf16[4,256,1024]{2,1,0:T(8,128)(2,1)} fusion(bf16[4,256,1024]{2,1,0:T(8,128)(2,1)S(1)} %pad_maximum_fusion, s32[1024]{0:T(1024)S(1)} %pad_clamp_fusion.1), kind=kCustom, calls=%fused_computation.clone | custom fusion | bytes 4194320 | tf_op jit(solution)/shard_map/jit(_take)/gather | solution.py:164
  42.0 2.0 %broadcast_select_fusion = bf16[4,256,1024]{2,1,0:T(8,128)(2,1)S(1)} fusion(bf16[4,256,1024]{2,1,0:T(8,128)(2,1)} %gather_fusion.1, pred[4]{0:T(512)(128)(4,1)S(1)} %compare_and_fusion), kind=kLoop, calls=%fused_computation.8 | loop fusion | flops 1048576 | bytes 4194308 | tf_op jit(solution)/shard_map/jit(_take)/select_n | solution.py:164
  44.1 3.1 %convolution_convert_fusion = bf16[1024,768]{0,1:T(8,128)(2,1)} fusion(bf16[1024,1024]{1,0:T(8,128)(2,1)S(1)} %bitcast.48, bf16[1024,768]{0,1:T(8,128)(2,1)S(1)} %bitcast.49), kind=kOutput, calls=%fused_computation.9 | convolution fusion | flops 1611399168 | bytes 5242880 | tf_op jit(solution)/shard_map/dot_general | solution.py:203
  47.1 1.7 %copy.21.kn_ref = bf16[1024,768]{1,0:T(8,128)(2,1)S(1)} copy(bf16[1024,768]{0,1:T(8,128)(2,1)} %convolution_convert_fusion) | data formatting | bytes 3145728 | tf_op jit(solution)/shard_map/convert_element_type | solution.py:207
  48.9 1.3 slice_bitcast_fusion
  50.2 15.7 %all-gather.2.cloned.1.call-done.cache_ref = bf16[2,64,128,256]{3,2,1,0:T(8,128)(2,1)} async-done(((bf16[2,2,128,256]{3,2,1,0:T(8,128)(2,1)}), bf16[2,64,128,256]{3,2,1,0:T(8,128)(2,1)}) %all-gather.2.cloned.1.call-update) | async-done | bytes 8388624 | tf_op jit(solution)/shard_map/all_gather | solution.py:238
  65.9 46.6 %shard_map.100 = bf16[256,1024]{1,0:T(8,128)(2,1)S(1)} custom-call(s32[256]{0:T(256)S(1)} %reshape.144.plist_ref, s32[4]{0:T(128)S(1)} %convert_reduce_fusion.1.pcount_ref, s32[64]{0:T(128)S(1)} %copy-done, s32[64]{0:T(128)S(1)} %copy-done.1, s32[4]{0:T(128)S(1)} %and_select_fusion.1.kfirst_ref, bf16[256,1024]{1,0:T(8,128)(2,1)S(1)} %get-tuple-element.7.qt_ref, ...), custom_call_target="tpu_custom_call" | custom-call | tf_op jit(solution)/shard_map/pallas_call | solution.py:144
  112.6 1.3 %collective-permute-start.3 = (bf16[256,256]{1,0:T(8,128)(2,1)S(1)}, bf16[256,256]{1,0:T(8,128)(2,1)S(1)}, u32[]{:S(2)}, u32[]{:S(2)}) collective-permute-start(bf16[256,256]{1,0:T(8,128)(2,1)S(1)} %get-tuple-element.11), channel_id=1, source_target_pairs={{0,32},{32,64},{64,96},{96,0},{1,33},{33,65},{65,97},{97,1},{2,34}... | collective-permute-start | bytes 393224 | tf_op jit(solution)/shard_map/ppermute | solution.py:247
  113.9 2.6 %collective-permute-start.4 = (bf16[256,256]{1,0:T(8,128)(2,1)S(1)}, bf16[256,256]{1,0:T(8,128)(2,1)S(1)}, u32[]{:S(2)}, u32[]{:S(2)}) collective-permute-start(bf16[256,256]{1,0:T(8,128)(2,1)S(1)} %get-tuple-element.10), channel_id=1, source_target_pairs={{0,64},{32,96},{64,0},{96,32},{1,65},{33,97},{65,1},{97,33},{2,66}... | collective-permute-start | bytes 393224 | tf_op jit(solution)/shard_map/ppermute | solution.py:247
  116.5 1.1 collective-permute-start.5
  117.6 1.6 %pad_maximum_fusion.1 = bf16[4,256,1024]{2,1,0:T(8,128)(2,1)S(1)} fusion(bf16[1,256,1024]{2,1,0:T(8,128)(2,1)} %bitcast.22, bf16[1,256,1024]{2,1,0:T(8,128)(2,1)} %bitcast.21, bf16[1,256,1024]{2,1,0:T(8,128)(2,1)} %bitcast.20, bf16[1,256,1024]{2,1,0:T(8,128)(2,1)S(1)} %bitcast.50), kind=kLoop, calls=%fused_computation.4 | loop fusion | flops 3145728 | bytes 4194304 | tf_op jit(solution)/shard_map/stack | solution.py:162
  119.2 2.0 %gather_fusion.2 = bf16[4,256,1024]{2,1,0:T(8,128)(2,1)} fusion(bf16[4,256,1024]{2,1,0:T(8,128)(2,1)S(1)} %pad_maximum_fusion.1, s32[1024]{0:T(1024)S(1)} %pad_clamp_fusion.1), kind=kCustom, calls=%fused_computation.1.clone | custom fusion | bytes 4194320 | tf_op jit(solution)/shard_map/jit(_take)/gather | solution.py:164
  122.9 1.6 %fusion.11 = bf16[1,256,1024]{2,1,0:T(8,128)(2,1)} fusion(bf16[4,256,1024]{2,1,0:T(8,128)(2,1)S(1)} %copy-done.3, pred[4]{0:T(512)(128)(4,1)S(1)} %compare_and_fusion, bf16[4,256,256]{2,1,0:T(8,128)(2,1)S(1)} %gather_fusion), kind=kOutput, calls=%fused_computation.16 | convolution fusion | flops 538443776 | bytes 3145732 | tf_op jit(solution)/shard_map/dot_general | solution.py:251
  (57 shorter events, 8.6 us)
Async XLA Ops:
  6.5 16.6 %copy-start.4 = (bf16[1024,3,256]{2,0,1:T(8,128)(2,1)S(1)}, bf16[1024,3,256]{2,0,1:T(8,128)(2,1)}, u32[]{:S(2)}) copy-start(bf16[1024,3,256]{2,0,1:T(8,128)(2,1)} %param.14) | copy-start | bytes 4718596
  6.5 59.4 %all-gather.2.cloned.1.call-start = ((), (), s32[]{:S(2)}) async-start(), calls=%async_computation | async-start | bytes 8650752 | tf_op jit(solution)/shard_map/all_gather | solution.py:238
  8.5 16.4 %copy-start.7 = (s32[1,1024]{1,0:T(1,128)S(1)}, s32[1,1024]{1,0:T(1,128)}, u32[]{:S(2)}) copy-start(s32[1,1024]{1,0:T(1,128)} %param.20) | copy-start | bytes 12292
  9.8 15.4 %copy-start.2 = (bf16[1,256,1024]{2,1,0:T(8,128)(2,1)S(1)}, bf16[1,256,1024]{2,1,0:T(8,128)(2,1)}, u32[]{:S(2)}) copy-start(bf16[1,256,1024]{2,1,0:T(8,128)(2,1)} %param.12) | copy-start | bytes 1572868
  9.8 15.4 %copy-start.8 = (f32[1024]{0:T(1024)S(1)}, f32[1024]{0:T(1024)}, u32[]{:S(2)}) copy-start(f32[1024]{0:T(1024)} %param.13) | copy-start | bytes 12292
  9.8 16.4 %collective-permute-start = (bf16[256,1024]{1,0:T(8,128)(2,1)S(1)}, bf16[256,1024]{1,0:T(8,128)(2,1)}, u32[]{:S(2)}, u32[]{:S(2)}) collective-permute-start(bf16[256,1024]{1,0:T(8,128)(2,1)S(1)} %fusion.16), channel_id=1, source_target_pairs={{0,32},{32,64},{64,96},{96,0},{1,33},{33,65},{65,97},{97,1},{2,34}... | collective-permute-start | bytes 1572872 | tf_op jit(solution)/shard_map/ppermute | solution.py:161
  12.3 26.0 %collective-permute-start.1 = (bf16[256,1024]{1,0:T(8,128)(2,1)S(1)}, bf16[256,1024]{1,0:T(8,128)(2,1)}, u32[]{:S(2)}, u32[]{:S(2)}) collective-permute-start(bf16[256,1024]{1,0:T(8,128)(2,1)S(1)} %fusion.16), channel_id=1, source_target_pairs={{0,64},{32,96},{64,0},{96,32},{1,65},{33,97},{65,1},{97,33},{2,66}... | collective-permute-start | bytes 1572872 | tf_op jit(solution)/shard_map/ppermute | solution.py:161
  15.6 22.7 %collective-permute-start.2 = (bf16[256,1024]{1,0:T(8,128)(2,1)S(1)}, bf16[256,1024]{1,0:T(8,128)(2,1)}, u32[]{:S(2)}, u32[]{:S(2)}) collective-permute-start(bf16[256,1024]{1,0:T(8,128)(2,1)S(1)} %fusion.16), channel_id=1, source_target_pairs={{0,96},{32,0},{64,32},{96,64},{1,97},{33,1},{65,33},{97,65},{2,98}... | collective-permute-start | bytes 1572872 | tf_op jit(solution)/shard_map/ppermute | solution.py:161
  16.3 100.2 %collective-permute-start.6 = (bf16[256,1024]{1,0:T(8,128)(2,1)}, bf16[256,1024]{1,0:T(8,128)(2,1)}, u32[]{:S(2)}, u32[]{:S(2)}) collective-permute-start(bf16[256,1024]{1,0:T(8,128)(2,1)} %param.15), channel_id=1, source_target_pairs={{0,32},{32,64},{64,96},{96,0},{1,33},{33,65},{65,97},{97,1},{2,34}... | collective-permute-start | bytes 1572872 | tf_op jit(solution)/shard_map/ppermute | solution.py:161
  17.1 100.5 %collective-permute-start.7 = (bf16[256,1024]{1,0:T(8,128)(2,1)}, bf16[256,1024]{1,0:T(8,128)(2,1)}, u32[]{:S(2)}, u32[]{:S(2)}) collective-permute-start(bf16[256,1024]{1,0:T(8,128)(2,1)} %param.15), channel_id=1, source_target_pairs={{0,64},{32,96},{64,0},{96,32},{1,65},{33,97},{65,1},{97,33},{2,66}... | collective-permute-start | bytes 1572872 | tf_op jit(solution)/shard_map/ppermute | solution.py:161
  26.2 91.5 %collective-permute-start.8 = (bf16[256,1024]{1,0:T(8,128)(2,1)}, bf16[256,1024]{1,0:T(8,128)(2,1)}, u32[]{:S(2)}, u32[]{:S(2)}) collective-permute-start(bf16[256,1024]{1,0:T(8,128)(2,1)} %param.15), channel_id=1, source_target_pairs={{0,96},{32,0},{64,32},{96,64},{1,97},{33,1},{65,33},{97,65},{2,98}... | collective-permute-start | bytes 1572872 | tf_op jit(solution)/shard_map/ppermute | solution.py:161
  42.0 2.0 %copy-start.5 = (bf16[1024,3,256]{0,2,1:T(8,128)(2,1)S(1)}, bf16[1024,3,256]{0,2,1:T(8,128)(2,1)}, u32[]{:S(2)}) copy-start(bf16[1024,3,256]{0,2,1:T(8,128)(2,1)} %copy.19) | copy-start | bytes 4718596
  47.1 18.8 %copy-start = (s32[64]{0:T(128)S(1)}, s32[64]{0:T(128)}, u32[]{:S(2)}) copy-start(s32[64]{0:T(128)} %pnode_ref.1) | copy-start | bytes 772
  47.1 18.8 %copy-start.1 = (s32[64]{0:T(128)S(1)}, s32[64]{0:T(128)}, u32[]{:S(2)}) copy-start(s32[64]{0:T(128)} %pfill_ref.1) | copy-start | bytes 772
  65.9 51.7 %copy-start.6 = (bf16[256,1024]{1,0:T(8,128)(2,1)S(1)}, bf16[256,1024]{1,0:T(8,128)(2,1)}, u32[]{:S(2)}) copy-start(bf16[256,1024]{1,0:T(8,128)(2,1)} %param.15) | copy-start | bytes 1572868
  112.6 8.7 %collective-permute-start.3 = (bf16[256,256]{1,0:T(8,128)(2,1)S(1)}, bf16[256,256]{1,0:T(8,128)(2,1)S(1)}, u32[]{:S(2)}, u32[]{:S(2)}) collective-permute-start(bf16[256,256]{1,0:T(8,128)(2,1)S(1)} %get-tuple-element.11), channel_id=1, source_target_pairs={{0,32},{32,64},{64,96},{96,0},{1,33},{33,65},{65,97},{97,1},{2,34}... | collective-permute-start | bytes 393224 | tf_op jit(solution)/shard_map/ppermute | solution.py:247
  113.9 8.0 %collective-permute-start.4 = (bf16[256,256]{1,0:T(8,128)(2,1)S(1)}, bf16[256,256]{1,0:T(8,128)(2,1)S(1)}, u32[]{:S(2)}, u32[]{:S(2)}) collective-permute-start(bf16[256,256]{1,0:T(8,128)(2,1)S(1)} %get-tuple-element.10), channel_id=1, source_target_pairs={{0,64},{32,96},{64,0},{96,32},{1,65},{33,97},{65,1},{97,33},{2,66}... | collective-permute-start | bytes 393224 | tf_op jit(solution)/shard_map/ppermute | solution.py:247
  116.5 5.5 %collective-permute-start.5 = (bf16[256,256]{1,0:T(8,128)(2,1)S(1)}, bf16[256,256]{1,0:T(8,128)(2,1)S(1)}, u32[]{:S(2)}, u32[]{:S(2)}) collective-permute-start(bf16[256,256]{1,0:T(8,128)(2,1)S(1)} %get-tuple-element.9), channel_id=1, source_target_pairs={{0,96},{32,0},{64,32},{96,64},{1,97},{33,1},{65,33},{97,65},{2,98}... | collective-permute-start | bytes 393224 | tf_op jit(solution)/shard_map/ppermute | solution.py:247
  121.3 1.6 %copy-start.3 = (bf16[4,256,1024]{2,1,0:T(8,128)(2,1)S(1)}, bf16[4,256,1024]{2,1,0:T(8,128)(2,1)}, u32[]{:S(2)}) copy-start(bf16[4,256,1024]{2,1,0:T(8,128)(2,1)} %gather_fusion.2) | copy-start | bytes 6291460
Sparse Core Ops, SparseCore 0:
  9.7 56.1 all-gather.1

commit v7 on v6

--- a/solution.py
+++ b/solution.py
@@ -10,6 +10,7 @@
 FLOOR_SCORE = -1e30
 Q_BLOCK = 256
 K_BLOCK = 128
+CHAINS = 3
 INTERPRET = False
 
 
@@ -22,8 +23,10 @@
     plist_ref, pcount_ref, pnode_ref, pfill_ref, kfirst_ref,
     qt_ref, tok_ref, kn_ref, vnt_ref, segk_ref, cache_ref,
     o_ref,
-    ma_sc, la_sc, acca_sc, mb_sc, lb_sc, accb_sc, cvt_ref,
+    *scratch,
 ):
+    cvt_ref = scratch[-1]
+    chains = [tuple(scratch[3 * c:3 * c + 3]) for c in range(CHAINS)]
     i = pl.program_id(0)
     width, tq = qt_ref.shape
     groups = width // HD
@@ -43,7 +46,7 @@
     leaf = tok_ref[1:2, :]
     upper = tok_ref[2:3, :]
     root = tok_ref[3:4, :]
-    for m_sc, l_sc, acc_sc in ((ma_sc, la_sc, acca_sc), (mb_sc, lb_sc, accb_sc)):
+    for m_sc, l_sc, acc_sc in chains:
         m_sc[...] = jnp.full(m_sc.shape, FLOOR_SCORE, jnp.float32)
         l_sc[...] = jnp.zeros(l_sc.shape, jnp.float32)
         acc_sc[...] = jnp.zeros(acc_sc.shape, jnp.float32)
@@ -73,8 +76,8 @@
         pv = jnp.dot(vbdt, jnp.concatenate(probs, axis=0), preferred_element_type=jnp.float32)
         acc_sc[...] = acc_sc[...] * jnp.concatenate(scales, axis=0) + pv
 
-    chain_a = (ma_sc, la_sc, acca_sc)
-    chain_b = (mb_sc, lb_sc, accb_sc)
+    chain_a = chains[0]
+    stride = plist_ref.shape[0] // kfirst_ref.shape[0]
     qpos = i * tq + lax.broadcasted_iota(jnp.int32, (1, tq), 1)
 
     def suffix_step(b, carry):
@@ -95,23 +98,29 @@
         tok_ok = (leaf == node) | (upper == node) | (root == node)
         return tok_ok & (slot < fill)
 
-    def pair_step(j, carry):
-        g0 = plist_ref[i * pages + 2 * j]
-        g1 = plist_ref[i * pages + 2 * j + 1]
-        update(chain_a, cache_ref[0, g0], cvt_ref[g0], page_mask(g0, True))
-        update(chain_b, cache_ref[0, g1], cvt_ref[g1], page_mask(g1, 2 * j + 1 < count))
+    def group_step(j, carry):
+        for c in range(CHAINS):
+            at = CHAINS * j + c
+            g = plist_ref[i * stride + at]
+            update(chains[c], cache_ref[0, g], cvt_ref[g], page_mask(g, at < count))
         return carry
 
-    lax.fori_loop(0, (count + 1) // 2, pair_step, 0)
+    lax.fori_loop(0, (count + CHAINS - 1) // CHAINS, group_step, 0)
 
     parts = []
     for h in range(groups):
-        m_all = jnp.maximum(ma_sc[h], mb_sc[h])
-        wa = jnp.exp(ma_sc[h] - m_all)
-        wb = jnp.exp(mb_sc[h] - m_all)
-        l_all = la_sc[h] * wa + lb_sc[h] * wb
+        m_all = chains[0][0][h]
+        for c in range(1, CHAINS):
+            m_all = jnp.maximum(m_all, chains[c][0][h])
         rows = slice(h * HD, (h + 1) * HD)
-        acc_h = acca_sc[rows, :] * wa + accb_sc[rows, :] * wb
+        l_all = None
+        acc_h = None
+        for m_sc, l_sc, acc_sc in chains:
+            w = jnp.exp(m_sc[h] - m_all)
+            l_part = l_sc[h] * w
+            acc_part = acc_sc[rows, :] * w
+            l_all = l_part if l_all is None else l_all + l_part
+            acc_h = acc_part if acc_h is None else acc_h + acc_part
         parts.append(acc_h / l_all)
     o_ref[...] = jnp.concatenate(parts, axis=0).astype(o_ref.dtype)
 
@@ -137,7 +146,7 @@
             pl.BlockSpec(memory_space=pltpu.VMEM),
         ],
         out_specs=pl.BlockSpec((width, Q_BLOCK), lambda i, *_: (0, i)),
-        scratch_shapes=state + state + [
+        scratch_shapes=state * CHAINS + [
             pltpu.VMEM((cache.shape[1], width, cache.shape[2]), jnp.bfloat16),
         ],
     )
@@ -226,7 +235,8 @@
     picked = (vis[:, :, None] > 0) & (rank[:, :, None] == jnp.arange(pages)[None, None, :])
     plist = jnp.sum(
         jnp.where(picked, jnp.arange(pages, dtype=jnp.int32)[None, :, None], 0), axis=1
-    ).astype(jnp.int32).reshape(-1)
+    ).astype(jnp.int32)
+    plist = jnp.pad(plist, ((0, 0), (0, CHAINS))).reshape(-1)
     pcount = jnp.sum(vis, axis=1).astype(jnp.int32)
     first_seg = segment[::Q_BLOCK]
     kfirst = (

time: 132 us -> 130 us (0.985); the launches traced: 131 us -> 131 us
  transfers between devices with their start and end apart: 10 -> 10, of which waited for: 4 -> 3; matrix products, arithmetic and copies ran while one was open for 20% -> 20% of each run, Pallas kernels for 35% -> 36%
where the time goes in v7:
time: 130 us; the launch traced here: 131 us
  Pallas kernels  46.7 us (36%)
  waiting for transfers between devices  28.1 us (22%)
  starting transfers between devices  14 us (11%)
  between operations  13.7 us (11%)
  other arithmetic  12.6 us (10%)
  local copies, waits for them, and re-layouts  11.7 us (9%)
  matrix products  4.68 us (4%)
    pallas_call x1, Pallas kernels, attention(): pl.pallas_call(attn_kernel, grid_spec=grid_spec, interpret=INTERPRET, out...  46.7 us
    all_gather x1, waiting for transfers between devices, shards(): cache = lax.all_gather(cache_kv, 'page', axis=1, tiled=True)  15.7 us
    ppermute x6, waiting for transfers between devices, head_gather(): lax.ppermute(x, 'head', shift_perm(n, d))  11.7 us
    ppermute x6, starting transfers between devices, head_gather(): lax.ppermute(x, 'head', shift_perm(n, d))  9 us
    ppermute x3, starting transfers between devices, shards(): parts.append(lax.ppermute(send, 'head', shift_perm(n_head, d)))  5.02 us
    gather x2, local copies, waits for them, and re-layouts, head_gather(): gathered = jnp.take(stacked, order, axis=0)  4.11 us
    another operation x2, other arithmetic, head_gather(): stacked = jnp.stack(parts)  3.24 us
    dot_general x1, matrix products, shards(): jnp.dot(head_gather(normed, n_head), weight_flat, preferred_element_type=...  3.06 us
  transfers between devices with their start and end apart: 10, of which 3 were waited for; matrix products, arithmetic and copies ran while one was open for 20% of the time, Pallas kernels for 36%

profile of v7, /device:TPU:1, one launch (start us, length us, event | category | flops | bytes accessed | tf_op | source)
XLA Modules:
  0.0 131.5 jit_solution(15673247303696536927)
XLA Ops:
  7.3 1.2 fusion.14
  8.5 1.2 fusion.16
  9.8 2.5 %collective-permute-start = (bf16[256,1024]{1,0:T(8,128)(2,1)S(1)}, bf16[256,1024]{1,0:T(8,128)(2,1)}, u32[]{:S(2)}, u32[]{:S(2)}) collective-permute-start(bf16[256,1024]{1,0:T(8,128)(2,1)S(1)} %fusion.16), channel_id=1, source_target_pairs={{0,32},{32,64},{64,96},{96,0},{1,33},{33,65},{65,97},{97,1},{2,34}... | collective-permute-start | bytes 1572872 | tf_op jit(solution)/shard_map/ppermute | solution.py:170
  12.3 3.3 %collective-permute-start.1 = (bf16[256,1024]{1,0:T(8,128)(2,1)S(1)}, bf16[256,1024]{1,0:T(8,128)(2,1)}, u32[]{:S(2)}, u32[]{:S(2)}) collective-permute-start(bf16[256,1024]{1,0:T(8,128)(2,1)S(1)} %fusion.16), channel_id=1, source_target_pairs={{0,64},{32,96},{64,0},{96,32},{1,65},{33,97},{65,1},{97,33},{2,66}... | collective-permute-start | bytes 1572872 | tf_op jit(solution)/shard_map/ppermute | solution.py:170
  20.6 0.9 or_reduce_fusion
  21.9 0.9 convert_reduce_fusion
  23.1 1.7 %copy.19 = bf16[1024,3,256]{0,2,1:T(8,128)(2,1)} copy(bf16[1024,3,256]{2,0,1:T(8,128)(2,1)S(1)} %copy-done.4) | data formatting | bytes 3145728 | tf_op args[2]
  26.2 1.3 collective-permute-start.8
  27.4 10.9 %collective-permute-done.1 = bf16[256,1024]{1,0:T(8,128)(2,1)} collective-permute-done((bf16[256,1024]{1,0:T(8,128)(2,1)S(1)}, bf16[256,1024]{1,0:T(8,128)(2,1)}, u32[]{:S(2)}, u32[]{:S(2)}) %collective-permute-start.1) | collective-permute-done | bytes 524320 | tf_op jit(solution)/shard_map/ppermute | solution.py:170
  38.3 1.6 %pad_maximum_fusion = bf16[4,256,1024]{2,1,0:T(8,128)(2,1)S(1)} fusion(bf16[1,256,1024]{2,1,0:T(8,128)(2,1)} %bitcast.5, bf16[1,256,1024]{2,1,0:T(8,128)(2,1)} %bitcast.4, bf16[1,256,1024]{2,1,0:T(8,128)(2,1)} %bitcast.3, bf16[1,256,1024]{2,1,0:T(8,128)(2,1)S(1)} %fusion.18), kind=kLoop, calls=%fused_computation.3 | loop fusion | flops 3145728 | bytes 4194304 | tf_op jit(solution)/shard_map/stack | solution.py:171
  40.0 2.1 %gather_fusion.1 = bf16[4,256,1024]{2,1,0:T(8,128)(2,1)} fusion(bf16[4,256,1024]{2,1,0:T(8,128)(2,1)S(1)} %pad_maximum_fusion, s32[1024]{0:T(1024)S(1)} %pad_clamp_fusion.1), kind=kCustom, calls=%fused_computation.clone | custom fusion | bytes 4194320 | tf_op jit(solution)/shard_map/jit(_take)/gather | solution.py:173
  42.0 2.0 %broadcast_select_fusion = bf16[4,256,1024]{2,1,0:T(8,128)(2,1)S(1)} fusion(bf16[4,256,1024]{2,1,0:T(8,128)(2,1)} %gather_fusion.1, pred[4]{0:T(512)(128)(4,1)S(1)} %compare_and_fusion), kind=kLoop, calls=%fused_computation.8 | loop fusion | flops 1048576 | bytes 4194308 | tf_op jit(solution)/shard_map/jit(_take)/select_n | solution.py:173
  44.1 3.1 %convolution_convert_fusion = bf16[1024,768]{0,1:T(8,128)(2,1)} fusion(bf16[1024,1024]{1,0:T(8,128)(2,1)S(1)} %bitcast.48, bf16[1024,768]{0,1:T(8,128)(2,1)S(1)} %bitcast.49), kind=kOutput, calls=%fused_computation.9 | convolution fusion | flops 1611399168 | bytes 5242880 | tf_op jit(solution)/shard_map/dot_general | solution.py:212
  47.1 1.7 %copy.21.kn_ref = bf16[1024,768]{1,0:T(8,128)(2,1)S(1)} copy(bf16[1024,768]{0,1:T(8,128)(2,1)} %convolution_convert_fusion) | data formatting | bytes 3145728 | tf_op jit(solution)/shard_map/convert_element_type | solution.py:216
  48.9 1.3 slice_bitcast_fusion
  50.2 15.7 %all-gather.2.cloned.1.call-done.cache_ref = bf16[2,64,128,256]{3,2,1,0:T(8,128)(2,1)} async-done(((bf16[2,2,128,256]{3,2,1,0:T(8,128)(2,1)}), bf16[2,64,128,256]{3,2,1,0:T(8,128)(2,1)}) %all-gather.2.cloned.1.call-update) | async-done | bytes 8388624 | tf_op jit(solution)/shard_map/all_gather | solution.py:248
  65.9 46.7 %shard_map.100 = bf16[256,1024]{1,0:T(8,128)(2,1)S(1)} custom-call(s32[268]{0:T(512)S(1)} %reshape.144.plist_ref, s32[4]{0:T(128)S(1)} %convert_reduce_fusion.1.pcount_ref, s32[64]{0:T(128)S(1)} %copy-done, s32[64]{0:T(128)S(1)} %copy-done.1, s32[4]{0:T(128)S(1)} %and_select_fusion.1.kfirst_ref, bf16[256,1024]{1,0:T(8,128)(2,1)S(1)} %get-tuple-element.7.qt_ref, ...), custom_call_target="tpu_custom_call" | custom-call | tf_op jit(solution)/shard_map/pallas_call | solution.py:153
  112.7 1.3 %collective-permute-start.3 = (bf16[256,256]{1,0:T(8,128)(2,1)S(1)}, bf16[256,256]{1,0:T(8,128)(2,1)S(1)}, u32[]{:S(2)}, u32[]{:S(2)}) collective-permute-start(bf16[256,256]{1,0:T(8,128)(2,1)S(1)} %get-tuple-element.11), channel_id=1, source_target_pairs={{0,32},{32,64},{64,96},{96,0},{1,33},{33,65},{65,97},{97,1},{2,34}... | collective-permute-start | bytes 393224 | tf_op jit(solution)/shard_map/ppermute | solution.py:257
  114.1 2.6 %collective-permute-start.4 = (bf16[256,256]{1,0:T(8,128)(2,1)S(1)}, bf16[256,256]{1,0:T(8,128)(2,1)S(1)}, u32[]{:S(2)}, u32[]{:S(2)}) collective-permute-start(bf16[256,256]{1,0:T(8,128)(2,1)S(1)} %get-tuple-element.10), channel_id=1, source_target_pairs={{0,64},{32,96},{64,0},{96,32},{1,65},{33,97},{65,1},{97,33},{2,66}... | collective-permute-start | bytes 393224 | tf_op jit(solution)/shard_map/ppermute | solution.py:257
  116.6 1.1 collective-permute-start.5
  117.7 1.6 %pad_maximum_fusion.1 = bf16[4,256,1024]{2,1,0:T(8,128)(2,1)S(1)} fusion(bf16[1,256,1024]{2,1,0:T(8,128)(2,1)} %bitcast.22, bf16[1,256,1024]{2,1,0:T(8,128)(2,1)} %bitcast.21, bf16[1,256,1024]{2,1,0:T(8,128)(2,1)} %bitcast.20, bf16[1,256,1024]{2,1,0:T(8,128)(2,1)S(1)} %bitcast.50), kind=kLoop, calls=%fused_computation.4 | loop fusion | flops 3145728 | bytes 4194304 | tf_op jit(solution)/shard_map/stack | solution.py:171
  119.4 2.0 %gather_fusion.2 = bf16[4,256,1024]{2,1,0:T(8,128)(2,1)} fusion(bf16[4,256,1024]{2,1,0:T(8,128)(2,1)S(1)} %pad_maximum_fusion.1, s32[1024]{0:T(1024)S(1)} %pad_clamp_fusion.1), kind=kCustom, calls=%fused_computation.1.clone | custom fusion | bytes 4194320 | tf_op jit(solution)/shard_map/jit(_take)/gather | solution.py:173
  122.1 0.9 copy-done.3
  123.0 1.6 %fusion.11 = bf16[1,256,1024]{2,1,0:T(8,128)(2,1)} fusion(bf16[4,256,1024]{2,1,0:T(8,128)(2,1)S(1)} %copy-done.3, pred[4]{0:T(512)(128)(4,1)S(1)} %compare_and_fusion, bf16[4,256,256]{2,1,0:T(8,128)(2,1)S(1)} %gather_fusion), kind=kOutput, calls=%fused_computation.16 | convolution fusion | flops 538443776 | bytes 3145732 | tf_op jit(solution)/shard_map/dot_general | solution.py:261
  (58 shorter events, 8.4 us)
Async XLA Ops:
  6.5 16.6 %copy-start.4 = (bf16[1024,3,256]{2,0,1:T(8,128)(2,1)S(1)}, bf16[1024,3,256]{2,0,1:T(8,128)(2,1)}, u32[]{:S(2)}) copy-start(bf16[1024,3,256]{2,0,1:T(8,128)(2,1)} %param.14) | copy-start | bytes 4718596
  6.5 59.4 %all-gather.2.cloned.1.call-start = ((), (), s32[]{:S(2)}) async-start(), calls=%async_computation | async-start | bytes 8650752 | tf_op jit(solution)/shard_map/all_gather | solution.py:248
  8.5 16.4 %copy-start.7 = (s32[1,1024]{1,0:T(1,128)S(1)}, s32[1,1024]{1,0:T(1,128)}, u32[]{:S(2)}) copy-start(s32[1,1024]{1,0:T(1,128)} %param.20) | copy-start | bytes 12292
  9.8 15.4 %copy-start.2 = (bf16[1,256,1024]{2,1,0:T(8,128)(2,1)S(1)}, bf16[1,256,1024]{2,1,0:T(8,128)(2,1)}, u32[]{:S(2)}) copy-start(bf16[1,256,1024]{2,1,0:T(8,128)(2,1)} %param.12) | copy-start | bytes 1572868
  9.8 15.4 %copy-start.8 = (f32[1024]{0:T(1024)S(1)}, f32[1024]{0:T(1024)}, u32[]{:S(2)}) copy-start(f32[1024]{0:T(1024)} %param.13) | copy-start | bytes 12292
  9.8 16.4 %collective-permute-start = (bf16[256,1024]{1,0:T(8,128)(2,1)S(1)}, bf16[256,1024]{1,0:T(8,128)(2,1)}, u32[]{:S(2)}, u32[]{:S(2)}) collective-permute-start(bf16[256,1024]{1,0:T(8,128)(2,1)S(1)} %fusion.16), channel_id=1, source_target_pairs={{0,32},{32,64},{64,96},{96,0},{1,33},{33,65},{65,97},{97,1},{2,34}... | collective-permute-start | bytes 1572872 | tf_op jit(solution)/shard_map/ppermute | solution.py:170
  12.3 26.0 %collective-permute-start.1 = (bf16[256,1024]{1,0:T(8,128)(2,1)S(1)}, bf16[256,1024]{1,0:T(8,128)(2,1)}, u32[]{:S(2)}, u32[]{:S(2)}) collective-permute-start(bf16[256,1024]{1,0:T(8,128)(2,1)S(1)} %fusion.16), channel_id=1, source_target_pairs={{0,64},{32,96},{64,0},{96,32},{1,65},{33,97},{65,1},{97,33},{2,66}... | collective-permute-start | bytes 1572872 | tf_op jit(solution)/shard_map/ppermute | solution.py:170
  15.6 22.7 %collective-permute-start.2 = (bf16[256,1024]{1,0:T(8,128)(2,1)S(1)}, bf16[256,1024]{1,0:T(8,128)(2,1)}, u32[]{:S(2)}, u32[]{:S(2)}) collective-permute-start(bf16[256,1024]{1,0:T(8,128)(2,1)S(1)} %fusion.16), channel_id=1, source_target_pairs={{0,96},{32,0},{64,32},{96,64},{1,97},{33,1},{65,33},{97,65},{2,98}... | collective-permute-start | bytes 1572872 | tf_op jit(solution)/shard_map/ppermute | solution.py:170
  16.3 100.3 %collective-permute-start.6 = (bf16[256,1024]{1,0:T(8,128)(2,1)}, bf16[256,1024]{1,0:T(8,128)(2,1)}, u32[]{:S(2)}, u32[]{:S(2)}) collective-permute-start(bf16[256,1024]{1,0:T(8,128)(2,1)} %param.15), channel_id=1, source_target_pairs={{0,32},{32,64},{64,96},{96,0},{1,33},{33,65},{65,97},{97,1},{2,34}... | collective-permute-start | bytes 1572872 | tf_op jit(solution)/shard_map/ppermute | solution.py:170
  17.1 100.7 %collective-permute-start.7 = (bf16[256,1024]{1,0:T(8,128)(2,1)}, bf16[256,1024]{1,0:T(8,128)(2,1)}, u32[]{:S(2)}, u32[]{:S(2)}) collective-permute-start(bf16[256,1024]{1,0:T(8,128)(2,1)} %param.15), channel_id=1, source_target_pairs={{0,64},{32,96},{64,0},{96,32},{1,65},{33,97},{65,1},{97,33},{2,66}... | collective-permute-start | bytes 1572872 | tf_op jit(solution)/shard_map/ppermute | solution.py:170
  26.2 91.6 %collective-permute-start.8 = (bf16[256,1024]{1,0:T(8,128)(2,1)}, bf16[256,1024]{1,0:T(8,128)(2,1)}, u32[]{:S(2)}, u32[]{:S(2)}) collective-permute-start(bf16[256,1024]{1,0:T(8,128)(2,1)} %param.15), channel_id=1, source_target_pairs={{0,96},{32,0},{64,32},{96,64},{1,97},{33,1},{65,33},{97,65},{2,98}... | collective-permute-start | bytes 1572872 | tf_op jit(solution)/shard_map/ppermute | solution.py:170
  42.0 2.0 %copy-start.5 = (bf16[1024,3,256]{0,2,1:T(8,128)(2,1)S(1)}, bf16[1024,3,256]{0,2,1:T(8,128)(2,1)}, u32[]{:S(2)}) copy-start(bf16[1024,3,256]{0,2,1:T(8,128)(2,1)} %copy.19) | copy-start | bytes 4718596
  47.1 18.8 %copy-start = (s32[64]{0:T(128)S(1)}, s32[64]{0:T(128)}, u32[]{:S(2)}) copy-start(s32[64]{0:T(128)} %pnode_ref.1) | copy-start | bytes 772
  47.1 18.8 %copy-start.1 = (s32[64]{0:T(128)S(1)}, s32[64]{0:T(128)}, u32[]{:S(2)}) copy-start(s32[64]{0:T(128)} %pfill_ref.1) | copy-start | bytes 772
  65.9 51.8 %copy-start.6 = (bf16[256,1024]{1,0:T(8,128)(2,1)S(1)}, bf16[256,1024]{1,0:T(8,128)(2,1)}, u32[]{:S(2)}) copy-start(bf16[256,1024]{1,0:T(8,128)(2,1)} %param.15) | copy-start | bytes 1572868
  112.7 8.7 %collective-permute-start.3 = (bf16[256,256]{1,0:T(8,128)(2,1)S(1)}, bf16[256,256]{1,0:T(8,128)(2,1)S(1)}, u32[]{:S(2)}, u32[]{:S(2)}) collective-permute-start(bf16[256,256]{1,0:T(8,128)(2,1)S(1)} %get-tuple-element.11), channel_id=1, source_target_pairs={{0,32},{32,64},{64,96},{96,0},{1,33},{33,65},{65,97},{97,1},{2,34}... | collective-permute-start | bytes 393224 | tf_op jit(solution)/shard_map/ppermute | solution.py:257
  114.1 7.3 %collective-permute-start.4 = (bf16[256,256]{1,0:T(8,128)(2,1)S(1)}, bf16[256,256]{1,0:T(8,128)(2,1)S(1)}, u32[]{:S(2)}, u32[]{:S(2)}) collective-permute-start(bf16[256,256]{1,0:T(8,128)(2,1)S(1)} %get-tuple-element.10), channel_id=1, source_target_pairs={{0,64},{32,96},{64,0},{96,32},{1,65},{33,97},{65,1},{97,33},{2,66}... | collective-permute-start | bytes 393224 | tf_op jit(solution)/shard_map/ppermute | solution.py:257
  116.6 4.8 %collective-permute-start.5 = (bf16[256,256]{1,0:T(8,128)(2,1)S(1)}, bf16[256,256]{1,0:T(8,128)(2,1)S(1)}, u32[]{:S(2)}, u32[]{:S(2)}) collective-permute-start(bf16[256,256]{1,0:T(8,128)(2,1)S(1)} %get-tuple-element.9), channel_id=1, source_target_pairs={{0,96},{32,0},{64,32},{96,64},{1,97},{33,1},{65,33},{97,65},{2,98}... | collective-permute-start | bytes 393224 | tf_op jit(solution)/shard_map/ppermute | solution.py:257
  121.4 1.6 %copy-start.3 = (bf16[4,256,1024]{2,1,0:T(8,128)(2,1)S(1)}, bf16[4,256,1024]{2,1,0:T(8,128)(2,1)}, u32[]{:S(2)}) copy-start(bf16[4,256,1024]{2,1,0:T(8,128)(2,1)} %gather_fusion.2) | copy-start | bytes 6291460
Sparse Core Ops, SparseCore 0:
  9.7 56.1 all-gather.1

commit v8 on v7

--- a/solution.py
+++ b/solution.py
@@ -76,19 +76,23 @@
         pv = jnp.dot(vbdt, jnp.concatenate(probs, axis=0), preferred_element_type=jnp.float32)
         acc_sc[...] = acc_sc[...] * jnp.concatenate(scales, axis=0) + pv
 
-    chain_a = chains[0]
     stride = plist_ref.shape[0] // kfirst_ref.shape[0]
     qpos = i * tq + lax.broadcasted_iota(jnp.int32, (1, tq), 1)
 
-    def suffix_step(b, carry):
-        start = pl.multiple_of(b * kb, kb)
-        kpos = start + slot
-        mask = (segk_ref[pl.ds(start, kb), :] == seg_q) & (kpos <= qpos)
-        update(chain_a, kn_ref[pl.ds(start, kb), :], vnt_ref[:, pl.ds(start, kb)], mask)
+    last = (i * tq + tq - 1) // kb
+    first = kfirst_ref[i]
+
+    def suffix_step(j, carry):
+        for c in range(CHAINS):
+            b = first + CHAINS * j + c
+            valid = b <= last
+            start = pl.multiple_of(jnp.minimum(b, last) * kb, kb)
+            kpos = start + slot
+            mask = (segk_ref[pl.ds(start, kb), :] == seg_q) & (kpos <= qpos) & valid
+            update(chains[c], kn_ref[pl.ds(start, kb), :], vnt_ref[:, pl.ds(start, kb)], mask)
         return carry
 
-    last = (i * tq + tq - 1) // kb
-    lax.fori_loop(kfirst_ref[i], last + 1, suffix_step, 0)
+    lax.fori_loop(0, (last - first + CHAINS) // CHAINS, suffix_step, 0)
 
     count = pcount_ref[i]
 

time: 130 us -> 125 us (0.962); the launches traced: 131 us -> 123 us
  Pallas kernels: 46.7 us -> 38.1 us
  waiting for transfers between devices: 28.1 us -> 29.5 us
    pallas_call x1, Pallas kernels: 46.7 us -> 38.1 us  [attention(): pl.pallas_call(attn_kernel, grid_spec=grid_spec, interpret=INTERPRET, out...]
    ppermute x3, waiting for transfers between devices: 0.01 us -> 1.39 us  [shards(): parts.append(lax.ppermute(send, 'head', shift_perm(n_head, d)))]
  transfers between devices with their start and end apart: 10 -> 10, of which waited for: 3 -> 4; matrix products, arithmetic and copies ran while one was open for 20% -> 21% of each run, Pallas kernels for 36% -> 31%
where the time goes in v8:
time: 125 us; the launch traced here: 123 us
  Pallas kernels  38.1 us (30%)
  waiting for transfers between devices  29.5 us (24%)
  starting transfers between devices  14 us (11%)
  between operations  13.7 us (11%)
  other arithmetic  12.6 us (10%)
  local copies, waits for them, and re-layouts  10.8 us (9%)
  matrix products  4.68 us (4%)
    pallas_call x1, Pallas kernels, attention(): pl.pallas_call(attn_kernel, grid_spec=grid_spec, interpret=INTERPRET, out...  38.1 us
    all_gather x1, waiting for transfers between devices, shards(): cache = lax.all_gather(cache_kv, 'page', axis=1, tiled=True)  15.7 us
    ppermute x6, waiting for transfers between devices, head_gather(): lax.ppermute(x, 'head', shift_perm(n, d))  11.7 us
    ppermute x6, starting transfers between devices, head_gather(): lax.ppermute(x, 'head', shift_perm(n, d))  9 us
    ppermute x3, starting transfers between devices, shards(): parts.append(lax.ppermute(send, 'head', shift_perm(n_head, d)))  5.01 us
    gather x2, local copies, waits for them, and re-layouts, head_gather(): gathered = jnp.take(stacked, order, axis=0)  4.11 us
    another operation x2, other arithmetic, head_gather(): stacked = jnp.stack(parts)  3.24 us
    dot_general x1, matrix products, shards(): jnp.dot(head_gather(normed, n_head), weight_flat, preferred_element_type=...  3.06 us
  transfers between devices with their start and end apart: 10, of which 4 were waited for; matrix products, arithmetic and copies ran while one was open for 21% of the time, Pallas kernels for 31%

profile of v8, /device:TPU:1, one launch (start us, length us, event | category | flops | bytes accessed | tf_op | source)
XLA Modules:
  0.0 123.3 jit_solution(17502457544962047736)
XLA Ops:
  7.3 1.2 fusion.14
  8.5 1.2 %fusion.16 = bf16[256,1024]{1,0:T(8,128)(2,1)S(1)} fusion(bf16[1,256,1024]{2,1,0:T(8,128)(2,1)} %param.12, f32[1024]{0:T(1024)} %param.13, f32[256]{0:T(256)S(1)} %add_rsqrt_fusion), kind=kLoop, calls=%fused_computation.19 | loop fusion | flops 1048576 | bytes 1053696 | tf_op jit(solution)/shard_map/convert_element_type | solution.py:210
  9.8 2.5 %collective-permute-start = (bf16[256,1024]{1,0:T(8,128)(2,1)S(1)}, bf16[256,1024]{1,0:T(8,128)(2,1)}, u32[]{:S(2)}, u32[]{:S(2)}) collective-permute-start(bf16[256,1024]{1,0:T(8,128)(2,1)S(1)} %fusion.16), channel_id=1, source_target_pairs={{0,32},{32,64},{64,96},{96,0},{1,33},{33,65},{65,97},{97,1},{2,34}... | collective-permute-start | bytes 1572872 | tf_op jit(solution)/shard_map/ppermute | solution.py:174
  12.3 3.3 %collective-permute-start.1 = (bf16[256,1024]{1,0:T(8,128)(2,1)S(1)}, bf16[256,1024]{1,0:T(8,128)(2,1)}, u32[]{:S(2)}, u32[]{:S(2)}) collective-permute-start(bf16[256,1024]{1,0:T(8,128)(2,1)S(1)} %fusion.16), channel_id=1, source_target_pairs={{0,64},{32,96},{64,0},{96,32},{1,65},{33,97},{65,1},{97,33},{2,66}... | collective-permute-start | bytes 1572872 | tf_op jit(solution)/shard_map/ppermute | solution.py:174
  20.6 0.9 or_reduce_fusion
  21.9 0.9 convert_reduce_fusion
  23.1 1.7 %copy.19 = bf16[1024,3,256]{0,2,1:T(8,128)(2,1)} copy(bf16[1024,3,256]{2,0,1:T(8,128)(2,1)S(1)} %copy-done.4) | data formatting | bytes 3145728 | tf_op args[2]
  26.2 1.3 %collective-permute-start.8 = (bf16[256,1024]{1,0:T(8,128)(2,1)}, bf16[256,1024]{1,0:T(8,128)(2,1)}, u32[]{:S(2)}, u32[]{:S(2)}) collective-permute-start(bf16[256,1024]{1,0:T(8,128)(2,1)} %param.15), channel_id=1, source_target_pairs={{0,96},{32,0},{64,32},{96,64},{1,97},{33,1},{65,33},{97,65},{2,98}... | collective-permute-start | bytes 1572872 | tf_op jit(solution)/shard_map/ppermute | solution.py:174
  27.4 10.9 %collective-permute-done.1 = bf16[256,1024]{1,0:T(8,128)(2,1)} collective-permute-done((bf16[256,1024]{1,0:T(8,128)(2,1)S(1)}, bf16[256,1024]{1,0:T(8,128)(2,1)}, u32[]{:S(2)}, u32[]{:S(2)}) %collective-permute-start.1) | collective-permute-done | bytes 524320 | tf_op jit(solution)/shard_map/ppermute | solution.py:174
  38.3 1.6 %pad_maximum_fusion = bf16[4,256,1024]{2,1,0:T(8,128)(2,1)S(1)} fusion(bf16[1,256,1024]{2,1,0:T(8,128)(2,1)} %bitcast.5, bf16[1,256,1024]{2,1,0:T(8,128)(2,1)} %bitcast.4, bf16[1,256,1024]{2,1,0:T(8,128)(2,1)} %bitcast.3, bf16[1,256,1024]{2,1,0:T(8,128)(2,1)S(1)} %fusion.18), kind=kLoop, calls=%fused_computation.3 | loop fusion | flops 3145728 | bytes 4194304 | tf_op jit(solution)/shard_map/stack | solution.py:175
  40.0 2.1 %gather_fusion.1 = bf16[4,256,1024]{2,1,0:T(8,128)(2,1)} fusion(bf16[4,256,1024]{2,1,0:T(8,128)(2,1)S(1)} %pad_maximum_fusion, s32[1024]{0:T(1024)S(1)} %pad_clamp_fusion.1), kind=kCustom, calls=%fused_computation.clone | custom fusion | bytes 4194320 | tf_op jit(solution)/shard_map/jit(_take)/gather | solution.py:177
  42.0 2.0 %broadcast_select_fusion = bf16[4,256,1024]{2,1,0:T(8,128)(2,1)S(1)} fusion(bf16[4,256,1024]{2,1,0:T(8,128)(2,1)} %gather_fusion.1, pred[4]{0:T(512)(128)(4,1)S(1)} %compare_and_fusion), kind=kLoop, calls=%fused_computation.8 | loop fusion | flops 1048576 | bytes 4194308 | tf_op jit(solution)/shard_map/jit(_take)/select_n | solution.py:177
  44.1 3.1 %convolution_convert_fusion = bf16[1024,768]{0,1:T(8,128)(2,1)} fusion(bf16[1024,1024]{1,0:T(8,128)(2,1)S(1)} %bitcast.48, bf16[1024,768]{0,1:T(8,128)(2,1)S(1)} %bitcast.49), kind=kOutput, calls=%fused_computation.9 | convolution fusion | flops 1611399168 | bytes 5242880 | tf_op jit(solution)/shard_map/dot_general | solution.py:216
  47.1 1.7 %copy.21.kn_ref = bf16[1024,768]{1,0:T(8,128)(2,1)S(1)} copy(bf16[1024,768]{0,1:T(8,128)(2,1)} %convolution_convert_fusion) | data formatting | bytes 3145728 | tf_op jit(solution)/shard_map/convert_element_type | solution.py:220
  48.9 1.3 %slice_bitcast_fusion = (bf16[256,1024]{1,0:T(8,128)(2,1)S(1)}, bf16[256,1024]{1,0:T(8,128)(2,1)S(1)}) fusion(bf16[1024,768]{0,1:T(8,128)(2,1)} %convolution_convert_fusion), kind=kLoop, calls=%fused_computation.23 | loop fusion | bytes 2097152 | tf_op jit(solution)/shard_map/transpose | solution.py:251
  50.2 15.7 %all-gather.2.cloned.1.call-done.cache_ref = bf16[2,64,128,256]{3,2,1,0:T(8,128)(2,1)} async-done(((bf16[2,2,128,256]{3,2,1,0:T(8,128)(2,1)}), bf16[2,64,128,256]{3,2,1,0:T(8,128)(2,1)}) %all-gather.2.cloned.1.call-update) | async-done | bytes 8388624 | tf_op jit(solution)/shard_map/all_gather | solution.py:252
  65.9 38.1 %shard_map.100 = bf16[256,1024]{1,0:T(8,128)(2,1)S(1)} custom-call(s32[268]{0:T(512)S(1)} %reshape.144.plist_ref, s32[4]{0:T(128)S(1)} %convert_reduce_fusion.1.pcount_ref, s32[64]{0:T(128)S(1)} %copy-done, s32[64]{0:T(128)S(1)} %copy-done.1, s32[4]{0:T(128)S(1)} %and_select_fusion.1.kfirst_ref, bf16[256,1024]{1,0:T(8,128)(2,1)S(1)} %get-tuple-element.7.qt_ref, ...), custom_call_target="tpu_custom_call" | custom-call | tf_op jit(solution)/shard_map/pallas_call | solution.py:157
  104.1 1.3 %collective-permute-start.3 = (bf16[256,256]{1,0:T(8,128)(2,1)S(1)}, bf16[256,256]{1,0:T(8,128)(2,1)S(1)}, u32[]{:S(2)}, u32[]{:S(2)}) collective-permute-start(bf16[256,256]{1,0:T(8,128)(2,1)S(1)} %get-tuple-element.11), channel_id=1, source_target_pairs={{0,32},{32,64},{64,96},{96,0},{1,33},{33,65},{65,97},{97,1},{2,34}... | collective-permute-start | bytes 393224 | tf_op jit(solution)/shard_map/ppermute | solution.py:261
  105.4 2.6 %collective-permute-start.4 = (bf16[256,256]{1,0:T(8,128)(2,1)S(1)}, bf16[256,256]{1,0:T(8,128)(2,1)S(1)}, u32[]{:S(2)}, u32[]{:S(2)}) collective-permute-start(bf16[256,256]{1,0:T(8,128)(2,1)S(1)} %get-tuple-element.10), channel_id=1, source_target_pairs={{0,64},{32,96},{64,0},{96,32},{1,65},{33,97},{65,1},{97,33},{2,66}... | collective-permute-start | bytes 393224 | tf_op jit(solution)/shard_map/ppermute | solution.py:261
  108.0 1.1 collective-permute-start.5
  109.1 1.6 %pad_maximum_fusion.1 = bf16[4,256,1024]{2,1,0:T(8,128)(2,1)S(1)} fusion(bf16[1,256,1024]{2,1,0:T(8,128)(2,1)} %bitcast.22, bf16[1,256,1024]{2,1,0:T(8,128)(2,1)} %bitcast.21, bf16[1,256,1024]{2,1,0:T(8,128)(2,1)} %bitcast.20, bf16[1,256,1024]{2,1,0:T(8,128)(2,1)S(1)} %bitcast.50), kind=kLoop, calls=%fused_computation.4 | loop fusion | flops 3145728 | bytes 4194304 | tf_op jit(solution)/shard_map/stack | solution.py:175
  110.7 2.0 %gather_fusion.2 = bf16[4,256,1024]{2,1,0:T(8,128)(2,1)} fusion(bf16[4,256,1024]{2,1,0:T(8,128)(2,1)S(1)} %pad_maximum_fusion.1, s32[1024]{0:T(1024)S(1)} %pad_clamp_fusion.1), kind=kCustom, calls=%fused_computation.1.clone | custom fusion | bytes 4194320 | tf_op jit(solution)/shard_map/jit(_take)/gather | solution.py:177
  112.7 1.4 %collective-permute-done.4 = bf16[256,256]{1,0:T(8,128)(2,1)S(1)} collective-permute-done((bf16[256,256]{1,0:T(8,128)(2,1)S(1)}, bf16[256,256]{1,0:T(8,128)(2,1)S(1)}, u32[]{:S(2)}, u32[]{:S(2)}) %collective-permute-start.4) | collective-permute-done | bytes 131104 | tf_op jit(solution)/shard_map/ppermute | solution.py:261
  114.8 1.6 %fusion.11 = bf16[1,256,1024]{2,1,0:T(8,128)(2,1)} fusion(bf16[4,256,1024]{2,1,0:T(8,128)(2,1)S(1)} %copy-done.3, pred[4]{0:T(512)(128)(4,1)S(1)} %compare_and_fusion, bf16[4,256,256]{2,1,0:T(8,128)(2,1)S(1)} %gather_fusion), kind=kOutput, calls=%fused_computation.16 | convolution fusion | flops 538443776 | bytes 3145732 | tf_op jit(solution)/shard_map/dot_general | solution.py:265
  (58 shorter events, 8.4 us)
Async XLA Ops:
  6.5 16.6 %copy-start.4 = (bf16[1024,3,256]{2,0,1:T(8,128)(2,1)S(1)}, bf16[1024,3,256]{2,0,1:T(8,128)(2,1)}, u32[]{:S(2)}) copy-start(bf16[1024,3,256]{2,0,1:T(8,128)(2,1)} %param.14) | copy-start | bytes 4718596
  6.5 59.4 %all-gather.2.cloned.1.call-start = ((), (), s32[]{:S(2)}) async-start(), calls=%async_computation | async-start | bytes 8650752 | tf_op jit(solution)/shard_map/all_gather | solution.py:252
  8.5 16.4 %copy-start.7 = (s32[1,1024]{1,0:T(1,128)S(1)}, s32[1,1024]{1,0:T(1,128)}, u32[]{:S(2)}) copy-start(s32[1,1024]{1,0:T(1,128)} %param.20) | copy-start | bytes 12292
  9.8 15.4 %copy-start.2 = (bf16[1,256,1024]{2,1,0:T(8,128)(2,1)S(1)}, bf16[1,256,1024]{2,1,0:T(8,128)(2,1)}, u32[]{:S(2)}) copy-start(bf16[1,256,1024]{2,1,0:T(8,128)(2,1)} %param.12) | copy-start | bytes 1572868
  9.8 15.4 %copy-start.8 = (f32[1024]{0:T(1024)S(1)}, f32[1024]{0:T(1024)}, u32[]{:S(2)}) copy-start(f32[1024]{0:T(1024)} %param.13) | copy-start | bytes 12292
  9.8 16.4 %collective-permute-start = (bf16[256,1024]{1,0:T(8,128)(2,1)S(1)}, bf16[256,1024]{1,0:T(8,128)(2,1)}, u32[]{:S(2)}, u32[]{:S(2)}) collective-permute-start(bf16[256,1024]{1,0:T(8,128)(2,1)S(1)} %fusion.16), channel_id=1, source_target_pairs={{0,32},{32,64},{64,96},{96,0},{1,33},{33,65},{65,97},{97,1},{2,34}... | collective-permute-start | bytes 1572872 | tf_op jit(solution)/shard_map/ppermute | solution.py:174
  12.3 26.0 %collective-permute-start.1 = (bf16[256,1024]{1,0:T(8,128)(2,1)S(1)}, bf16[256,1024]{1,0:T(8,128)(2,1)}, u32[]{:S(2)}, u32[]{:S(2)}) collective-permute-start(bf16[256,1024]{1,0:T(8,128)(2,1)S(1)} %fusion.16), channel_id=1, source_target_pairs={{0,64},{32,96},{64,0},{96,32},{1,65},{33,97},{65,1},{97,33},{2,66}... | collective-permute-start | bytes 1572872 | tf_op jit(solution)/shard_map/ppermute | solution.py:174
  15.6 22.7 %collective-permute-start.2 = (bf16[256,1024]{1,0:T(8,128)(2,1)S(1)}, bf16[256,1024]{1,0:T(8,128)(2,1)}, u32[]{:S(2)}, u32[]{:S(2)}) collective-permute-start(bf16[256,1024]{1,0:T(8,128)(2,1)S(1)} %fusion.16), channel_id=1, source_target_pairs={{0,96},{32,0},{64,32},{96,64},{1,97},{33,1},{65,33},{97,65},{2,98}... | collective-permute-start | bytes 1572872 | tf_op jit(solution)/shard_map/ppermute | solution.py:174
  16.3 91.7 %collective-permute-start.6 = (bf16[256,1024]{1,0:T(8,128)(2,1)}, bf16[256,1024]{1,0:T(8,128)(2,1)}, u32[]{:S(2)}, u32[]{:S(2)}) collective-permute-start(bf16[256,1024]{1,0:T(8,128)(2,1)} %param.15), channel_id=1, source_target_pairs={{0,32},{32,64},{64,96},{96,0},{1,33},{33,65},{65,97},{97,1},{2,34}... | collective-permute-start | bytes 1572872 | tf_op jit(solution)/shard_map/ppermute | solution.py:174
  17.1 92.0 %collective-permute-start.7 = (bf16[256,1024]{1,0:T(8,128)(2,1)}, bf16[256,1024]{1,0:T(8,128)(2,1)}, u32[]{:S(2)}, u32[]{:S(2)}) collective-permute-start(bf16[256,1024]{1,0:T(8,128)(2,1)} %param.15), channel_id=1, source_target_pairs={{0,64},{32,96},{64,0},{96,32},{1,65},{33,97},{65,1},{97,33},{2,66}... | collective-permute-start | bytes 1572872 | tf_op jit(solution)/shard_map/ppermute | solution.py:174
  26.2 82.9 %collective-permute-start.8 = (bf16[256,1024]{1,0:T(8,128)(2,1)}, bf16[256,1024]{1,0:T(8,128)(2,1)}, u32[]{:S(2)}, u32[]{:S(2)}) collective-permute-start(bf16[256,1024]{1,0:T(8,128)(2,1)} %param.15), channel_id=1, source_target_pairs={{0,96},{32,0},{64,32},{96,64},{1,97},{33,1},{65,33},{97,65},{2,98}... | collective-permute-start | bytes 1572872 | tf_op jit(solution)/shard_map/ppermute | solution.py:174
  42.0 2.0 %copy-start.5 = (bf16[1024,3,256]{0,2,1:T(8,128)(2,1)S(1)}, bf16[1024,3,256]{0,2,1:T(8,128)(2,1)}, u32[]{:S(2)}) copy-start(bf16[1024,3,256]{0,2,1:T(8,128)(2,1)} %copy.19) | copy-start | bytes 4718596
  47.1 18.8 %copy-start = (s32[64]{0:T(128)S(1)}, s32[64]{0:T(128)}, u32[]{:S(2)}) copy-start(s32[64]{0:T(128)} %pnode_ref.1) | copy-start | bytes 772
  47.1 18.8 %copy-start.1 = (s32[64]{0:T(128)S(1)}, s32[64]{0:T(128)}, u32[]{:S(2)}) copy-start(s32[64]{0:T(128)} %pfill_ref.1) | copy-start | bytes 772
  65.9 43.2 %copy-start.6 = (bf16[256,1024]{1,0:T(8,128)(2,1)S(1)}, bf16[256,1024]{1,0:T(8,128)(2,1)}, u32[]{:S(2)}) copy-start(bf16[256,1024]{1,0:T(8,128)(2,1)} %param.15) | copy-start | bytes 1572868
  104.1 8.7 %collective-permute-start.3 = (bf16[256,256]{1,0:T(8,128)(2,1)S(1)}, bf16[256,256]{1,0:T(8,128)(2,1)S(1)}, u32[]{:S(2)}, u32[]{:S(2)}) collective-permute-start(bf16[256,256]{1,0:T(8,128)(2,1)S(1)} %get-tuple-element.11), channel_id=1, source_target_pairs={{0,32},{32,64},{64,96},{96,0},{1,33},{33,65},{65,97},{97,1},{2,34}... | collective-permute-start | bytes 393224 | tf_op jit(solution)/shard_map/ppermute | solution.py:261
  105.4 8.7 %collective-permute-start.4 = (bf16[256,256]{1,0:T(8,128)(2,1)S(1)}, bf16[256,256]{1,0:T(8,128)(2,1)S(1)}, u32[]{:S(2)}, u32[]{:S(2)}) collective-permute-start(bf16[256,256]{1,0:T(8,128)(2,1)S(1)} %get-tuple-element.10), channel_id=1, source_target_pairs={{0,64},{32,96},{64,0},{96,32},{1,65},{33,97},{65,1},{97,33},{2,66}... | collective-permute-start | bytes 393224 | tf_op jit(solution)/shard_map/ppermute | solution.py:261
  108.0 6.2 %collective-permute-start.5 = (bf16[256,256]{1,0:T(8,128)(2,1)S(1)}, bf16[256,256]{1,0:T(8,128)(2,1)S(1)}, u32[]{:S(2)}, u32[]{:S(2)}) collective-permute-start(bf16[256,256]{1,0:T(8,128)(2,1)S(1)} %get-tuple-element.9), channel_id=1, source_target_pairs={{0,96},{32,0},{64,32},{96,64},{1,97},{33,1},{65,33},{97,65},{2,98}... | collective-permute-start | bytes 393224 | tf_op jit(solution)/shard_map/ppermute | solution.py:261
  112.7 2.1 %copy-start.3 = (bf16[4,256,1024]{2,1,0:T(8,128)(2,1)S(1)}, bf16[4,256,1024]{2,1,0:T(8,128)(2,1)}, u32[]{:S(2)}) copy-start(bf16[4,256,1024]{2,1,0:T(8,128)(2,1)} %gather_fusion.2) | copy-start | bytes 6291460
Sparse Core Ops, SparseCore 0:
  9.7 56.1 all-gather.1

commit v9 on v8

--- a/solution.py
+++ b/solution.py
@@ -10,7 +10,7 @@
 FLOOR_SCORE = -1e30
 Q_BLOCK = 256
 K_BLOCK = 128
-CHAINS = 3
+CHAINS = 4
 INTERPRET = False
 
 

time: 125 us -> 127 us (1.016); the launches traced: 123 us -> 127 us
  Pallas kernels: 38.1 us -> 42.2 us
    pallas_call x1, Pallas kernels: 38.1 us -> 42.2 us  [attention(): pl.pallas_call(attn_kernel, grid_spec=grid_spec, interpret=INTERPRET, out...]
  transfers between devices with their start and end apart: 10 -> 10, of which waited for: 4 -> 4; matrix products, arithmetic and copies ran while one was open for 21% -> 20% of each run, Pallas kernels for 31% -> 33%
where the time goes in v9:
time: 127 us
  Pallas kernels  42.2 us (33%)
  waiting for transfers between devices  28.5 us (22%)
  starting transfers between devices  14 us (11%)
  between operations  13.6 us (11%)
  other arithmetic  12.6 us (10%)
  local copies, waits for them, and re-layouts  11.4 us (9%)
  matrix products  4.68 us (4%)
    pallas_call x1, Pallas kernels, attention(): pl.pallas_call(attn_kernel, grid_spec=grid_spec, interpret=INTERPRET, out...  42.2 us
    all_gather x1, waiting for transfers between devices, shards(): cache = lax.all_gather(cache_kv, 'page', axis=1, tiled=True)  15.7 us
    ppermute x6, waiting for transfers between devices, head_gather(): lax.ppermute(x, 'head', shift_perm(n, d))  11.7 us
    ppermute x6, starting transfers between devices, head_gather(): lax.ppermute(x, 'head', shift_perm(n, d))  9 us
    ppermute x3, starting transfers between devices, shards(): parts.append(lax.ppermute(send, 'head', shift_perm(n_head, d)))  5 us
    gather x2, local copies, waits for them, and re-layouts, head_gather(): gathered = jnp.take(stacked, order, axis=0)  4.11 us
    another operation x2, other arithmetic, head_gather(): stacked = jnp.stack(parts)  3.24 us
    dot_general x1, matrix products, shards(): jnp.dot(head_gather(normed, n_head), weight_flat, preferred_element_type=...  3.06 us
  transfers between devices with their start and end apart: 10, of which 4 were waited for; matrix products, arithmetic and copies ran while one was open for 20% of the time, Pallas kernels for 33%

profile of v9, /device:TPU:1, one launch (start us, length us, event | category | flops | bytes accessed | tf_op | source)
XLA Modules:
  0.0 127.0 jit_solution(6568743993148414692)
XLA Ops:
  7.3 1.2 fusion.14
  8.5 1.2 fusion.16
  9.8 2.5 %collective-permute-start = (bf16[256,1024]{1,0:T(8,128)(2,1)S(1)}, bf16[256,1024]{1,0:T(8,128)(2,1)}, u32[]{:S(2)}, u32[]{:S(2)}) collective-permute-start(bf16[256,1024]{1,0:T(8,128)(2,1)S(1)} %fusion.16), channel_id=1, source_target_pairs={{0,32},{32,64},{64,96},{96,0},{1,33},{33,65},{65,97},{97,1},{2,34}... | collective-permute-start | bytes 1572872 | tf_op jit(solution)/shard_map/ppermute | solution.py:174
  12.3 3.3 %collective-permute-start.1 = (bf16[256,1024]{1,0:T(8,128)(2,1)S(1)}, bf16[256,1024]{1,0:T(8,128)(2,1)}, u32[]{:S(2)}, u32[]{:S(2)}) collective-permute-start(bf16[256,1024]{1,0:T(8,128)(2,1)S(1)} %fusion.16), channel_id=1, source_target_pairs={{0,64},{32,96},{64,0},{96,32},{1,65},{33,97},{65,1},{97,33},{2,66}... | collective-permute-start | bytes 1572872 | tf_op jit(solution)/shard_map/ppermute | solution.py:174
  18.3 0.8 select_reduce_fusion.3
  20.6 0.9 or_reduce_fusion
  21.9 0.9 convert_reduce_fusion
  23.1 1.7 %copy.19 = bf16[1024,3,256]{0,2,1:T(8,128)(2,1)} copy(bf16[1024,3,256]{2,0,1:T(8,128)(2,1)S(1)} %copy-done.4) | data formatting | bytes 3145728 | tf_op args[2]
  26.2 1.3 collective-permute-start.8
  27.4 10.9 %collective-permute-done.1 = bf16[256,1024]{1,0:T(8,128)(2,1)} collective-permute-done((bf16[256,1024]{1,0:T(8,128)(2,1)S(1)}, bf16[256,1024]{1,0:T(8,128)(2,1)}, u32[]{:S(2)}, u32[]{:S(2)}) %collective-permute-start.1) | collective-permute-done | bytes 524320 | tf_op jit(solution)/shard_map/ppermute | solution.py:174
  38.3 1.6 %pad_maximum_fusion = bf16[4,256,1024]{2,1,0:T(8,128)(2,1)S(1)} fusion(bf16[1,256,1024]{2,1,0:T(8,128)(2,1)} %bitcast.5, bf16[1,256,1024]{2,1,0:T(8,128)(2,1)} %bitcast.4, bf16[1,256,1024]{2,1,0:T(8,128)(2,1)} %bitcast.3, bf16[1,256,1024]{2,1,0:T(8,128)(2,1)S(1)} %fusion.18), kind=kLoop, calls=%fused_computation.3 | loop fusion | flops 3145728 | bytes 4194304 | tf_op jit(solution)/shard_map/stack | solution.py:175
  40.0 2.1 %gather_fusion.1 = bf16[4,256,1024]{2,1,0:T(8,128)(2,1)} fusion(bf16[4,256,1024]{2,1,0:T(8,128)(2,1)S(1)} %pad_maximum_fusion, s32[1024]{0:T(1024)S(1)} %pad_clamp_fusion.1), kind=kCustom, calls=%fused_computation.clone | custom fusion | bytes 4194320 | tf_op jit(solution)/shard_map/jit(_take)/gather | solution.py:177
  42.0 2.0 %broadcast_select_fusion = bf16[4,256,1024]{2,1,0:T(8,128)(2,1)S(1)} fusion(bf16[4,256,1024]{2,1,0:T(8,128)(2,1)} %gather_fusion.1, pred[4]{0:T(512)(128)(4,1)S(1)} %compare_and_fusion), kind=kLoop, calls=%fused_computation.8 | loop fusion | flops 1048576 | bytes 4194308 | tf_op jit(solution)/shard_map/jit(_take)/select_n | solution.py:177
  44.1 3.1 %convolution_convert_fusion = bf16[1024,768]{0,1:T(8,128)(2,1)} fusion(bf16[1024,1024]{1,0:T(8,128)(2,1)S(1)} %bitcast.48, bf16[1024,768]{0,1:T(8,128)(2,1)S(1)} %bitcast.49), kind=kOutput, calls=%fused_computation.9 | convolution fusion | flops 1611399168 | bytes 5242880 | tf_op jit(solution)/shard_map/dot_general | solution.py:216
  47.1 1.7 %copy.21.kn_ref = bf16[1024,768]{1,0:T(8,128)(2,1)S(1)} copy(bf16[1024,768]{0,1:T(8,128)(2,1)} %convolution_convert_fusion) | data formatting | bytes 3145728 | tf_op jit(solution)/shard_map/convert_element_type | solution.py:220
  48.9 1.3 %slice_bitcast_fusion = (bf16[256,1024]{1,0:T(8,128)(2,1)S(1)}, bf16[256,1024]{1,0:T(8,128)(2,1)S(1)}) fusion(bf16[1024,768]{0,1:T(8,128)(2,1)} %convolution_convert_fusion), kind=kLoop, calls=%fused_computation.23 | loop fusion | bytes 2097152 | tf_op jit(solution)/shard_map/transpose | solution.py:251
  50.2 15.7 %all-gather.2.cloned.1.call-done.cache_ref = bf16[2,64,128,256]{3,2,1,0:T(8,128)(2,1)} async-done(((bf16[2,2,128,256]{3,2,1,0:T(8,128)(2,1)}), bf16[2,64,128,256]{3,2,1,0:T(8,128)(2,1)}) %all-gather.2.cloned.1.call-update) | async-done | bytes 8388624 | tf_op jit(solution)/shard_map/all_gather | solution.py:252
  65.9 42.2 %shard_map.100 = bf16[256,1024]{1,0:T(8,128)(2,1)S(1)} custom-call(s32[272]{0:T(512)S(1)} %reshape.144.plist_ref, s32[4]{0:T(128)S(1)} %convert_reduce_fusion.1.pcount_ref, s32[64]{0:T(128)S(1)} %copy-done, s32[64]{0:T(128)S(1)} %copy-done.1, s32[4]{0:T(128)S(1)} %and_select_fusion.1.kfirst_ref, bf16[256,1024]{1,0:T(8,128)(2,1)S(1)} %get-tuple-element.7.qt_ref, ...), custom_call_target="tpu_custom_call" | custom-call | tf_op jit(solution)/shard_map/pallas_call | solution.py:157
  108.2 1.3 %collective-permute-start.3 = (bf16[256,256]{1,0:T(8,128)(2,1)S(1)}, bf16[256,256]{1,0:T(8,128)(2,1)S(1)}, u32[]{:S(2)}, u32[]{:S(2)}) collective-permute-start(bf16[256,256]{1,0:T(8,128)(2,1)S(1)} %get-tuple-element.11), channel_id=1, source_target_pairs={{0,32},{32,64},{64,96},{96,0},{1,33},{33,65},{65,97},{97,1},{2,34}... | collective-permute-start | bytes 393224 | tf_op jit(solution)/shard_map/ppermute | solution.py:261
  109.6 2.6 %collective-permute-start.4 = (bf16[256,256]{1,0:T(8,128)(2,1)S(1)}, bf16[256,256]{1,0:T(8,128)(2,1)S(1)}, u32[]{:S(2)}, u32[]{:S(2)}) collective-permute-start(bf16[256,256]{1,0:T(8,128)(2,1)S(1)} %get-tuple-element.10), channel_id=1, source_target_pairs={{0,64},{32,96},{64,0},{96,32},{1,65},{33,97},{65,1},{97,33},{2,66}... | collective-permute-start | bytes 393224 | tf_op jit(solution)/shard_map/ppermute | solution.py:261
  112.2 1.1 collective-permute-start.5
  113.3 1.6 %pad_maximum_fusion.1 = bf16[4,256,1024]{2,1,0:T(8,128)(2,1)S(1)} fusion(bf16[1,256,1024]{2,1,0:T(8,128)(2,1)} %bitcast.22, bf16[1,256,1024]{2,1,0:T(8,128)(2,1)} %bitcast.21, bf16[1,256,1024]{2,1,0:T(8,128)(2,1)} %bitcast.20, bf16[1,256,1024]{2,1,0:T(8,128)(2,1)S(1)} %bitcast.50), kind=kLoop, calls=%fused_computation.4 | loop fusion | flops 3145728 | bytes 4194304 | tf_op jit(solution)/shard_map/stack | solution.py:175
  114.9 2.0 %gather_fusion.2 = bf16[4,256,1024]{2,1,0:T(8,128)(2,1)} fusion(bf16[4,256,1024]{2,1,0:T(8,128)(2,1)S(1)} %pad_maximum_fusion.1, s32[1024]{0:T(1024)S(1)} %pad_clamp_fusion.1), kind=kCustom, calls=%fused_computation.1.clone | custom fusion | bytes 4194320 | tf_op jit(solution)/shard_map/jit(_take)/gather | solution.py:177
  118.5 1.6 %fusion.11 = bf16[1,256,1024]{2,1,0:T(8,128)(2,1)} fusion(bf16[4,256,1024]{2,1,0:T(8,128)(2,1)S(1)} %copy-done.3, pred[4]{0:T(512)(128)(4,1)S(1)} %compare_and_fusion, bf16[4,256,256]{2,1,0:T(8,128)(2,1)S(1)} %gather_fusion), kind=kOutput, calls=%fused_computation.16 | convolution fusion | flops 538443776 | bytes 3145732 | tf_op jit(solution)/shard_map/dot_general | solution.py:265
  (58 shorter events, 8.6 us)
Async XLA Ops:
  6.5 16.6 %copy-start.4 = (bf16[1024,3,256]{2,0,1:T(8,128)(2,1)S(1)}, bf16[1024,3,256]{2,0,1:T(8,128)(2,1)}, u32[]{:S(2)}) copy-start(bf16[1024,3,256]{2,0,1:T(8,128)(2,1)} %param.14) | copy-start | bytes 4718596
  6.5 59.4 %all-gather.2.cloned.1.call-start = ((), (), s32[]{:S(2)}) async-start(), calls=%async_computation | async-start | bytes 8650752 | tf_op jit(solution)/shard_map/all_gather | solution.py:252
  8.5 16.4 %copy-start.7 = (s32[1,1024]{1,0:T(1,128)S(1)}, s32[1,1024]{1,0:T(1,128)}, u32[]{:S(2)}) copy-start(s32[1,1024]{1,0:T(1,128)} %param.20) | copy-start | bytes 12292
  9.8 15.4 %copy-start.2 = (bf16[1,256,1024]{2,1,0:T(8,128)(2,1)S(1)}, bf16[1,256,1024]{2,1,0:T(8,128)(2,1)}, u32[]{:S(2)}) copy-start(bf16[1,256,1024]{2,1,0:T(8,128)(2,1)} %param.12) | copy-start | bytes 1572868
  9.8 15.4 %copy-start.8 = (f32[1024]{0:T(1024)S(1)}, f32[1024]{0:T(1024)}, u32[]{:S(2)}) copy-start(f32[1024]{0:T(1024)} %param.13) | copy-start | bytes 12292
  9.8 16.4 %collective-permute-start = (bf16[256,1024]{1,0:T(8,128)(2,1)S(1)}, bf16[256,1024]{1,0:T(8,128)(2,1)}, u32[]{:S(2)}, u32[]{:S(2)}) collective-permute-start(bf16[256,1024]{1,0:T(8,128)(2,1)S(1)} %fusion.16), channel_id=1, source_target_pairs={{0,32},{32,64},{64,96},{96,0},{1,33},{33,65},{65,97},{97,1},{2,34}... | collective-permute-start | bytes 1572872 | tf_op jit(solution)/shard_map/ppermute | solution.py:174
  12.3 26.0 %collective-permute-start.1 = (bf16[256,1024]{1,0:T(8,128)(2,1)S(1)}, bf16[256,1024]{1,0:T(8,128)(2,1)}, u32[]{:S(2)}, u32[]{:S(2)}) collective-permute-start(bf16[256,1024]{1,0:T(8,128)(2,1)S(1)} %fusion.16), channel_id=1, source_target_pairs={{0,64},{32,96},{64,0},{96,32},{1,65},{33,97},{65,1},{97,33},{2,66}... | collective-permute-start | bytes 1572872 | tf_op jit(solution)/shard_map/ppermute | solution.py:174
  15.6 22.7 %collective-permute-start.2 = (bf16[256,1024]{1,0:T(8,128)(2,1)S(1)}, bf16[256,1024]{1,0:T(8,128)(2,1)}, u32[]{:S(2)}, u32[]{:S(2)}) collective-permute-start(bf16[256,1024]{1,0:T(8,128)(2,1)S(1)} %fusion.16), channel_id=1, source_target_pairs={{0,96},{32,0},{64,32},{96,64},{1,97},{33,1},{65,33},{97,65},{2,98}... | collective-permute-start | bytes 1572872 | tf_op jit(solution)/shard_map/ppermute | solution.py:174
  16.3 95.8 %collective-permute-start.6 = (bf16[256,1024]{1,0:T(8,128)(2,1)}, bf16[256,1024]{1,0:T(8,128)(2,1)}, u32[]{:S(2)}, u32[]{:S(2)}) collective-permute-start(bf16[256,1024]{1,0:T(8,128)(2,1)} %param.15), channel_id=1, source_target_pairs={{0,32},{32,64},{64,96},{96,0},{1,33},{33,65},{65,97},{97,1},{2,34}... | collective-permute-start | bytes 1572872 | tf_op jit(solution)/shard_map/ppermute | solution.py:174
  17.1 96.2 %collective-permute-start.7 = (bf16[256,1024]{1,0:T(8,128)(2,1)}, bf16[256,1024]{1,0:T(8,128)(2,1)}, u32[]{:S(2)}, u32[]{:S(2)}) collective-permute-start(bf16[256,1024]{1,0:T(8,128)(2,1)} %param.15), channel_id=1, source_target_pairs={{0,64},{32,96},{64,0},{96,32},{1,65},{33,97},{65,1},{97,33},{2,66}... | collective-permute-start | bytes 1572872 | tf_op jit(solution)/shard_map/ppermute | solution.py:174
  26.2 87.1 %collective-permute-start.8 = (bf16[256,1024]{1,0:T(8,128)(2,1)}, bf16[256,1024]{1,0:T(8,128)(2,1)}, u32[]{:S(2)}, u32[]{:S(2)}) collective-permute-start(bf16[256,1024]{1,0:T(8,128)(2,1)} %param.15), channel_id=1, source_target_pairs={{0,96},{32,0},{64,32},{96,64},{1,97},{33,1},{65,33},{97,65},{2,98}... | collective-permute-start | bytes 1572872 | tf_op jit(solution)/shard_map/ppermute | solution.py:174
  42.0 2.0 %copy-start.5 = (bf16[1024,3,256]{0,2,1:T(8,128)(2,1)S(1)}, bf16[1024,3,256]{0,2,1:T(8,128)(2,1)}, u32[]{:S(2)}) copy-start(bf16[1024,3,256]{0,2,1:T(8,128)(2,1)} %copy.19) | copy-start | bytes 4718596
  47.1 18.8 %copy-start = (s32[64]{0:T(128)S(1)}, s32[64]{0:T(128)}, u32[]{:S(2)}) copy-start(s32[64]{0:T(128)} %pnode_ref.1) | copy-start | bytes 772
  47.1 18.8 %copy-start.1 = (s32[64]{0:T(128)S(1)}, s32[64]{0:T(128)}, u32[]{:S(2)}) copy-start(s32[64]{0:T(128)} %pfill_ref.1) | copy-start | bytes 772
  65.9 47.4 %copy-start.6 = (bf16[256,1024]{1,0:T(8,128)(2,1)S(1)}, bf16[256,1024]{1,0:T(8,128)(2,1)}, u32[]{:S(2)}) copy-start(bf16[256,1024]{1,0:T(8,128)(2,1)} %param.15) | copy-start | bytes 1572868
  108.2 8.7 %collective-permute-start.3 = (bf16[256,256]{1,0:T(8,128)(2,1)S(1)}, bf16[256,256]{1,0:T(8,128)(2,1)S(1)}, u32[]{:S(2)}, u32[]{:S(2)}) collective-permute-start(bf16[256,256]{1,0:T(8,128)(2,1)S(1)} %get-tuple-element.11), channel_id=1, source_target_pairs={{0,32},{32,64},{64,96},{96,0},{1,33},{33,65},{65,97},{97,1},{2,34}... | collective-permute-start | bytes 393224 | tf_op jit(solution)/shard_map/ppermute | solution.py:261
  109.6 7.3 %collective-permute-start.4 = (bf16[256,256]{1,0:T(8,128)(2,1)S(1)}, bf16[256,256]{1,0:T(8,128)(2,1)S(1)}, u32[]{:S(2)}, u32[]{:S(2)}) collective-permute-start(bf16[256,256]{1,0:T(8,128)(2,1)S(1)} %get-tuple-element.10), channel_id=1, source_target_pairs={{0,64},{32,96},{64,0},{96,32},{1,65},{33,97},{65,1},{97,33},{2,66}... | collective-permute-start | bytes 393224 | tf_op jit(solution)/shard_map/ppermute | solution.py:261
  112.2 5.1 %collective-permute-start.5 = (bf16[256,256]{1,0:T(8,128)(2,1)S(1)}, bf16[256,256]{1,0:T(8,128)(2,1)S(1)}, u32[]{:S(2)}, u32[]{:S(2)}) collective-permute-start(bf16[256,256]{1,0:T(8,128)(2,1)S(1)} %get-tuple-element.9), channel_id=1, source_target_pairs={{0,96},{32,0},{64,32},{96,64},{1,97},{33,1},{65,33},{97,65},{2,98}... | collective-permute-start | bytes 393224 | tf_op jit(solution)/shard_map/ppermute | solution.py:261
  116.9 1.6 %copy-start.3 = (bf16[4,256,1024]{2,1,0:T(8,128)(2,1)S(1)}, bf16[4,256,1024]{2,1,0:T(8,128)(2,1)}, u32[]{:S(2)}) copy-start(bf16[4,256,1024]{2,1,0:T(8,128)(2,1)} %gather_fusion.2) | copy-start | bytes 6291460
Sparse Core Ops, SparseCore 0:
  9.7 56.1 all-gather.1

commit v10 on v9

--- a/solution.py
+++ b/solution.py
@@ -10,7 +10,7 @@
 FLOOR_SCORE = -1e30
 Q_BLOCK = 256
 K_BLOCK = 128
-CHAINS = 4
+CHAINS = 5
 INTERPRET = False
 
 

time: 127 us -> 128 us (level)
  the two profiles are of different devices: /device:TPU:1 before, /device:TPU:12 now
where the time goes in v10:
time: 128 us; the launch traced here: 125 us
  Pallas kernels  42.3 us (33%)
  waiting for transfers between devices  25.1 us (20%)
  starting transfers between devices  15.1 us (12%)
  between operations  13.7 us (11%)
  other arithmetic  12.6 us (10%)
  local copies, waits for them, and re-layouts  11.7 us (9%)
  matrix products  4.68 us (4%)
    pallas_call x1, Pallas kernels, attention(): pl.pallas_call(attn_kernel, grid_spec=grid_spec, interpret=INTERPRET, out...  42.3 us
    ppermute x6, waiting for transfers between devices, head_gather(): lax.ppermute(x, 'head', shift_perm(n, d))  12.6 us
    all_gather x1, waiting for transfers between devices, shards(): cache = lax.all_gather(cache_kv, 'page', axis=1, tiled=True)  11.8 us
    ppermute x6, starting transfers between devices, head_gather(): lax.ppermute(x, 'head', shift_perm(n, d))  9.26 us
    ppermute x3, starting transfers between devices, shards(): parts.append(lax.ppermute(send, 'head', shift_perm(n_head, d)))  5.86 us
    gather x2, local copies, waits for them, and re-layouts, head_gather(): gathered = jnp.take(stacked, order, axis=0)  4.11 us
    another operation x2, other arithmetic, head_gather(): stacked = jnp.stack(parts)  3.24 us
    dot_general x1, matrix products, shards(): jnp.dot(head_gather(normed, n_head), weight_flat, preferred_element_type=...  3.06 us
  transfers between devices with their start and end apart: 10, of which 3 were waited for; matrix products, arithmetic and copies ran while one was open for 21% of the time, Pallas kernels for 34%

profile of v10, /device:TPU:12, one launch (start us, length us, event | category | flops | bytes accessed | tf_op | source)
XLA Modules:
  0.0 125.2 jit_solution(14035866302342362903)
XLA Ops:
  7.3 1.2 fusion.14
  8.5 1.2 fusion.16
  9.8 2.0 %collective-permute-start = (bf16[256,1024]{1,0:T(8,128)(2,1)S(1)}, bf16[256,1024]{1,0:T(8,128)(2,1)}, u32[]{:S(2)}, u32[]{:S(2)}) collective-permute-start(bf16[256,1024]{1,0:T(8,128)(2,1)S(1)} %fusion.16), channel_id=1, source_target_pairs={{0,32},{32,64},{64,96},{96,0},{1,33},{33,65},{65,97},{97,1},{2,34}... | collective-permute-start | bytes 1572872 | tf_op jit(solution)/shard_map/ppermute | solution.py:174
  11.8 3.6 %collective-permute-start.1 = (bf16[256,1024]{1,0:T(8,128)(2,1)S(1)}, bf16[256,1024]{1,0:T(8,128)(2,1)}, u32[]{:S(2)}, u32[]{:S(2)}) collective-permute-start(bf16[256,1024]{1,0:T(8,128)(2,1)S(1)} %fusion.16), channel_id=1, source_target_pairs={{0,64},{32,96},{64,0},{96,32},{1,65},{33,97},{65,1},{97,33},{2,66}... | collective-permute-start | bytes 1572872 | tf_op jit(solution)/shard_map/ppermute | solution.py:174
  15.3 1.0 collective-permute-start.2
  16.4 1.0 collective-permute-start.6
  23.4 1.7 %copy.19 = bf16[1024,3,256]{0,2,1:T(8,128)(2,1)} copy(bf16[1024,3,256]{2,0,1:T(8,128)(2,1)S(1)} %copy-done.4) | data formatting | bytes 3145728 | tf_op args[2]
  25.7 1.9 %collective-permute-done = bf16[256,1024]{1,0:T(8,128)(2,1)} collective-permute-done((bf16[256,1024]{1,0:T(8,128)(2,1)S(1)}, bf16[256,1024]{1,0:T(8,128)(2,1)}, u32[]{:S(2)}, u32[]{:S(2)}) %collective-permute-start) | collective-permute-done | bytes 524320 | tf_op jit(solution)/shard_map/ppermute | solution.py:174
  27.6 1.2 collective-permute-start.8
  28.8 10.7 %collective-permute-done.1 = bf16[256,1024]{1,0:T(8,128)(2,1)} collective-permute-done((bf16[256,1024]{1,0:T(8,128)(2,1)S(1)}, bf16[256,1024]{1,0:T(8,128)(2,1)}, u32[]{:S(2)}, u32[]{:S(2)}) %collective-permute-start.1) | collective-permute-done | bytes 524320 | tf_op jit(solution)/shard_map/ppermute | solution.py:174
  39.5 1.6 %pad_maximum_fusion = bf16[4,256,1024]{2,1,0:T(8,128)(2,1)S(1)} fusion(bf16[1,256,1024]{2,1,0:T(8,128)(2,1)} %bitcast.5, bf16[1,256,1024]{2,1,0:T(8,128)(2,1)} %bitcast.4, bf16[1,256,1024]{2,1,0:T(8,128)(2,1)} %bitcast.3, bf16[1,256,1024]{2,1,0:T(8,128)(2,1)S(1)} %fusion.18), kind=kLoop, calls=%fused_computation.3 | loop fusion | flops 3145728 | bytes 4194304 | tf_op jit(solution)/shard_map/stack | solution.py:175
  41.1 2.1 %gather_fusion.1 = bf16[4,256,1024]{2,1,0:T(8,128)(2,1)} fusion(bf16[4,256,1024]{2,1,0:T(8,128)(2,1)S(1)} %pad_maximum_fusion, s32[1024]{0:T(1024)S(1)} %pad_clamp_fusion.1), kind=kCustom, calls=%fused_computation.clone | custom fusion | bytes 4194320 | tf_op jit(solution)/shard_map/jit(_take)/gather | solution.py:177
  43.2 2.0 %broadcast_select_fusion = bf16[4,256,1024]{2,1,0:T(8,128)(2,1)S(1)} fusion(bf16[4,256,1024]{2,1,0:T(8,128)(2,1)} %gather_fusion.1, pred[4]{0:T(512)(128)(4,1)S(1)} %compare_and_fusion), kind=kLoop, calls=%fused_computation.8 | loop fusion | flops 1048576 | bytes 4194308 | tf_op jit(solution)/shard_map/jit(_take)/select_n | solution.py:177
  45.2 3.1 %convolution_convert_fusion = bf16[1024,768]{0,1:T(8,128)(2,1)} fusion(bf16[1024,1024]{1,0:T(8,128)(2,1)S(1)} %bitcast.48, bf16[1024,768]{0,1:T(8,128)(2,1)S(1)} %bitcast.49), kind=kOutput, calls=%fused_computation.9 | convolution fusion | flops 1611399168 | bytes 5242880 | tf_op jit(solution)/shard_map/dot_general | solution.py:216
  48.3 1.8 %copy.21.kn_ref = bf16[1024,768]{1,0:T(8,128)(2,1)S(1)} copy(bf16[1024,768]{0,1:T(8,128)(2,1)} %convolution_convert_fusion) | data formatting | bytes 3145728 | tf_op jit(solution)/shard_map/convert_element_type | solution.py:220
  50.1 1.3 %slice_bitcast_fusion = (bf16[256,1024]{1,0:T(8,128)(2,1)S(1)}, bf16[256,1024]{1,0:T(8,128)(2,1)S(1)}) fusion(bf16[1024,768]{0,1:T(8,128)(2,1)} %convolution_convert_fusion), kind=kLoop, calls=%fused_computation.23 | loop fusion | bytes 2097152 | tf_op jit(solution)/shard_map/transpose | solution.py:251
  51.4 11.8 %all-gather.2.cloned.1.call-done.cache_ref = bf16[2,64,128,256]{3,2,1,0:T(8,128)(2,1)} async-done(((bf16[2,2,128,256]{3,2,1,0:T(8,128)(2,1)}), bf16[2,64,128,256]{3,2,1,0:T(8,128)(2,1)}) %all-gather.2.cloned.1.call-update) | async-done | bytes 8388624 | tf_op jit(solution)/shard_map/all_gather | solution.py:252
  63.2 42.3 %shard_map.100 = bf16[256,1024]{1,0:T(8,128)(2,1)S(1)} custom-call(s32[276]{0:T(512)S(1)} %reshape.144.plist_ref, s32[4]{0:T(128)S(1)} %convert_reduce_fusion.1.pcount_ref, s32[64]{0:T(128)S(1)} %copy-done, s32[64]{0:T(128)S(1)} %copy-done.1, s32[4]{0:T(128)S(1)} %and_select_fusion.1.kfirst_ref, bf16[256,1024]{1,0:T(8,128)(2,1)S(1)} %get-tuple-element.7.qt_ref, ...), custom_call_target="tpu_custom_call" | custom-call | tf_op jit(solution)/shard_map/pallas_call | solution.py:157
  105.6 1.6 %collective-permute-start.3 = (bf16[256,256]{1,0:T(8,128)(2,1)S(1)}, bf16[256,256]{1,0:T(8,128)(2,1)S(1)}, u32[]{:S(2)}, u32[]{:S(2)}) collective-permute-start(bf16[256,256]{1,0:T(8,128)(2,1)S(1)} %get-tuple-element.11), channel_id=1, source_target_pairs={{0,32},{32,64},{64,96},{96,0},{1,33},{33,65},{65,97},{97,1},{2,34}... | collective-permute-start | bytes 393224 | tf_op jit(solution)/shard_map/ppermute | solution.py:261
  107.3 2.9 %collective-permute-start.4 = (bf16[256,256]{1,0:T(8,128)(2,1)S(1)}, bf16[256,256]{1,0:T(8,128)(2,1)S(1)}, u32[]{:S(2)}, u32[]{:S(2)}) collective-permute-start(bf16[256,256]{1,0:T(8,128)(2,1)S(1)} %get-tuple-element.10), channel_id=1, source_target_pairs={{0,64},{32,96},{64,0},{96,32},{1,65},{33,97},{65,1},{97,33},{2,66}... | collective-permute-start | bytes 393224 | tf_op jit(solution)/shard_map/ppermute | solution.py:261
  110.1 1.4 %collective-permute-start.5 = (bf16[256,256]{1,0:T(8,128)(2,1)S(1)}, bf16[256,256]{1,0:T(8,128)(2,1)S(1)}, u32[]{:S(2)}, u32[]{:S(2)}) collective-permute-start(bf16[256,256]{1,0:T(8,128)(2,1)S(1)} %get-tuple-element.9), channel_id=1, source_target_pairs={{0,96},{32,0},{64,32},{96,64},{1,97},{33,1},{65,33},{97,65},{2,98}... | collective-permute-start | bytes 393224 | tf_op jit(solution)/shard_map/ppermute | solution.py:261
  111.5 1.6 %pad_maximum_fusion.1 = bf16[4,256,1024]{2,1,0:T(8,128)(2,1)S(1)} fusion(bf16[1,256,1024]{2,1,0:T(8,128)(2,1)} %bitcast.22, bf16[1,256,1024]{2,1,0:T(8,128)(2,1)} %bitcast.21, bf16[1,256,1024]{2,1,0:T(8,128)(2,1)} %bitcast.20, bf16[1,256,1024]{2,1,0:T(8,128)(2,1)S(1)} %bitcast.50), kind=kLoop, calls=%fused_computation.4 | loop fusion | flops 3145728 | bytes 4194304 | tf_op jit(solution)/shard_map/stack | solution.py:175
  113.1 2.0 %gather_fusion.2 = bf16[4,256,1024]{2,1,0:T(8,128)(2,1)} fusion(bf16[4,256,1024]{2,1,0:T(8,128)(2,1)S(1)} %pad_maximum_fusion.1, s32[1024]{0:T(1024)S(1)} %pad_clamp_fusion.1), kind=kCustom, calls=%fused_computation.1.clone | custom fusion | bytes 4194320 | tf_op jit(solution)/shard_map/jit(_take)/gather | solution.py:177
  116.8 1.6 %fusion.11 = bf16[1,256,1024]{2,1,0:T(8,128)(2,1)} fusion(bf16[4,256,1024]{2,1,0:T(8,128)(2,1)S(1)} %copy-done.3, pred[4]{0:T(512)(128)(4,1)S(1)} %compare_and_fusion, bf16[4,256,256]{2,1,0:T(8,128)(2,1)S(1)} %gather_fusion), kind=kOutput, calls=%fused_computation.16 | convolution fusion | flops 538443776 | bytes 3145732 | tf_op jit(solution)/shard_map/dot_general | solution.py:265
  (58 shorter events, 8.9 us)
Async XLA Ops:
  6.5 16.9 %copy-start.4 = (bf16[1024,3,256]{2,0,1:T(8,128)(2,1)S(1)}, bf16[1024,3,256]{2,0,1:T(8,128)(2,1)}, u32[]{:S(2)}) copy-start(bf16[1024,3,256]{2,0,1:T(8,128)(2,1)} %param.14) | copy-start | bytes 4718596
  6.5 56.7 %all-gather.2.cloned.1.call-start = ((), (), s32[]{:S(2)}) async-start(), calls=%async_computation | async-start | bytes 8650752 | tf_op jit(solution)/shard_map/all_gather | solution.py:252
  8.5 16.7 %copy-start.7 = (s32[1,1024]{1,0:T(1,128)S(1)}, s32[1,1024]{1,0:T(1,128)}, u32[]{:S(2)}) copy-start(s32[1,1024]{1,0:T(1,128)} %param.20) | copy-start | bytes 12292
  9.8 15.7 %copy-start.2 = (bf16[1,256,1024]{2,1,0:T(8,128)(2,1)S(1)}, bf16[1,256,1024]{2,1,0:T(8,128)(2,1)}, u32[]{:S(2)}) copy-start(bf16[1,256,1024]{2,1,0:T(8,128)(2,1)} %param.12) | copy-start | bytes 1572868
  9.8 15.7 %copy-start.8 = (f32[1024]{0:T(1024)S(1)}, f32[1024]{0:T(1024)}, u32[]{:S(2)}) copy-start(f32[1024]{0:T(1024)} %param.13) | copy-start | bytes 12292
  9.8 17.8 %collective-permute-start = (bf16[256,1024]{1,0:T(8,128)(2,1)S(1)}, bf16[256,1024]{1,0:T(8,128)(2,1)}, u32[]{:S(2)}, u32[]{:S(2)}) collective-permute-start(bf16[256,1024]{1,0:T(8,128)(2,1)S(1)} %fusion.16), channel_id=1, source_target_pairs={{0,32},{32,64},{64,96},{96,0},{1,33},{33,65},{65,97},{97,1},{2,34}... | collective-permute-start | bytes 1572872 | tf_op jit(solution)/shard_map/ppermute | solution.py:174
  11.8 27.7 %collective-permute-start.1 = (bf16[256,1024]{1,0:T(8,128)(2,1)S(1)}, bf16[256,1024]{1,0:T(8,128)(2,1)}, u32[]{:S(2)}, u32[]{:S(2)}) collective-permute-start(bf16[256,1024]{1,0:T(8,128)(2,1)S(1)} %fusion.16), channel_id=1, source_target_pairs={{0,64},{32,96},{64,0},{96,32},{1,65},{33,97},{65,1},{97,33},{2,66}... | collective-permute-start | bytes 1572872 | tf_op jit(solution)/shard_map/ppermute | solution.py:174
  15.3 24.2 %collective-permute-start.2 = (bf16[256,1024]{1,0:T(8,128)(2,1)S(1)}, bf16[256,1024]{1,0:T(8,128)(2,1)}, u32[]{:S(2)}, u32[]{:S(2)}) collective-permute-start(bf16[256,1024]{1,0:T(8,128)(2,1)S(1)} %fusion.16), channel_id=1, source_target_pairs={{0,96},{32,0},{64,32},{96,64},{1,97},{33,1},{65,33},{97,65},{2,98}... | collective-permute-start | bytes 1572872 | tf_op jit(solution)/shard_map/ppermute | solution.py:174
  16.4 93.8 %collective-permute-start.6 = (bf16[256,1024]{1,0:T(8,128)(2,1)}, bf16[256,1024]{1,0:T(8,128)(2,1)}, u32[]{:S(2)}, u32[]{:S(2)}) collective-permute-start(bf16[256,1024]{1,0:T(8,128)(2,1)} %param.15), channel_id=1, source_target_pairs={{0,32},{32,64},{64,96},{96,0},{1,33},{33,65},{65,97},{97,1},{2,34}... | collective-permute-start | bytes 1572872 | tf_op jit(solution)/shard_map/ppermute | solution.py:174
  17.4 94.1 %collective-permute-start.7 = (bf16[256,1024]{1,0:T(8,128)(2,1)}, bf16[256,1024]{1,0:T(8,128)(2,1)}, u32[]{:S(2)}, u32[]{:S(2)}) collective-permute-start(bf16[256,1024]{1,0:T(8,128)(2,1)} %param.15), channel_id=1, source_target_pairs={{0,64},{32,96},{64,0},{96,32},{1,65},{33,97},{65,1},{97,33},{2,66}... | collective-permute-start | bytes 1572872 | tf_op jit(solution)/shard_map/ppermute | solution.py:174
  27.6 83.9 %collective-permute-start.8 = (bf16[256,1024]{1,0:T(8,128)(2,1)}, bf16[256,1024]{1,0:T(8,128)(2,1)}, u32[]{:S(2)}, u32[]{:S(2)}) collective-permute-start(bf16[256,1024]{1,0:T(8,128)(2,1)} %param.15), channel_id=1, source_target_pairs={{0,96},{32,0},{64,32},{96,64},{1,97},{33,1},{65,33},{97,65},{2,98}... | collective-permute-start | bytes 1572872 | tf_op jit(solution)/shard_map/ppermute | solution.py:174
  43.2 2.0 %copy-start.5 = (bf16[1024,3,256]{0,2,1:T(8,128)(2,1)S(1)}, bf16[1024,3,256]{0,2,1:T(8,128)(2,1)}, u32[]{:S(2)}) copy-start(bf16[1024,3,256]{0,2,1:T(8,128)(2,1)} %copy.19) | copy-start | bytes 4718596
  48.3 14.9 %copy-start = (s32[64]{0:T(128)S(1)}, s32[64]{0:T(128)}, u32[]{:S(2)}) copy-start(s32[64]{0:T(128)} %pnode_ref.1) | copy-start | bytes 772
  48.3 14.9 %copy-start.1 = (s32[64]{0:T(128)S(1)}, s32[64]{0:T(128)}, u32[]{:S(2)}) copy-start(s32[64]{0:T(128)} %pfill_ref.1) | copy-start | bytes 772
  63.2 48.3 %copy-start.6 = (bf16[256,1024]{1,0:T(8,128)(2,1)S(1)}, bf16[256,1024]{1,0:T(8,128)(2,1)}, u32[]{:S(2)}) copy-start(bf16[256,1024]{1,0:T(8,128)(2,1)} %param.15) | copy-start | bytes 1572868
  105.6 9.5 %collective-permute-start.3 = (bf16[256,256]{1,0:T(8,128)(2,1)S(1)}, bf16[256,256]{1,0:T(8,128)(2,1)S(1)}, u32[]{:S(2)}, u32[]{:S(2)}) collective-permute-start(bf16[256,256]{1,0:T(8,128)(2,1)S(1)} %get-tuple-element.11), channel_id=1, source_target_pairs={{0,32},{32,64},{64,96},{96,0},{1,33},{33,65},{65,97},{97,1},{2,34}... | collective-permute-start | bytes 393224 | tf_op jit(solution)/shard_map/ppermute | solution.py:261
  107.3 7.9 %collective-permute-start.4 = (bf16[256,256]{1,0:T(8,128)(2,1)S(1)}, bf16[256,256]{1,0:T(8,128)(2,1)S(1)}, u32[]{:S(2)}, u32[]{:S(2)}) collective-permute-start(bf16[256,256]{1,0:T(8,128)(2,1)S(1)} %get-tuple-element.10), channel_id=1, source_target_pairs={{0,64},{32,96},{64,0},{96,32},{1,65},{33,97},{65,1},{97,33},{2,66}... | collective-permute-start | bytes 393224 | tf_op jit(solution)/shard_map/ppermute | solution.py:261
  110.1 5.1 %collective-permute-start.5 = (bf16[256,256]{1,0:T(8,128)(2,1)S(1)}, bf16[256,256]{1,0:T(8,128)(2,1)S(1)}, u32[]{:S(2)}, u32[]{:S(2)}) collective-permute-start(bf16[256,256]{1,0:T(8,128)(2,1)S(1)} %get-tuple-element.9), channel_id=1, source_target_pairs={{0,96},{32,0},{64,32},{96,64},{1,97},{33,1},{65,33},{97,65},{2,98}... | collective-permute-start | bytes 393224 | tf_op jit(solution)/shard_map/ppermute | solution.py:261
  115.2 1.6 %copy-start.3 = (bf16[4,256,1024]{2,1,0:T(8,128)(2,1)S(1)}, bf16[4,256,1024]{2,1,0:T(8,128)(2,1)}, u32[]{:S(2)}) copy-start(bf16[4,256,1024]{2,1,0:T(8,128)(2,1)} %gather_fusion.2) | copy-start | bytes 6291460
Sparse Core Ops, SparseCore 0:
  9.7 53.4 all-gather.1
